TPU v7x, 512 devices: a whole 4x4x16 slice. The times are simulated.
512 devices in a mesh: tm: 64 (over z, y), area: 8 (over x, core).
Axes of the slice: x: 4, y: 4, z: 16, core: 2. Of those that a mesh axis runs over, the one named last changes fastest.
Arguments:
- demand: float32 [256, 71680], P('tm', 'area'), may hold values from -6 to 6
- unit_cost: float32 [256, 65536], P('tm', 'area'), may hold values from -18 to 18
- ptdf_tiles: bfloat16 [192, 128, 256], P('area'), may hold values from -0.25 to 0.25
- tile_area: int32 [192, 1], replicated, may hold values from 0 to 7; in each aligned block of 24 rows (0 to 23, 24 to 47, ...) at most 6 rows name the same one
- tile_block: int32 [192], replicated, may hold values from 0 to 34
- tile_row: int32 [192], replicated, may hold values from 0 to 11
- unit_bus: int32 [65536], P('area'), may hold values from 0 to 8959
- unit_class: int32 [65536], P('area'), may hold values from 0 to 2
- power_cap: float32 [65536], P('area'), may hold values from 0.1 to 2
- line_limit: float32 [12288], P('area'), may hold values from 0.2 to 2
- smoother: float32 [3, 256], replicated, as said below
Outputs:
- power: float32 [256, 65536], P('tm', 'area')
- line_duals: float32 [256, 12288], P('tm', 'area')
- primal_rms: float32 [2], replicated
Inputs may be any that keep to these rules, and one draw needn't show every extreme that they name: `tile_area`: among the 24 tiles of one holder, at most 6 have their column block in one area, and some holder reaches 6. `smoother`: row k is the first column of the inverse of (c1 I + L)(c2 I + L) / (c1 c2) of order 256, with L = 2 I - S - S^T the cyclic second difference and class constants 1e-5 <= c1 < c2 <= 1.
All inputs are finite; a program needn't handle non-finite values.
Results may differ from a plain program's by a relative error of at most 0.0028.
Values may be sent and summed in bfloat16 or wider, within the bound.
No kernel may reach another device: no remote copies, remote signals or barrier semaphores. Data moves between devices by JAX's collectives and lax.ppermute only.
A program may use at most 64 MiB of HBM per device.

v0:
```python
import functools
import math

import jax
import jax.numpy as jnp
from jax import lax
from jax.sharding import Mesh
from jax.sharding import PartitionSpec as P

ITERATIONS = 2
TM = ("tm_0", "tm_1")
AREA = ("area_0", "area_1")
TM_AREA = ("tm_0", "tm_1", "area_0", "area_1")


step_size = 0.5
rho_weight = 1.0


def laid_out(tiles, dim):
    dims = list(tiles.shape[1:])
    dims[dim] *= tiles.shape[0]
    return jnp.moveaxis(tiles, 0, dim).reshape(dims)


def copy_for_each(array, axis):
    count = lax.axis_size(axis)
    return lax.all_to_all(
        jnp.broadcast_to(array[None], (count, *array.shape)), axis, 0, 0, tiled=True
    )


def collect(array, axis, dim):
    return laid_out(copy_for_each(array, axis), dim)


def one_axis_at_a_time(array, axes):
    return functools.reduce(lax.psum, axes, array)


def per_device(
    demand,
    unit_cost,
    ptdf_tiles,
    tile_area,
    tile_block,
    tile_row,
    unit_bus,
    unit_class,
    power_cap,
    line_limit,
    smoother,
):
    time_devices = lax.axis_size(TM)
    area_devices = lax.axis_size(AREA)
    block_steps, bus_area = demand.shape
    unit_area = unit_cost.shape[1]
    tile_count, line_block, panel_width = ptdf_tiles.shape
    col_blocks = bus_area // panel_width
    row_blocks = line_limit.shape[0] // line_block
    capacity = 2 * tile_count // area_devices
    horizon = block_steps * time_devices
    unit_width = unit_area // time_devices
    area_index = lax.axis_index(AREA)
    time_index = lax.axis_index(TM)
    tile_areas = tile_area.reshape(area_devices, tile_count)
    block_grid = tile_block.reshape(area_devices, tile_count)
    row_grid = tile_row.reshape(area_devices, tile_count)
    is_source = (tile_areas == area_index).astype(jnp.int32)
    rank_source = jnp.cumsum(is_source, axis=1) - 1
    slot_ids = jnp.arange(capacity, dtype=jnp.int32)
    chosen = is_source[:, None, :] * (rank_source[:, None, :] == slot_ids[None, :, None]).astype(
        jnp.int32
    )
    send_block = jnp.sum(chosen * block_grid[:, None, :], axis=2).reshape(-1)
    my_areas = lax.dynamic_index_in_dim(tile_areas, area_index, 0, keepdims=False)
    my_blocks = lax.dynamic_index_in_dim(block_grid, area_index, 0, keepdims=False)
    my_rows = lax.dynamic_index_in_dim(row_grid, area_index, 0, keepdims=False)
    positions = jnp.arange(tile_count, dtype=jnp.int32)
    earlier = positions[None, :] <= positions[:, None]
    same_area = my_areas[None, :] == my_areas[:, None]
    rank_mine = jnp.sum((same_area & earlier).astype(jnp.int32), axis=1) - 1
    slot_of_tile = my_areas * capacity + rank_mine
    my_columns = my_areas * col_blocks + my_blocks
    my_class = lax.dynamic_slice_in_dim(unit_class, time_index * unit_width, unit_width)
    my_cap = lax.dynamic_slice_in_dim(power_cap, time_index * unit_width, unit_width)
    half_steps = horizon // 2
    steps_line = jnp.arange(horizon, dtype=jnp.int32)
    frequency = jnp.concatenate(
        [jnp.arange(half_steps + 1, dtype=jnp.int32), jnp.arange(1, half_steps, dtype=jnp.int32)]
    )
    angle = (frequency[:, None] * steps_line[None, :] % horizon).astype(jnp.float32) * (
        2.0 * math.pi / horizon
    )
    cosine_rows = (steps_line <= half_steps)[:, None]
    forward = jnp.where(cosine_rows, jnp.cos(angle), -jnp.sin(angle))
    edge_rows = (frequency == 0) | (frequency == half_steps)
    row_weight = (jnp.where(edge_rows, 1.0, 2.0).astype(jnp.float32) / horizon)[:, None]
    kernel_spectrum = jnp.dot(
        forward, smoother.T, precision=lax.Precision.HIGHEST, preferred_element_type=jnp.float32
    )
    class_table = (
        my_class[None, :] == jnp.arange(smoother.shape[0], dtype=jnp.int32)[:, None]
    ).astype(jnp.float32)
    unit_spectrum = jnp.dot(
        kernel_spectrum,
        class_table,
        precision=lax.Precision.HIGHEST,
        preferred_element_type=jnp.float32,
    )
    empty_row = jnp.zeros((1, unit_width), jnp.float32)
    kernel_real = unit_spectrum[: half_steps + 1]
    kernel_imag = jnp.concatenate([empty_row, unit_spectrum[half_steps + 1 :], empty_row], axis=0)
    power_time = jnp.zeros((block_steps, unit_area), jnp.float32)
    line_duals = jnp.zeros((block_steps, line_limit.shape[0]), jnp.float32)
    totals = []
    for repeat in range(ITERATIONS):
        injection = demand.at[:, unit_bus].add(power_time).astype(jnp.bfloat16)
        gathered = collect(injection, AREA, 1)
        panels = jnp.take(
            gathered.reshape(block_steps, area_devices * col_blocks, panel_width),
            my_columns,
            axis=1,
        )
        partial_value = jnp.einsum(
            "tjb,jlb->tjl", panels, ptdf_tiles, preferred_element_type=jnp.float32
        )
        line_flows = (
            jnp.zeros((block_steps, row_blocks, line_block), jnp.float32)
            .at[:, my_rows]
            .add(partial_value)
        )
        line_flows = line_flows.reshape(block_steps, row_blocks * line_block)
        limits = line_limit[None, :]
        clipped = jnp.clip(line_flows + line_duals, -limits, limits)
        line_duals = line_duals + line_flows - clipped
        excess = line_flows - clipped
        local_total = jnp.sum(excess * excess)
        totals.append(local_total)
        weights = (line_duals + line_flows - clipped).astype(jnp.bfloat16)
        picked = jnp.take(weights.reshape(block_steps, row_blocks, line_block), my_rows, axis=1)
        contrib = jnp.einsum("tjl,jlb->tjb", picked, ptdf_tiles, preferred_element_type=jnp.float32)
        outbound = (
            jnp.zeros((block_steps, area_devices * capacity, panel_width), jnp.float32)
            .at[:, slot_of_tile]
            .set(contrib)
        )
        outbound = outbound.reshape(block_steps, area_devices, capacity, panel_width)
        returned = lax.all_to_all(outbound, AREA, split_axis=1, concat_axis=1, tiled=True)
        prices = (
            jnp.zeros((block_steps, col_blocks, panel_width), jnp.float32)
            .at[:, send_block]
            .add(returned.reshape(block_steps, area_devices * capacity, panel_width))
        )
        prices = prices.reshape(block_steps, bus_area)
        gradient = unit_cost + rho_weight * jnp.take(prices, unit_bus, axis=1)
        target = power_time - step_size * gradient
        columns = lax.all_to_all(target, TM, split_axis=1, concat_axis=0, tiled=True)
        spectrum = jnp.dot(
            forward, columns, precision=lax.Precision.HIGHEST, preferred_element_type=jnp.float32
        )
        spectrum_real = spectrum[: half_steps + 1]
        spectrum_imag = jnp.concatenate([empty_row, spectrum[half_steps + 1 :], empty_row], axis=0)
        product_real = spectrum_real * kernel_real - spectrum_imag * kernel_imag
        product_imag = spectrum_real * kernel_imag + spectrum_imag * kernel_real
        stacked = jnp.concatenate([product_real, product_imag[1:half_steps]], axis=0) * row_weight
        smoothed = lax.dot_general(
            forward,
            stacked,
            (((0,), (0,)), ((), ())),
            precision=lax.Precision.HIGHEST,
            preferred_element_type=jnp.float32,
        )
        power_cols = jnp.clip(smoothed, -my_cap[None, :], my_cap[None, :])
        power_time = lax.all_to_all(power_cols, TM, split_axis=0, concat_axis=1, tiled=True)
    entries = float(horizon * line_limit.shape[0] * area_devices)
    summed = one_axis_at_a_time(jnp.stack(totals), TM_AREA)
    primal_rms = jnp.sqrt(summed / entries)
    return (power_time, line_duals, primal_rms)


def solution(mesh):
    finer = Mesh(mesh.devices.reshape(16, 4, 4, 2), ("tm_0", "tm_1", "area_0", "area_1"))
    placed = (
        P(TM, AREA),
        P(TM, AREA),
        P(AREA, None, None),
        P(),
        P(),
        P(),
        P(AREA),
        P(AREA),
        P(AREA),
        P(AREA),
        P(),
    )
    return jax.shard_map(
        per_device,
        mesh=finer,
        in_specs=placed,
        out_specs=(P(TM, AREA), P(TM, AREA), P()),
        check_vma=False,
    )
```

profile of v0, /device:TPU:2, one launch (start us, length us, event | category | flops | bytes accessed | tf_op | source)
XLA Modules:
  0.0 404.4 jit_solution(14348011206463100626)
XLA Ops:
  1.5 3.8 copy.88
  5.3 3.8 copy.108
  9.1 48.5 %scatter_custom_fusion = f32[4,8960]{0,1:T(8,128)} fusion(f32[4,8960]{0,1:T(8,128)} %copy.88, s32[8192]{0:T(1024)S(1)} %get-tuple-element.26, f32[]{:T(128)} %constant.63.clone.1), kind=kCustom, calls=%fused_computation.14 | custom fusion | flops 32768 | bytes 143872 | tf_op jit(solution)/shard_map/scatter-add | solution.py:118
  57.7 3.1 copy.89
  61.7 9.3 %all-to-all-start = ((bf16[8,4,8960]{2,1,0:T(4,128)(2,1)}), bf16[8,4,8960]{2,1,0:T(4,128)(2,1)S(1)}, u32[]{:S(2)}, u32[]{:S(2)}) async-start(bf16[8,4,8960]{2,1,0:T(4,128)(2,1)} %broadcast_in_dim.56), calls=%async_computation | async-start | bytes 1146880 | tf_op jit(solution)/shard_map/all_to_all | solution.py:28
  74.2 6.3 %all-to-all-done = bf16[8,4,8960]{2,1,0:T(4,128)(2,1)S(1)} async-done(((bf16[8,4,8960]{2,1,0:T(4,128)(2,1)}), bf16[8,4,8960]{2,1,0:T(4,128)(2,1)S(1)}, u32[]{:S(2)}, u32[]{:S(2)}) %all-to-all-start) | async-done | bytes 573472 | tf_op jit(solution)/shard_map/all_to_all | solution.py:28
  85.1 3.6 scatter_fusion.1
  88.7 4.8 %all-to-all-start.1 = ((f32[4,8,6,256]{3,0,2,1:T(4,128)}), f32[4,8,6,256]{3,0,2,1:T(4,128)S(1)}, u32[]{:S(2)}, u32[]{:S(2)}) async-start(f32[4,8,6,256]{3,0,2,1:T(4,128)} %bitcast.15), calls=%async_computation.1 | async-start | bytes 393216 | tf_op jit(solution)/shard_map/all_to_all | solution.py:149
  93.5 5.4 %all-to-all-done.1 = f32[4,8,6,256]{3,0,2,1:T(4,128)S(1)} async-done(((f32[4,8,6,256]{3,0,2,1:T(4,128)}), f32[4,8,6,256]{3,0,2,1:T(4,128)S(1)}, u32[]{:S(2)}, u32[]{:S(2)}) %all-to-all-start.1) | async-done | bytes 196640 | tf_op jit(solution)/shard_map/all_to_all | solution.py:149
  98.9 2.4 scatter_fusion.2
  101.3 2.9 copy.92
  104.2 30.0 %gather_fusion.2 = f32[8192,4]{1,0:T(8,128)} fusion(f32[4,8960]{0,1:T(8,128)} %copy.92, s32[8192]{0:T(1024)S(1)} %get-tuple-element.25), kind=kCustom, calls=%fused_computation.2.clone | custom fusion | bytes 294912 | tf_op jit(solution)/shard_map/jit(_take)/gather | solution.py:156
  134.2 2.8 copy.93
  137.8 14.2 %all-to-all-start.2 = ((f32[4,64,128]{2,0,1:T(4,128)}), f32[4,64,128]{2,0,1:T(4,128)S(1)}, u32[]{:S(2)}, u32[]{:S(2)}) async-start(f32[4,64,128]{2,0,1:T(4,128)} %fusion.19), calls=%async_computation.2 | async-start | bytes 262144 | tf_op jit(solution)/shard_map/all_to_all | solution.py:158
  154.8 14.6 %all-to-all-done.2 = f32[4,64,128]{2,0,1:T(4,128)S(1)} async-done(((f32[4,64,128]{2,0,1:T(4,128)}), f32[4,64,128]{2,0,1:T(4,128)S(1)}, u32[]{:S(2)}, u32[]{:S(2)}) %all-to-all-start.2) | async-done | bytes 131104 | tf_op jit(solution)/shard_map/all_to_all | solution.py:158
  173.4 21.0 %all_to_all.96 = f32[64,4,128]{2,1,0:T(4,128)S(1)} all-to-all(f32[64,4,128]{2,1,0:T(4,128)S(1)} %bitcast.134), channel_id=1, replica_groups=mesh['tm_0'=16,'tm_1'=4,'area_0'=4,'area_1'=2] {'tm_0','tm_1'}, dimensions={0} | all-to-all | bytes 262144 | tf_op jit(solution)/shard_map/all_to_all | solution.py:175
  194.4 2.7 copy.96
  197.0 44.2 %scatter_fusion.3 = f32[4,8960]{0,1:T(8,128)} fusion(f32[4,8960]{0,1:T(8,128)} %copy.108, s32[8192]{0:T(1024)S(1)} %get-tuple-element.26, f32[8192,4]{1,0:T(8,128)} %copy.96), kind=kCustom, calls=%fused_computation.10 | custom fusion | flops 32768 | bytes 425984 | tf_op jit(solution)/shard_map/scatter-add | solution.py:118
  241.3 3.0 copy.97
  244.5 13.2 %all_to_all.97 = bf16[8,4,8960]{2,1,0:T(4,128)(2,1)S(1)} all-to-all(bf16[8,4,8960]{2,1,0:T(4,128)(2,1)S(1)} %broadcast_in_dim.60), channel_id=1, replica_groups=mesh['tm_0'=16,'tm_1'=4,'area_0'=4,'area_1'=2] {'area_0','area_1'}, dimensions={0} | all-to-all | bytes 1146880 | tf_op jit(solution)/shard_map/all_to_all | solution.py:28
  263.7 9.2 %all_to_all.98 = f32[4,8,6,256]{3,0,2,1:T(4,128)S(1)} all-to-all(f32[4,8,6,256]{3,0,2,1:T(4,128)S(1)} %bitcast.125), channel_id=1, replica_groups=mesh['tm_0'=16,'tm_1'=4,'area_0'=4,'area_1'=2] {'area_0','area_1'}, dimensions={1} | all-to-all | bytes 393216 | tf_op jit(solution)/shard_map/all_to_all | solution.py:149
  273.0 2.4 scatter_fusion.6
  275.3 2.8 copy.100
  278.1 30.0 %gather_fusion.5 = f32[8192,4]{1,0:T(8,128)} fusion(f32[4,8960]{0,1:T(8,128)} %copy.100, s32[8192]{0:T(1024)S(1)} %get-tuple-element.25), kind=kCustom, calls=%fused_computation.5.clone | custom fusion | bytes 294912 | tf_op jit(solution)/shard_map/jit(_take)/gather | solution.py:156
  308.1 2.8 copy.101
  311.7 4.6 %all-to-all-start.6 = ((f32[4,64,128]{2,0,1:T(4,128)}), f32[4,64,128]{2,0,1:T(4,128)S(1)}, u32[]{:S(2)}, u32[]{:S(2)}) async-start(f32[4,64,128]{2,0,1:T(4,128)} %fusion.16), calls=%async_computation.6 | async-start | bytes 262144 | tf_op jit(solution)/shard_map/all_to_all | solution.py:158
  317.7 30.6 %psum.28 = f32[2]{0:T(128)S(1)} all-reduce(f32[2]{0:T(128)S(1)} %pad_maximum_fusion.6), channel_id=1, replica_groups=mesh['tm_0'=16,'tm_1'=4,'area_0'=4,'area_1'=2] {'tm_0'}, use_global_device_ids=true, to_apply=%region_13.17 | all-reduce | flops 2 | bytes 16 | tf_op jit(solution)/shard_map/psum | solution.py:38
  348.3 10.4 %psum.29 = f32[2]{0:T(128)S(1)} all-reduce(f32[2]{0:T(128)S(1)} %psum.28), channel_id=1, replica_groups=mesh['tm_0'=16,'tm_1'=4,'area_0'=4,'area_1'=2] {'tm_1'}, use_global_device_ids=true, to_apply=%region_14.18 | all-reduce | flops 2 | bytes 16 | tf_op jit(solution)/shard_map/psum | solution.py:38
  358.7 9.1 %psum.30 = f32[2]{0:T(128)S(1)} all-reduce(f32[2]{0:T(128)S(1)} %psum.29), channel_id=1, replica_groups=mesh['tm_0'=16,'tm_1'=4,'area_0'=4,'area_1'=2] {'area_0'}, use_global_device_ids=true, to_apply=%region_15.19 | all-reduce | flops 2 | bytes 16 | tf_op jit(solution)/shard_map/psum | solution.py:38
  367.8 2.5 psum.31
  374.9 10.8 %all-to-all-start.7 = ((f32[64,4,128]{2,1,0:T(4,128)}), f32[64,4,128]{2,1,0:T(4,128)S(1)}, u32[]{:S(2)}, u32[]{:S(2)}) async-start(f32[64,4,128]{2,1,0:T(4,128)} %bitcast.40), calls=%async_computation.7 | async-start | bytes 262144 | tf_op jit(solution)/shard_map/all_to_all | solution.py:175
  386.9 16.8 %all-to-all-done.7 = f32[64,4,128]{2,1,0:T(4,128)S(1)} async-done(((f32[64,4,128]{2,1,0:T(4,128)}), f32[64,4,128]{2,1,0:T(4,128)S(1)}, u32[]{:S(2)}, u32[]{:S(2)}) %all-to-all-start.7) | async-done | bytes 131104 | tf_op jit(solution)/shard_map/all_to_all | solution.py:175
  (86 shorter events, 31.8 us)
Async XLA Ops:
  0.6 80.5 %copy-start = (bf16[24,128,256]{2,1,0:T(8,128)(2,1)S(1)}, bf16[24,128,256]{2,1,0:T(8,128)(2,1)}, u32[]{:S(2)}) copy-start(bf16[24,128,256]{2,1,0:T(8,128)(2,1)} %param.19) | copy-start | bytes 4718596
  57.6 13.9 %copy-start.6 = (s32[192,1]{0,1:T(1,128)S(1)}, s32[192,1]{0,1:T(1,128)}, u32[]{:S(2)}) copy-start(s32[192,1]{0,1:T(1,128)} %param.20) | copy-start | bytes 2308
  57.7 14.7 %copy-start.4 = (s32[192]{0:T(256)S(1)}, s32[192]{0:T(256)}, u32[]{:S(2)}) copy-start(s32[192]{0:T(256)} %param.21) | copy-start | bytes 2308
  57.7 15.0 %copy-start.5 = (s32[192]{0:T(256)S(1)}, s32[192]{0:T(256)}, u32[]{:S(2)}) copy-start(s32[192]{0:T(256)} %param.22) | copy-start | bytes 2308
  57.7 16.5 %copy-start.3 = (f32[1536]{0:T(1024)S(1)}, f32[1536]{0:T(1024)}, u32[]{:S(2)}) copy-start(f32[1536]{0:T(1024)} %param.26) | copy-start | bytes 18436
  57.7 16.5 %copy-start.2 = (s32[8192]{0:T(1024)S(1)}, s32[8192]{0:T(1024)}, u32[]{:S(2)}) copy-start(s32[8192]{0:T(1024)} %param.23) | copy-start | bytes 98308
  61.7 18.7 %all-to-all-start = ((bf16[8,4,8960]{2,1,0:T(4,128)(2,1)}), bf16[8,4,8960]{2,1,0:T(4,128)(2,1)S(1)}, u32[]{:S(2)}, u32[]{:S(2)}) async-start(bf16[8,4,8960]{2,1,0:T(4,128)(2,1)} %broadcast_in_dim.56), calls=%async_computation | async-start | bytes 1146880 | tf_op jit(solution)/shard_map/all_to_all | solution.py:28
  88.7 10.1 %all-to-all-start.1 = ((f32[4,8,6,256]{3,0,2,1:T(4,128)}), f32[4,8,6,256]{3,0,2,1:T(4,128)S(1)}, u32[]{:S(2)}, u32[]{:S(2)}) async-start(f32[4,8,6,256]{3,0,2,1:T(4,128)} %bitcast.15), calls=%async_computation.1 | async-start | bytes 393216 | tf_op jit(solution)/shard_map/all_to_all | solution.py:149
  101.3 35.8 %copy-start.1 = (f32[4,8192]{1,0:T(4,128)S(1)}, f32[4,8192]{1,0:T(4,128)}, u32[]{:S(2)}) copy-start(f32[4,8192]{1,0:T(4,128)} %param.18) | copy-start | bytes 393220
  104.2 47.8 %copy-start.7 = (f32[3,256]{1,0:T(4,128)S(1)}, f32[3,256]{1,0:T(4,128)}, u32[]{:S(2)}) copy-start(f32[3,256]{1,0:T(4,128)} %param.27) | copy-start | bytes 9220
  137.8 31.6 %all-to-all-start.2 = ((f32[4,64,128]{2,0,1:T(4,128)}), f32[4,64,128]{2,0,1:T(4,128)S(1)}, u32[]{:S(2)}, u32[]{:S(2)}) async-start(f32[4,64,128]{2,0,1:T(4,128)} %fusion.19), calls=%async_computation.2 | async-start | bytes 262144 | tf_op jit(solution)/shard_map/all_to_all | solution.py:158
  311.7 58.6 %all-to-all-start.6 = ((f32[4,64,128]{2,0,1:T(4,128)}), f32[4,64,128]{2,0,1:T(4,128)S(1)}, u32[]{:S(2)}, u32[]{:S(2)}) async-start(f32[4,64,128]{2,0,1:T(4,128)} %fusion.16), calls=%async_computation.6 | async-start | bytes 262144 | tf_op jit(solution)/shard_map/all_to_all | solution.py:158
  374.9 28.8 %all-to-all-start.7 = ((f32[64,4,128]{2,1,0:T(4,128)}), f32[64,4,128]{2,1,0:T(4,128)S(1)}, u32[]{:S(2)}, u32[]{:S(2)}) async-start(f32[64,4,128]{2,1,0:T(4,128)} %bitcast.40), calls=%async_computation.7 | async-start | bytes 262144 | tf_op jit(solution)/shard_map/all_to_all | solution.py:175
where the time goes:
time: 405 us; the launch traced here: 404 us
  other arithmetic  109 us (27%)
  local copies, waits for them, and re-layouts  99.7 us (25%)
  blocking collectives  96 us (24%)
  starting transfers between devices  43.7 us (11%)
  waiting for transfers between devices  43.1 us (11%)
  matrix products  12.3 us (3%)
    scatter-add x2, other arithmetic, per_device(): injection = demand.at[:, unit_bus].add(power_time).astype(jnp.bfloat16)  92.7 us
    gather x4, local copies, waits for them, and re-layouts, per_device(): gradient = unit_cost + rho_weight * jnp.take(prices, unit_bus, axis=1)  65.7 us
    psum x4, blocking collectives, one_axis_at_a_time(): return functools.reduce(lax.psum, axes, array)  52.6 us
    all_to_all x1, blocking collectives, per_device(): lax.all_to_all(power_cols, TM, split_axis=0, concat_axis=1, tiled=True)  21 us
    all_to_all x2, starting transfers between devices, per_device(): lax.all_to_all(target, TM, split_axis=1, concat_axis=0, tiled=True)  18.8 us
    all_to_all x1, waiting for transfers between devices, per_device(): lax.all_to_all(power_cols, TM, split_axis=0, concat_axis=1, tiled=True)  16.8 us
    all_to_all x2, waiting for transfers between devices, per_device(): lax.all_to_all(target, TM, split_axis=1, concat_axis=0, tiled=True)  14.6 us
    all_to_all x1, blocking collectives, copy_for_each(): lax.all_to_all(jnp.broadcast_to(array[None], (count, *array.shape)), axis...  13.2 us
  transfers between devices with their start and end apart: 5, of which 4 were waited for; matrix products, arithmetic and copies ran while one was open for 2% of the time, Pallas kernels for 0%

commit v1 on v0

--- a/solution.py
+++ b/solution.py
@@ -115,7 +115,10 @@
     line_duals = jnp.zeros((block_steps, line_limit.shape[0]), jnp.float32)
     totals = []
     for repeat in range(ITERATIONS):
-        injection = demand.at[:, unit_bus].add(power_time).astype(jnp.bfloat16)
+        if repeat == 0:
+            injection = demand.astype(jnp.bfloat16)
+        else:
+            injection = demand.at[:, unit_bus].add(power_time).astype(jnp.bfloat16)
         gathered = collect(injection, AREA, 1)
         panels = jnp.take(
             gathered.reshape(block_steps, area_devices * col_blocks, panel_width),
@@ -174,7 +177,7 @@
         power_cols = jnp.clip(smoothed, -my_cap[None, :], my_cap[None, :])
         power_time = lax.all_to_all(power_cols, TM, split_axis=0, concat_axis=1, tiled=True)
     entries = float(horizon * line_limit.shape[0] * area_devices)
-    summed = one_axis_at_a_time(jnp.stack(totals), TM_AREA)
+    summed = lax.psum(jnp.stack(totals), TM_AREA)
     primal_rms = jnp.sqrt(summed / entries)
     return (power_time, line_duals, primal_rms)
 

time: 405 us -> 398 us (0.983)
  the two profiles are of different devices: /device:TPU:2 before, /device:TPU:8 now
where the time goes in v1:
time: 398 us; the launch traced here: 397 us
  blocking collectives  125 us (31%)
  local copies, waits for them, and re-layouts  93 us (23%)
  other arithmetic  63.2 us (16%)
  waiting for transfers between devices  51.9 us (13%)
  starting transfers between devices  49.4 us (12%)
  matrix products  12.9 us (3%)
    psum x1, blocking collectives, per_device(): summed = lax.psum(jnp.stack(totals), TM_AREA)  103 us
    gather x4, local copies, waits for them, and re-layouts, per_device(): gradient = unit_cost + rho_weight * jnp.take(prices, unit_bus, axis=1)  65.7 us
    scatter-add x1, other arithmetic, per_device(): injection = demand.at[:, unit_bus].add(power_time).astype(jnp.bfloat16)  44.2 us
    all_to_all x2, waiting for transfers between devices, per_device(): lax.all_to_all(power_cols, TM, split_axis=0, concat_axis=1, tiled=True)  28.2 us
    all_to_all x2, starting transfers between devices, per_device(): lax.all_to_all(target, TM, split_axis=1, concat_axis=0, tiled=True)  24.5 us
    all_to_all x2, starting transfers between devices, per_device(): lax.all_to_all(power_cols, TM, split_axis=0, concat_axis=1, tiled=True)  17.2 us
    all_to_all x2, waiting for transfers between devices, per_device(): lax.all_to_all(target, TM, split_axis=1, concat_axis=0, tiled=True)  13.5 us
    all_to_all x1, blocking collectives, copy_for_each(): lax.all_to_all(jnp.broadcast_to(array[None], (count, *array.shape)), axis...  13.3 us
  transfers between devices with their start and end apart: 6, of which 5 were waited for; matrix products, arithmetic and copies ran while one was open for 4% of the time, Pallas kernels for 0%

profile of v1, /device:TPU:8, one launch (start us, length us, event | category | flops | bytes accessed | tf_op | source)
XLA Modules:
  0.0 396.6 jit_solution(17762997398970816326)
XLA Ops:
  2.7 4.3 %all-to-all-start = ((bf16[8,4,8960]{2,1,0:T(4,128)(2,1)}), bf16[8,4,8960]{2,1,0:T(4,128)(2,1)S(1)}, u32[]{:S(2)}, u32[]{:S(2)}) async-start(bf16[8,4,8960]{2,1,0:T(4,128)(2,1)} %broadcast_in_dim.55), calls=%async_computation | async-start | bytes 1146880 | tf_op jit(solution)/shard_map/all_to_all | solution.py:28
  14.3 3.5 all-to-all-done
  19.0 1.7 scatter_fusion
  22.4 3.6 scatter_fusion.1
  26.0 3.4 all-to-all-start.1
  29.5 6.7 %all-to-all-done.1 = f32[4,8,6,256]{3,0,2,1:T(4,128)S(1)} async-done(((f32[4,8,6,256]{3,0,2,1:T(4,128)}), f32[4,8,6,256]{3,0,2,1:T(4,128)S(1)}, u32[]{:S(2)}, u32[]{:S(2)}) %all-to-all-start.1) | async-done | bytes 196640 | tf_op jit(solution)/shard_map/all_to_all | solution.py:152
  36.2 2.3 scatter_fusion.2
  38.6 2.8 copy.80
  41.4 30.0 %gather_fusion.2 = f32[8192,4]{1,0:T(8,128)} fusion(f32[4,8960]{0,1:T(8,128)} %copy.80, s32[8192]{0:T(1024)S(1)} %get-tuple-element.26), kind=kCustom, calls=%fused_computation.2.clone | custom fusion | bytes 294912 | tf_op jit(solution)/shard_map/jit(_take)/gather | solution.py:159
  71.4 2.8 copy.81
  75.0 18.7 %all-to-all-start.2 = ((f32[4,64,128]{2,0,1:T(4,128)}), f32[4,64,128]{2,0,1:T(4,128)S(1)}, u32[]{:S(2)}, u32[]{:S(2)}) async-start(f32[4,64,128]{2,0,1:T(4,128)} %fusion.17), calls=%async_computation.2 | async-start | bytes 262144 | tf_op jit(solution)/shard_map/all_to_all | solution.py:161
  96.5 13.5 %all-to-all-done.2 = f32[4,64,128]{2,0,1:T(4,128)S(1)} async-done(((f32[4,64,128]{2,0,1:T(4,128)}), f32[4,64,128]{2,0,1:T(4,128)S(1)}, u32[]{:S(2)}, u32[]{:S(2)}) %all-to-all-start.2) | async-done | bytes 131104 | tf_op jit(solution)/shard_map/all_to_all | solution.py:161
  110.0 2.2 fusion.20
  112.3 2.3 fusion.1
  114.6 5.6 %all-to-all-start.3 = ((f32[64,4,128]{2,1,0:T(4,128)}), f32[64,4,128]{2,1,0:T(4,128)S(1)}, u32[]{:S(2)}, u32[]{:S(2)}) async-start(f32[64,4,128]{2,1,0:T(4,128)} %bitcast.23), calls=%async_computation.3 | async-start | bytes 262144 | tf_op jit(solution)/shard_map/all_to_all | solution.py:178
  120.3 2.8 copy.83
  123.0 12.8 %all-to-all-done.3 = f32[64,4,128]{2,1,0:T(4,128)S(1)} async-done(((f32[64,4,128]{2,1,0:T(4,128)}), f32[64,4,128]{2,1,0:T(4,128)S(1)}, u32[]{:S(2)}, u32[]{:S(2)}) %all-to-all-start.3) | async-done | bytes 131104 | tf_op jit(solution)/shard_map/all_to_all | solution.py:178
  135.8 2.7 copy.84
  138.5 44.2 %scatter_fusion.3 = f32[4,8960]{0,1:T(8,128)} fusion(f32[4,8960]{0,1:T(8,128)} %copy.83, s32[8192]{0:T(1024)S(1)} %get-tuple-element.25, f32[8192,4]{1,0:T(8,128)} %copy.84), kind=kCustom, calls=%fused_computation.9 | custom fusion | flops 32768 | bytes 425984 | tf_op jit(solution)/shard_map/scatter-add | solution.py:121
  182.7 3.0 copy.85
  185.9 13.3 %all_to_all.96 = bf16[8,4,8960]{2,1,0:T(4,128)(2,1)S(1)} all-to-all(bf16[8,4,8960]{2,1,0:T(4,128)(2,1)S(1)} %broadcast_in_dim.60), channel_id=1, replica_groups=mesh['tm_0'=16,'tm_1'=4,'area_0'=4,'area_1'=2] {'area_0','area_1'}, dimensions={0} | all-to-all | bytes 1146880 | tf_op jit(solution)/shard_map/all_to_all | solution.py:28
  205.2 9.2 %all_to_all.97 = f32[4,8,6,256]{3,0,2,1:T(4,128)S(1)} all-to-all(f32[4,8,6,256]{3,0,2,1:T(4,128)S(1)} %bitcast.125), channel_id=1, replica_groups=mesh['tm_0'=16,'tm_1'=4,'area_0'=4,'area_1'=2] {'area_0','area_1'}, dimensions={1} | all-to-all | bytes 393216 | tf_op jit(solution)/shard_map/all_to_all | solution.py:152
  214.5 2.3 scatter_fusion.6
  216.8 2.8 copy.88
  219.6 30.0 %gather_fusion.5 = f32[8192,4]{1,0:T(8,128)} fusion(f32[4,8960]{0,1:T(8,128)} %copy.88, s32[8192]{0:T(1024)S(1)} %get-tuple-element.26), kind=kCustom, calls=%fused_computation.5.clone | custom fusion | bytes 294912 | tf_op jit(solution)/shard_map/jit(_take)/gather | solution.py:159
  249.6 2.8 copy.89
  253.2 5.8 %all-to-all-start.6 = ((f32[4,64,128]{2,0,1:T(4,128)}), f32[4,64,128]{2,0,1:T(4,128)S(1)}, u32[]{:S(2)}, u32[]{:S(2)}) async-start(f32[4,64,128]{2,0,1:T(4,128)} %fusion.14), calls=%async_computation.6 | async-start | bytes 262144 | tf_op jit(solution)/shard_map/all_to_all | solution.py:161
  260.4 102.7 %psum.7 = f32[2]{0:T(128)S(1)} all-reduce(f32[2]{0:T(128)S(1)} %pad_maximum_fusion.6), channel_id=1, replica_groups=mesh['tm_0'=16,'tm_1'=4,'area_0'=4,'area_1'=2] {'tm_0','tm_1','area_0','..., use_global_device_ids=true, to_apply=%region_12.16 | all-reduce | flops 2 | bytes 16 | tf_op jit(solution)/shard_map/psum | solution.py:180
  363.1 2.2 fusion.18
  365.4 2.3 fusion
  367.7 11.6 %all-to-all-start.7 = ((f32[64,4,128]{2,1,0:T(4,128)}), f32[64,4,128]{2,1,0:T(4,128)S(1)}, u32[]{:S(2)}, u32[]{:S(2)}) async-start(f32[64,4,128]{2,1,0:T(4,128)} %bitcast.40), calls=%async_computation.7 | async-start | bytes 262144 | tf_op jit(solution)/shard_map/all_to_all | solution.py:178
  380.5 15.4 %all-to-all-done.7 = f32[64,4,128]{2,1,0:T(4,128)S(1)} async-done(((f32[64,4,128]{2,1,0:T(4,128)}), f32[64,4,128]{2,1,0:T(4,128)S(1)}, u32[]{:S(2)}, u32[]{:S(2)}) %all-to-all-start.7) | async-done | bytes 131104 | tf_op jit(solution)/shard_map/all_to_all | solution.py:178
  (76 shorter events, 26.0 us)
Async XLA Ops:
  0.6 17.8 %copy-start = (bf16[24,128,256]{2,1,0:T(8,128)(2,1)S(1)}, bf16[24,128,256]{2,1,0:T(8,128)(2,1)}, u32[]{:S(2)}) copy-start(bf16[24,128,256]{2,1,0:T(8,128)(2,1)} %param.19) | copy-start | bytes 4718596
  0.6 20.1 %copy-start.3 = (f32[1536]{0:T(1024)S(1)}, f32[1536]{0:T(1024)}, u32[]{:S(2)}) copy-start(f32[1536]{0:T(1024)} %param.26) | copy-start | bytes 18436
  2.7 15.1 %all-to-all-start = ((bf16[8,4,8960]{2,1,0:T(4,128)(2,1)}), bf16[8,4,8960]{2,1,0:T(4,128)(2,1)S(1)}, u32[]{:S(2)}, u32[]{:S(2)}) async-start(bf16[8,4,8960]{2,1,0:T(4,128)(2,1)} %broadcast_in_dim.55), calls=%async_computation | async-start | bytes 1146880 | tf_op jit(solution)/shard_map/all_to_all | solution.py:28
  26.0 10.1 %all-to-all-start.1 = ((f32[4,8,6,256]{3,0,2,1:T(4,128)}), f32[4,8,6,256]{3,0,2,1:T(4,128)S(1)}, u32[]{:S(2)}, u32[]{:S(2)}) async-start(f32[4,8,6,256]{3,0,2,1:T(4,128)} %bitcast.15), calls=%async_computation.1 | async-start | bytes 393216 | tf_op jit(solution)/shard_map/all_to_all | solution.py:152
  38.6 35.7 %copy-start.2 = (f32[4,8192]{1,0:T(4,128)S(1)}, f32[4,8192]{1,0:T(4,128)}, u32[]{:S(2)}) copy-start(f32[4,8192]{1,0:T(4,128)} %param.18) | copy-start | bytes 393220
  41.4 52.3 %copy-start.4 = (f32[3,256]{1,0:T(4,128)S(1)}, f32[3,256]{1,0:T(4,128)}, u32[]{:S(2)}) copy-start(f32[3,256]{1,0:T(4,128)} %param.27) | copy-start | bytes 9220
  74.2 46.0 %copy-start.1 = (f32[4,8960]{1,0:T(4,128)S(1)}, f32[4,8960]{1,0:T(4,128)}, u32[]{:S(2)}) copy-start(f32[4,8960]{1,0:T(4,128)} %param.17) | copy-start | bytes 430084
  75.0 35.0 %all-to-all-start.2 = ((f32[4,64,128]{2,0,1:T(4,128)}), f32[4,64,128]{2,0,1:T(4,128)S(1)}, u32[]{:S(2)}, u32[]{:S(2)}) async-start(f32[4,64,128]{2,0,1:T(4,128)} %fusion.17), calls=%async_computation.2 | async-start | bytes 262144 | tf_op jit(solution)/shard_map/all_to_all | solution.py:161
  114.6 21.2 %all-to-all-start.3 = ((f32[64,4,128]{2,1,0:T(4,128)}), f32[64,4,128]{2,1,0:T(4,128)S(1)}, u32[]{:S(2)}, u32[]{:S(2)}) async-start(f32[64,4,128]{2,1,0:T(4,128)} %bitcast.23), calls=%async_computation.3 | async-start | bytes 262144 | tf_op jit(solution)/shard_map/all_to_all | solution.py:178
  253.2 109.9 %all-to-all-start.6 = ((f32[4,64,128]{2,0,1:T(4,128)}), f32[4,64,128]{2,0,1:T(4,128)S(1)}, u32[]{:S(2)}, u32[]{:S(2)}) async-start(f32[4,64,128]{2,0,1:T(4,128)} %fusion.14), calls=%async_computation.6 | async-start | bytes 262144 | tf_op jit(solution)/shard_map/all_to_all | solution.py:161
  367.7 28.2 %all-to-all-start.7 = ((f32[64,4,128]{2,1,0:T(4,128)}), f32[64,4,128]{2,1,0:T(4,128)S(1)}, u32[]{:S(2)}, u32[]{:S(2)}) async-start(f32[64,4,128]{2,1,0:T(4,128)} %bitcast.40), calls=%async_computation.7 | async-start | bytes 262144 | tf_op jit(solution)/shard_map/all_to_all | solution.py:178

commit v2 on v1

--- a/solution.py
+++ b/solution.py
@@ -6,6 +6,7 @@
 from jax import lax
 from jax.sharding import Mesh
 from jax.sharding import PartitionSpec as P
+from jax.experimental import pallas as pl
 
 ITERATIONS = 2
 TM = ("tm_0", "tm_1")
@@ -32,6 +33,94 @@
 
 def collect(array, axis, dim):
     return laid_out(copy_for_each(array, axis), dim)
+
+
+PARTS = 3
+ROWS = 16
+UNIT_BLOCK = 1024
+
+
+def split_parts(values):
+    pieces = []
+    rest = values
+    for _ in range(PARTS):
+        piece = rest.astype(jnp.bfloat16)
+        pieces.append(piece)
+        rest = rest - piece.astype(jnp.float32)
+    return pieces
+
+
+def gather_kernel(table_ref, lo_ref, hi_ref, out_ref):
+    lanes = table_ref.shape[1]
+    width = lo_ref.shape[1]
+    onehot = (lax.broadcasted_iota(jnp.int32, (lanes, width), 0) == lo_ref[...]).astype(jnp.bfloat16)
+    picked = jnp.dot(table_ref[...], onehot, preferred_element_type=jnp.float32)
+    hi = hi_ref[...]
+    total = jnp.zeros((ROWS, width), jnp.float32)
+    for block in range(table_ref.shape[0] // ROWS):
+        total = total + jnp.where(hi == block, picked[block * ROWS : (block + 1) * ROWS], 0.0)
+    out_ref[...] = total
+
+
+def bus_to_units(prices, lo_row, hi_row):
+    steps, buses = prices.shape
+    panel = 256
+    blocks = buses // panel
+    units = lo_row.shape[1]
+    pieces = split_parts(prices.reshape(steps, blocks, panel))
+    stacked = jnp.stack(pieces, axis=1).reshape(steps * PARTS, blocks, panel)
+    stacked = jnp.pad(stacked, ((0, ROWS - steps * PARTS), (0, 0), (0, 0)))
+    table = jnp.transpose(stacked, (1, 0, 2)).reshape(blocks * ROWS, panel)
+    picked = pl.pallas_call(
+        gather_kernel,
+        grid=(units // UNIT_BLOCK,),
+        in_specs=[
+            pl.BlockSpec((blocks * ROWS, panel), lambda i: (0, 0)),
+            pl.BlockSpec((1, UNIT_BLOCK), lambda i: (0, i)),
+            pl.BlockSpec((1, UNIT_BLOCK), lambda i: (0, i)),
+        ],
+        out_specs=pl.BlockSpec((ROWS, UNIT_BLOCK), lambda i: (0, i)),
+        out_shape=jax.ShapeDtypeStruct((ROWS, units), jnp.float32),
+    )(table, lo_row, hi_row)
+    parts = picked[: steps * PARTS].reshape(steps, PARTS, units)
+    return parts[:, 0] + parts[:, 1] + parts[:, 2]
+
+
+def scatter_kernel(parts_ref, lo_ref, hi_ref, out_ref):
+    @pl.when(pl.program_id(0) == 0)
+    def _():
+        out_ref[...] = jnp.zeros(out_ref.shape, out_ref.dtype)
+
+    width = parts_ref.shape[1]
+    lanes = out_ref.shape[1]
+    onehot = (lax.broadcasted_iota(jnp.int32, (width, lanes), 1) == lo_ref[...]).astype(jnp.bfloat16)
+    parts = parts_ref[...]
+    hi = hi_ref[...]
+    masked = jnp.concatenate(
+        [jnp.where(hi == block, parts, jnp.zeros_like(parts)) for block in range(out_ref.shape[0] // ROWS)],
+        axis=0,
+    )
+    out_ref[...] += jnp.dot(masked, onehot, preferred_element_type=jnp.float32)
+
+
+def units_to_bus(power, lo_col, hi_row, blocks, panel):
+    steps, units = power.shape
+    pieces = split_parts(power)
+    parts = jnp.concatenate(pieces + [jnp.zeros((ROWS - steps * PARTS, units), jnp.bfloat16)], axis=0)
+    summed = pl.pallas_call(
+        scatter_kernel,
+        grid=(units // UNIT_BLOCK,),
+        in_specs=[
+            pl.BlockSpec((ROWS, UNIT_BLOCK), lambda i: (0, i)),
+            pl.BlockSpec((UNIT_BLOCK, 1), lambda i: (i, 0)),
+            pl.BlockSpec((1, UNIT_BLOCK), lambda i: (0, i)),
+        ],
+        out_specs=pl.BlockSpec((blocks * ROWS, panel), lambda i: (0, 0)),
+        out_shape=jax.ShapeDtypeStruct((blocks * ROWS, panel), jnp.float32),
+    )(parts, lo_col, hi_row)
+    summed = summed.reshape(blocks, ROWS, panel)[:, : steps * PARTS].reshape(blocks, PARTS, steps, panel)
+    summed = summed[:, 0] + summed[:, 1] + summed[:, 2]
+    return jnp.transpose(summed, (1, 0, 2)).reshape(steps, blocks * panel)
 
 
 def one_axis_at_a_time(array, axes):
@@ -111,6 +200,9 @@
     empty_row = jnp.zeros((1, unit_width), jnp.float32)
     kernel_real = unit_spectrum[: half_steps + 1]
     kernel_imag = jnp.concatenate([empty_row, unit_spectrum[half_steps + 1 :], empty_row], axis=0)
+    lo_row = (unit_bus % panel_width).reshape(1, unit_area)
+    hi_row = (unit_bus // panel_width).reshape(1, unit_area)
+    lo_col = lo_row.reshape(unit_area, 1)
     power_time = jnp.zeros((block_steps, unit_area), jnp.float32)
     line_duals = jnp.zeros((block_steps, line_limit.shape[0]), jnp.float32)
     totals = []
@@ -118,7 +210,9 @@
         if repeat == 0:
             injection = demand.astype(jnp.bfloat16)
         else:
-            injection = demand.at[:, unit_bus].add(power_time).astype(jnp.bfloat16)
+            injection = (demand + units_to_bus(power_time, lo_col, hi_row, col_blocks, panel_width)).astype(
+                jnp.bfloat16
+            )
         gathered = collect(injection, AREA, 1)
         panels = jnp.take(
             gathered.reshape(block_steps, area_devices * col_blocks, panel_width),
@@ -149,14 +243,25 @@
             .set(contrib)
         )
         outbound = outbound.reshape(block_steps, area_devices, capacity, panel_width)
+        last = repeat == ITERATIONS - 1
+        if last:
+            extra = (
+                jnp.zeros((block_steps, area_devices, 1, panel_width), jnp.float32)
+                .at[0, :, 0, :ITERATIONS]
+                .set(jnp.broadcast_to(jnp.stack(totals), (area_devices, ITERATIONS)))
+            )
+            outbound = jnp.concatenate([outbound, extra], axis=2)
         returned = lax.all_to_all(outbound, AREA, split_axis=1, concat_axis=1, tiled=True)
+        if last:
+            area_totals = jnp.sum(returned[0, :, capacity, :ITERATIONS], axis=0)
+            returned = returned[:, :, :capacity]
         prices = (
             jnp.zeros((block_steps, col_blocks, panel_width), jnp.float32)
             .at[:, send_block]
             .add(returned.reshape(block_steps, area_devices * capacity, panel_width))
         )
         prices = prices.reshape(block_steps, bus_area)
-        gradient = unit_cost + rho_weight * jnp.take(prices, unit_bus, axis=1)
+        gradient = unit_cost + rho_weight * bus_to_units(prices, lo_row, hi_row)
         target = power_time - step_size * gradient
         columns = lax.all_to_all(target, TM, split_axis=1, concat_axis=0, tiled=True)
         spectrum = jnp.dot(
@@ -175,9 +280,21 @@
             preferred_element_type=jnp.float32,
         )
         power_cols = jnp.clip(smoothed, -my_cap[None, :], my_cap[None, :])
-        power_time = lax.all_to_all(power_cols, TM, split_axis=0, concat_axis=1, tiled=True)
+        if last:
+            chunks = power_cols.reshape(time_devices, block_steps, unit_width)
+            extra = (
+                jnp.zeros((time_devices, 1, unit_width), jnp.float32)
+                .at[:, 0, :ITERATIONS]
+                .set(jnp.broadcast_to(area_totals, (time_devices, ITERATIONS)))
+            )
+            received = lax.all_to_all(
+                jnp.concatenate([chunks, extra], axis=1), TM, split_axis=0, concat_axis=0, tiled=True
+            )
+            summed = jnp.sum(received[:, block_steps, :ITERATIONS], axis=0)
+            power_time = jnp.transpose(received[:, :block_steps], (1, 0, 2)).reshape(block_steps, unit_area)
+        else:
+            power_time = lax.all_to_all(power_cols, TM, split_axis=0, concat_axis=1, tiled=True)
     entries = float(horizon * line_limit.shape[0] * area_devices)
-    summed = lax.psum(jnp.stack(totals), TM_AREA)
     primal_rms = jnp.sqrt(summed / entries)
     return (power_time, line_duals, primal_rms)
 

time: 398 us -> 219 us (0.55)
  the two profiles are of different devices: /device:TPU:8 before, /device:TPU:2 now
where the time goes in v2:
time: 219 us; the launch traced here: 217 us
  waiting for transfers between devices  78.2 us (36%)
  starting transfers between devices  42.1 us (19%)
  blocking collectives  23 us (11%)
  local copies, waits for them, and re-layouts  20.7 us (9%)
  Pallas kernels  20.4 us (9%)
  other arithmetic  19.5 us (9%)
  matrix products  12.3 us (6%)
    all_to_all x2, waiting for transfers between devices, per_device(): lax.all_to_all(target, TM, split_axis=1, concat_axis=0, tiled=True)  32.2 us
    all_to_all x1, waiting for transfers between devices, per_device(): lax.all_to_all(jnp.concatenate([chunks, extra], axis=1), TM, split_axis=0...  20.9 us
    all_to_all x2, starting transfers between devices, per_device(): lax.all_to_all(target, TM, split_axis=1, concat_axis=0, tiled=True)  18.8 us
    all_to_all x1, waiting for transfers between devices, per_device(): lax.all_to_all(power_cols, TM, split_axis=0, concat_axis=1, tiled=True)  14.1 us
    all_to_all x1, blocking collectives, copy_for_each(): lax.all_to_all(jnp.broadcast_to(array[None], (count, *array.shape)), axis...  13.5 us
    pallas_call x2, Pallas kernels, bus_to_units(): pl.pallas_call(gather_kernel, grid=(units // UNIT_BLOCK,), in_specs=[pl.B...  12.4 us
    all_to_all x1, blocking collectives, per_device(): lax.all_to_all(outbound, AREA, split_axis=1, concat_axis=1, tiled=True)  9.57 us
    all_to_all x1, starting transfers between devices, copy_for_each(): lax.all_to_all(jnp.broadcast_to(array[None], (count, *array.shape)), axis...  9.33 us
  transfers between devices with their start and end apart: 6, of which 6 were waited for; matrix products, arithmetic and copies ran while one was open for 5% of the time, Pallas kernels for 0%

profile of v2, /device:TPU:2, one launch (start us, length us, event | category | flops | bytes accessed | tf_op | source)
XLA Modules:
  0.0 217.4 jit_solution(2245267648249690515)
XLA Ops:
  2.7 9.3 %all-to-all-start = ((bf16[8,4,8960]{2,1,0:T(4,128)(2,1)}), bf16[8,4,8960]{2,1,0:T(4,128)(2,1)S(1)}, u32[]{:S(2)}, u32[]{:S(2)}) async-start(bf16[8,4,8960]{2,1,0:T(4,128)(2,1)} %broadcast_in_dim.46), calls=%async_computation | async-start | bytes 1146880 | tf_op jit(solution)/shard_map/all_to_all | solution.py:29
  15.8 5.6 %all-to-all-done = bf16[8,4,8960]{2,1,0:T(4,128)(2,1)S(1)} async-done(((bf16[8,4,8960]{2,1,0:T(4,128)(2,1)}), bf16[8,4,8960]{2,1,0:T(4,128)(2,1)S(1)}, u32[]{:S(2)}, u32[]{:S(2)}) %all-to-all-start) | async-done | bytes 573472 | tf_op jit(solution)/shard_map/all_to_all | solution.py:29
  22.6 1.7 scatter_fusion
  26.0 3.6 %scatter_fusion.1 = f32[4,48,256]{2,0,1:T(4,128)} fusion(f32[4,48,256]{2,0,1:T(4,128)} %broadcast.322.clone, s32[24]{0:T(128)S(1)} %get-tuple-element.66, f32[24,4,256]{2,1,0:T(4,128)S(1)} %fusion.49), kind=kCustom, calls=%fused_computation.5 | custom fusion | bytes 295008 | tf_op jit(solution)/shard_map/scatter | solution.py:243
  29.7 4.7 %all-to-all-start.1 = ((f32[4,8,6,256]{3,0,2,1:T(4,128)}), f32[4,8,6,256]{3,0,2,1:T(4,128)S(1)}, u32[]{:S(2)}, u32[]{:S(2)}) async-start(f32[4,8,6,256]{3,0,2,1:T(4,128)} %bitcast.15), calls=%async_computation.1 | async-start | bytes 393216 | tf_op jit(solution)/shard_map/all_to_all | solution.py:254
  34.4 5.4 %all-to-all-done.1 = f32[4,8,6,256]{3,0,2,1:T(4,128)S(1)} async-done(((f32[4,8,6,256]{3,0,2,1:T(4,128)}), f32[4,8,6,256]{3,0,2,1:T(4,128)S(1)}, u32[]{:S(2)}, u32[]{:S(2)}) %all-to-all-start.1) | async-done | bytes 196640 | tf_op jit(solution)/shard_map/all_to_all | solution.py:254
  39.8 2.4 %scatter_fusion.2 = f32[4,35,256]{2,0,1:T(4,128)S(1)} fusion(f32[4,35,256]{2,0,1:T(4,128)S(1)} %broadcast.317.clone, s32[48]{0:T(128)S(1)} %fusion.73, f32[48,4,256]{2,1,0:T(4,128)S(1)} %bitcast.181), kind=kCustom, calls=%fused_computation.6 | custom fusion | flops 49152 | bytes 590016 | tf_op jit(solution)/shard_map/scatter-add | solution.py:261
  43.3 6.2 %shard_map.130 = f32[16,8192]{1,0:T(8,128)} custom-call(bf16[560,256]{1,0:T(8,128)(2,1)} %bitcast.178, s32[1,8192]{1,0:T(1,128)} %bitcast.189, s32[1,8192]{1,0:T(1,128)} %bitcast.186), custom_call_target="tpu_custom_call" | custom-call | tf_op jit(solution)/shard_map/pallas_call | solution.py:74
  49.4 1.2 reshape.384
  51.9 14.2 %all-to-all-start.2 = ((f32[4,64,128]{2,0,1:T(4,128)}), f32[4,64,128]{2,0,1:T(4,128)S(1)}, u32[]{:S(2)}, u32[]{:S(2)}) async-start(f32[4,64,128]{2,0,1:T(4,128)} %fusion.22), calls=%async_computation.2 | async-start | bytes 262144 | tf_op jit(solution)/shard_map/all_to_all | solution.py:266
  66.1 1.6 fusion.24
  68.9 14.6 %all-to-all-done.2 = f32[4,64,128]{2,0,1:T(4,128)S(1)} async-done(((f32[4,64,128]{2,0,1:T(4,128)}), f32[4,64,128]{2,0,1:T(4,128)S(1)}, u32[]{:S(2)}, u32[]{:S(2)}) %all-to-all-start.2) | async-done | bytes 131104 | tf_op jit(solution)/shard_map/all_to_all | solution.py:266
  83.5 2.2 %fusion.25 = f32[256,128]{1,0:T(8,128)S(1)} fusion(f32[256,128]{1,0:T(8,128)S(1)} %bitcast.192, s32[256]{0:T(256)S(1)} %get-tuple-element.34, pred[256]{0:T(512)(128)(4,1)S(1)} %iota_compare_fusion.4), kind=kOutput, calls=%fused_computation.65 | convolution fusion | flops 101711872 | bytes 263424 | tf_op jit(solution)/shard_map/dot_general | solution.py:267
  85.8 2.3 %fusion.1 = f32[256,128]{1,0:T(8,128)} fusion(f32[127,128]{1,0:T(8,128)S(1)} %fusion.34, f32[129,128]{1,0:T(8,128)S(1)} %get-tuple-element.55, s32[256]{0:T(256)S(1)} %get-tuple-element.34, pred[256]{0:T(512)(128)(4,1)S(1)} %iota_compare_fusion.4, f32[256]{0:T(256)S(1)} %get-tuple-element.33, f32[128]{0:T(128)S(1)} %get-tuple-element.31, ...), kind=kOutput, calls=%fused_computation.13 | convolution fusion | flops 101842944 | bytes 265472 | tf_op jit(solution)/shard_map/dot_general | solution.py:275
  88.1 4.6 %all-to-all-start.3 = ((f32[64,4,128]{2,1,0:T(4,128)}), f32[64,4,128]{2,1,0:T(4,128)S(1)}, u32[]{:S(2)}, u32[]{:S(2)}) async-start(f32[64,4,128]{2,1,0:T(4,128)} %bitcast.30), calls=%async_computation.3 | async-start | bytes 262144 | tf_op jit(solution)/shard_map/all_to_all | solution.py:296
  92.8 2.6 %copy.68.lo_ref = s32[8192,1]{1,0:T(8,128)} copy(s32[8192,1]{0,1:T(1,128)S(1)} %bitcast.191) | data formatting | bytes 65536 | tf_op jit(solution)/shard_map/reshape;reshape | solution.py:205
  95.5 14.1 %all-to-all-done.3 = f32[64,4,128]{2,1,0:T(4,128)S(1)} async-done(((f32[64,4,128]{2,1,0:T(4,128)}), f32[64,4,128]{2,1,0:T(4,128)S(1)}, u32[]{:S(2)}, u32[]{:S(2)}) %all-to-all-start.3) | async-done | bytes 131104 | tf_op jit(solution)/shard_map/all_to_all | solution.py:296
  110.5 8.1 %shard_map.131 = f32[560,256]{1,0:T(8,128)} custom-call(bf16[16,8192]{1,0:T(8,128)(2,1)} %maximum_maximum_fusion.parts_ref, s32[8192,1]{1,0:T(8,128)} %copy.68.lo_ref, s32[1,8192]{1,0:T(1,128)} %bitcast.187), custom_call_target="tpu_custom_call" | custom-call | tf_op jit(solution)/shard_map/pallas_call | solution.py:110
  118.5 1.3 copy.82
  120.2 13.5 %all_to_all.83 = bf16[8,4,8960]{2,1,0:T(4,128)(2,1)S(1)} all-to-all(bf16[8,4,8960]{2,1,0:T(4,128)(2,1)S(1)} %broadcast_in_dim.51), channel_id=1, replica_groups=mesh['tm_0'=16,'tm_1'=4,'area_0'=4,'area_1'=2] {'area_0','area_1'}, dimensions={0} | all-to-all | bytes 1146880 | tf_op jit(solution)/shard_map/all_to_all | solution.py:29
  134.8 1.7 scatter_fusion.3
  138.2 1.5 scatter_fusion.4
  139.7 1.4 maximum_bitcast_fusion
  141.2 9.6 %all_to_all.82 = f32[4,8,7,256]{3,0,2,1:T(4,128)S(1)} all-to-all(f32[4,8,7,256]{3,0,2,1:T(4,128)S(1)} %pad_maximum_fusion.1), channel_id=1, replica_groups=mesh['tm_0'=16,'tm_1'=4,'area_0'=4,'area_1'=2] {'area_0','area_1'}, dimensions={1} | all-to-all | bytes 458752 | tf_op jit(solution)/shard_map/all_to_all | solution.py:254
  150.8 2.4 %scatter_fusion.5 = f32[4,35,256]{2,0,1:T(4,128)S(1)} fusion(f32[4,35,256]{2,0,1:T(4,128)S(1)} %broadcast.317, s32[48]{0:T(128)S(1)} %fusion.73, f32[48,4,256]{2,1,0:T(4,128)S(1)} %bitcast.182), kind=kCustom, calls=%fused_computation.9 | custom fusion | flops 49152 | bytes 590016 | tf_op jit(solution)/shard_map/scatter-add | solution.py:261
  154.2 6.2 %shard_map.132 = f32[16,8192]{1,0:T(8,128)} custom-call(bf16[560,256]{1,0:T(8,128)(2,1)} %bitcast.177, s32[1,8192]{1,0:T(1,128)} %bitcast.190, s32[1,8192]{1,0:T(1,128)} %bitcast.188), custom_call_target="tpu_custom_call" | custom-call | tf_op jit(solution)/shard_map/pallas_call | solution.py:74
  162.9 4.6 %all-to-all-start.6 = ((f32[4,64,128]{2,0,1:T(4,128)}), f32[4,64,128]{2,0,1:T(4,128)S(1)}, u32[]{:S(2)}, u32[]{:S(2)}) async-start(f32[4,64,128]{2,0,1:T(4,128)} %fusion.17), calls=%async_computation.6 | async-start | bytes 262144 | tf_op jit(solution)/shard_map/all_to_all | solution.py:266
  167.5 17.7 %all-to-all-done.6 = f32[4,64,128]{2,0,1:T(4,128)S(1)} async-done(((f32[4,64,128]{2,0,1:T(4,128)}), f32[4,64,128]{2,0,1:T(4,128)S(1)}, u32[]{:S(2)}, u32[]{:S(2)}) %all-to-all-start.6) | async-done | bytes 131104 | tf_op jit(solution)/shard_map/all_to_all | solution.py:266
  185.2 2.2 %fusion.23 = f32[256,128]{1,0:T(8,128)S(1)} fusion(f32[256,128]{1,0:T(8,128)S(1)} %bitcast.193, s32[256]{0:T(256)S(1)} %get-tuple-element.34, pred[256]{0:T(512)(128)(4,1)S(1)} %iota_compare_fusion.4), kind=kOutput, calls=%fused_computation.63 | convolution fusion | flops 101711872 | bytes 263424 | tf_op jit(solution)/shard_map/dot_general | solution.py:267
  187.5 1.7 fusion
  190.0 4.6 %all-to-all-start.7 = ((f32[64,5,128]{2,1,0:T(8,128)}), f32[64,5,128]{2,1,0:T(8,128)S(1)}, u32[]{:S(2)}, u32[]{:S(2)}) async-start(f32[64,5,128]{2,1,0:T(8,128)} %pad_maximum_fusion), calls=%async_computation.7 | async-start | bytes 524288 | tf_op jit(solution)/shard_map/all_to_all | solution.py:290
  195.2 20.9 %all-to-all-done.7 = f32[64,5,128]{2,1,0:T(8,128)S(1)} async-done(((f32[64,5,128]{2,1,0:T(8,128)}), f32[64,5,128]{2,1,0:T(8,128)S(1)}, u32[]{:S(2)}, u32[]{:S(2)}) %all-to-all-start.7) | async-done | bytes 163872 | tf_op jit(solution)/shard_map/all_to_all | solution.py:290
  (110 shorter events, 22.4 us)
Async XLA Ops:
  0.6 21.4 %copy-start = (bf16[24,128,256]{2,1,0:T(8,128)(2,1)S(1)}, bf16[24,128,256]{2,1,0:T(8,128)(2,1)}, u32[]{:S(2)}) copy-start(bf16[24,128,256]{2,1,0:T(8,128)(2,1)} %param.21) | copy-start | bytes 4718596
  0.6 11.9 %copy-start.8 = (s32[192,1]{0,1:T(1,128)S(1)}, s32[192,1]{0,1:T(1,128)}, u32[]{:S(2)}) copy-start(s32[192,1]{0,1:T(1,128)} %param.22) | copy-start | bytes 2308
  0.7 12.6 %copy-start.6 = (s32[192]{0:T(256)S(1)}, s32[192]{0:T(256)}, u32[]{:S(2)}) copy-start(s32[192]{0:T(256)} %param.23) | copy-start | bytes 2308
  0.7 12.9 %copy-start.7 = (s32[192]{0:T(256)S(1)}, s32[192]{0:T(256)}, u32[]{:S(2)}) copy-start(s32[192]{0:T(256)} %param.24) | copy-start | bytes 2308
  0.7 14.5 %copy-start.4 = (f32[1536]{0:T(1024)S(1)}, f32[1536]{0:T(1024)}, u32[]{:S(2)}) copy-start(f32[1536]{0:T(1024)} %param.28) | copy-start | bytes 18436
  0.7 14.5 %copy-start.5 = (s32[8192]{0:T(1024)S(1)}, s32[8192]{0:T(1024)}, u32[]{:S(2)}) copy-start(s32[8192]{0:T(1024)} %param.25) | copy-start | bytes 98308
  2.7 18.7 %all-to-all-start = ((bf16[8,4,8960]{2,1,0:T(4,128)(2,1)}), bf16[8,4,8960]{2,1,0:T(4,128)(2,1)S(1)}, u32[]{:S(2)}, u32[]{:S(2)}) async-start(bf16[8,4,8960]{2,1,0:T(4,128)(2,1)} %broadcast_in_dim.46), calls=%async_computation | async-start | bytes 1146880 | tf_op jit(solution)/shard_map/all_to_all | solution.py:29
  29.7 10.1 %all-to-all-start.1 = ((f32[4,8,6,256]{3,0,2,1:T(4,128)}), f32[4,8,6,256]{3,0,2,1:T(4,128)S(1)}, u32[]{:S(2)}, u32[]{:S(2)}) async-start(f32[4,8,6,256]{3,0,2,1:T(4,128)} %bitcast.15), calls=%async_computation.1 | async-start | bytes 393216 | tf_op jit(solution)/shard_map/all_to_all | solution.py:254
  42.5 8.5 %copy-start.3 = (f32[4,8192]{1,0:T(4,128)S(1)}, f32[4,8192]{1,0:T(4,128)}, u32[]{:S(2)}) copy-start(f32[4,8192]{1,0:T(4,128)} %param.20) | copy-start | bytes 393220
  49.4 16.7 %copy-start.9 = (f32[3,256]{1,0:T(4,128)S(1)}, f32[3,256]{1,0:T(4,128)}, u32[]{:S(2)}) copy-start(f32[3,256]{1,0:T(4,128)} %param.29) | copy-start | bytes 9220
  51.9 31.6 %all-to-all-start.2 = ((f32[4,64,128]{2,0,1:T(4,128)}), f32[4,64,128]{2,0,1:T(4,128)S(1)}, u32[]{:S(2)}, u32[]{:S(2)}) async-start(f32[4,64,128]{2,0,1:T(4,128)} %fusion.22), calls=%async_computation.2 | async-start | bytes 262144 | tf_op jit(solution)/shard_map/all_to_all | solution.py:266
  85.7 7.1 %copy-start.2 = (s32[8192]{0:T(1024)S(1)}, s32[8192]{0:T(1024)}, u32[]{:S(2)}) copy-start(s32[8192]{0:T(1024)} %get-tuple-element.63) | copy-start | bytes 98308
  88.1 21.4 %all-to-all-start.3 = ((f32[64,4,128]{2,1,0:T(4,128)}), f32[64,4,128]{2,1,0:T(4,128)S(1)}, u32[]{:S(2)}, u32[]{:S(2)}) async-start(f32[64,4,128]{2,1,0:T(4,128)} %bitcast.30), calls=%async_computation.3 | async-start | bytes 262144 | tf_op jit(solution)/shard_map/all_to_all | solution.py:296
  118.5 1.5 copy-start.1
  162.9 22.4 %all-to-all-start.6 = ((f32[4,64,128]{2,0,1:T(4,128)}), f32[4,64,128]{2,0,1:T(4,128)S(1)}, u32[]{:S(2)}, u32[]{:S(2)}) async-start(f32[4,64,128]{2,0,1:T(4,128)} %fusion.17), calls=%async_computation.6 | async-start | bytes 262144 | tf_op jit(solution)/shard_map/all_to_all | solution.py:266
  190.0 26.2 %all-to-all-start.7 = ((f32[64,5,128]{2,1,0:T(8,128)}), f32[64,5,128]{2,1,0:T(8,128)S(1)}, u32[]{:S(2)}, u32[]{:S(2)}) async-start(f32[64,5,128]{2,1,0:T(8,128)} %pad_maximum_fusion), calls=%async_computation.7 | async-start | bytes 524288 | tf_op jit(solution)/shard_map/all_to_all | solution.py:290

commit v3 on v2

--- a/solution.py
+++ b/solution.py
@@ -213,11 +213,16 @@
             injection = (demand + units_to_bus(power_time, lo_col, hi_row, col_blocks, panel_width)).astype(
                 jnp.bfloat16
             )
-        gathered = collect(injection, AREA, 1)
+        sending = jnp.take(injection.reshape(block_steps, col_blocks, panel_width), send_block, axis=1)
+        arrived = lax.all_to_all(
+            sending.reshape(block_steps, area_devices, capacity, panel_width),
+            AREA,
+            split_axis=1,
+            concat_axis=1,
+            tiled=True,
+        )
         panels = jnp.take(
-            gathered.reshape(block_steps, area_devices * col_blocks, panel_width),
-            my_columns,
-            axis=1,
+            arrived.reshape(block_steps, area_devices * capacity, panel_width), slot_of_tile, axis=1
         )
         partial_value = jnp.einsum(
             "tjb,jlb->tjl", panels, ptdf_tiles, preferred_element_type=jnp.float32

time: 219 us -> 213 us (0.973)
  waiting for transfers between devices: 78.2 us -> 72.7 us
  blocking collectives: 23 us -> 17.7 us
  other arithmetic: 19.5 us -> 22.4 us
    all_to_all x1, blocking collectives: 13.5 us -> 8.1 us  [per_device(): lax.all_to_all(sending.reshape(block_steps, area_devices, capacity, panel...]
    all_to_all x1, waiting for transfers between devices: 5.64 us -> 0.29 us  [per_device(): lax.all_to_all(sending.reshape(block_steps, area_devices, capacity, panel...]
where the time goes in v3:
time: 213 us; the launch traced here: 211 us
  waiting for transfers between devices  72.7 us (34%)
  starting transfers between devices  42.3 us (20%)
  other arithmetic  22.4 us (11%)
  local copies, waits for them, and re-layouts  22.3 us (10%)
  Pallas kernels  20.4 us (10%)
  blocking collectives  17.7 us (8%)
  matrix products  12.3 us (6%)
    all_to_all x2, waiting for transfers between devices, per_device(): lax.all_to_all(target, TM, split_axis=1, concat_axis=0, tiled=True)  32.3 us
    all_to_all x1, waiting for transfers between devices, per_device(): lax.all_to_all(jnp.concatenate([chunks, extra], axis=1), TM, split_axis=0...  20.9 us
    all_to_all x2, starting transfers between devices, per_device(): lax.all_to_all(target, TM, split_axis=1, concat_axis=0, tiled=True)  19 us
    all_to_all x1, waiting for transfers between devices, per_device(): lax.all_to_all(power_cols, TM, split_axis=0, concat_axis=1, tiled=True)  13.9 us
    pallas_call x2, Pallas kernels, bus_to_units(): pl.pallas_call(gather_kernel, grid=(units // UNIT_BLOCK,), in_specs=[pl.B...  12.4 us
    all_to_all x1, blocking collectives, per_device(): lax.all_to_all(outbound, AREA, split_axis=1, concat_axis=1, tiled=True)  9.55 us
    all_to_all x1, starting transfers between devices, per_device(): lax.all_to_all(sending.reshape(block_steps, area_devices, capacity, panel...  9.15 us
    all_to_all x1, blocking collectives, per_device(): lax.all_to_all(sending.reshape(block_steps, area_devices, capacity, panel...  8.1 us
  transfers between devices with their start and end apart: 6, of which 6 were waited for; matrix products, arithmetic and copies ran while one was open for 5% of the time, Pallas kernels for 0%

profile of v3, /device:TPU:2, one launch (start us, length us, event | category | flops | bytes accessed | tf_op | source)
XLA Modules:
  0.0 211.3 jit_solution(13962086750827749604)
XLA Ops:
  1.2 1.3 reduce.11
  6.3 9.2 %all-to-all-start = ((bf16[4,8,6,256]{3,0,2,1:T(4,128)(2,1)}), bf16[4,8,6,256]{3,0,2,1:T(4,128)(2,1)S(1)}, u32[]{:S(2)}, u32[]{:S(2)}) async-start(bf16[4,8,6,256]{3,0,2,1:T(4,128)(2,1)} %bitcast.10), calls=%async_computation | async-start | bytes 196608 | tf_op jit(solution)/shard_map/all_to_all | solution.py:217
  17.3 1.4 add_select_fusion.1
  21.0 1.7 scatter_fusion
  24.4 3.6 %scatter_fusion.1 = f32[4,48,256]{2,0,1:T(4,128)} fusion(f32[4,48,256]{2,0,1:T(4,128)} %broadcast.322.clone, s32[24]{0:T(128)S(1)} %get-tuple-element.67, f32[24,4,256]{2,1,0:T(4,128)S(1)} %fusion.49), kind=kCustom, calls=%fused_computation.7 | custom fusion | bytes 295008 | tf_op jit(solution)/shard_map/scatter | solution.py:248
  28.1 4.7 %all-to-all-start.1 = ((f32[4,8,6,256]{3,0,2,1:T(4,128)}), f32[4,8,6,256]{3,0,2,1:T(4,128)S(1)}, u32[]{:S(2)}, u32[]{:S(2)}) async-start(f32[4,8,6,256]{3,0,2,1:T(4,128)} %bitcast.16), calls=%async_computation.1 | async-start | bytes 393216 | tf_op jit(solution)/shard_map/all_to_all | solution.py:259
  32.8 5.4 %all-to-all-done.1 = f32[4,8,6,256]{3,0,2,1:T(4,128)S(1)} async-done(((f32[4,8,6,256]{3,0,2,1:T(4,128)}), f32[4,8,6,256]{3,0,2,1:T(4,128)S(1)}, u32[]{:S(2)}, u32[]{:S(2)}) %all-to-all-start.1) | async-done | bytes 196640 | tf_op jit(solution)/shard_map/all_to_all | solution.py:259
  38.2 2.4 %scatter_fusion.2 = f32[4,35,256]{2,0,1:T(4,128)S(1)} fusion(f32[4,35,256]{2,0,1:T(4,128)S(1)} %broadcast.317.clone, s32[48]{0:T(128)S(1)} %fusion.66, f32[48,4,256]{2,1,0:T(4,128)S(1)} %bitcast.177), kind=kCustom, calls=%fused_computation.8 | custom fusion | flops 49152 | bytes 590016 | tf_op jit(solution)/shard_map/scatter-add | solution.py:266
  41.7 6.2 %shard_map.130 = f32[16,8192]{1,0:T(8,128)} custom-call(bf16[560,256]{1,0:T(8,128)(2,1)} %bitcast.174, s32[1,8192]{1,0:T(1,128)} %bitcast.183, s32[1,8192]{1,0:T(1,128)} %bitcast.180), custom_call_target="tpu_custom_call" | custom-call | tf_op jit(solution)/shard_map/pallas_call | solution.py:74
  50.3 14.4 %all-to-all-start.2 = ((f32[4,64,128]{2,0,1:T(4,128)}), f32[4,64,128]{2,0,1:T(4,128)S(1)}, u32[]{:S(2)}, u32[]{:S(2)}) async-start(f32[4,64,128]{2,0,1:T(4,128)} %fusion.22), calls=%async_computation.2 | async-start | bytes 262144 | tf_op jit(solution)/shard_map/all_to_all | solution.py:271
  64.7 1.7 fusion.24
  67.5 14.6 %all-to-all-done.2 = f32[4,64,128]{2,0,1:T(4,128)S(1)} async-done(((f32[4,64,128]{2,0,1:T(4,128)}), f32[4,64,128]{2,0,1:T(4,128)S(1)}, u32[]{:S(2)}, u32[]{:S(2)}) %all-to-all-start.2) | async-done | bytes 131104 | tf_op jit(solution)/shard_map/all_to_all | solution.py:271
  82.1 2.2 %fusion.25 = f32[256,128]{1,0:T(8,128)S(1)} fusion(f32[256,128]{1,0:T(8,128)S(1)} %bitcast.191, s32[256]{0:T(256)S(1)} %get-tuple-element.35, pred[256]{0:T(512)(128)(4,1)S(1)} %iota_compare_fusion.4), kind=kOutput, calls=%fused_computation.67 | convolution fusion | flops 101711872 | bytes 263424 | tf_op jit(solution)/shard_map/dot_general | solution.py:272
  84.4 2.3 %fusion.1 = f32[256,128]{1,0:T(8,128)} fusion(f32[127,128]{1,0:T(8,128)S(1)} %fusion.34, f32[129,128]{1,0:T(8,128)S(1)} %get-tuple-element.56, s32[256]{0:T(256)S(1)} %get-tuple-element.35, pred[256]{0:T(512)(128)(4,1)S(1)} %iota_compare_fusion.4, f32[256]{0:T(256)S(1)} %get-tuple-element.34, f32[128]{0:T(128)S(1)} %get-tuple-element.32, ...), kind=kOutput, calls=%fused_computation.15 | convolution fusion | flops 101842944 | bytes 265472 | tf_op jit(solution)/shard_map/dot_general | solution.py:280
  86.7 4.8 %all-to-all-start.3 = ((f32[64,4,128]{2,1,0:T(4,128)}), f32[64,4,128]{2,1,0:T(4,128)S(1)}, u32[]{:S(2)}, u32[]{:S(2)}) async-start(f32[64,4,128]{2,1,0:T(4,128)} %bitcast.31), calls=%async_computation.3 | async-start | bytes 262144 | tf_op jit(solution)/shard_map/all_to_all | solution.py:301
  91.6 2.6 %copy.66.lo_ref = s32[8192,1]{1,0:T(8,128)} copy(s32[8192,1]{0,1:T(1,128)S(1)} %bitcast.185) | data formatting | bytes 65536 | tf_op jit(solution)/shard_map/reshape;reshape | solution.py:205
  94.3 13.9 %all-to-all-done.3 = f32[64,4,128]{2,1,0:T(4,128)S(1)} async-done(((f32[64,4,128]{2,1,0:T(4,128)}), f32[64,4,128]{2,1,0:T(4,128)S(1)}, u32[]{:S(2)}, u32[]{:S(2)}) %all-to-all-start.3) | async-done | bytes 131104 | tf_op jit(solution)/shard_map/all_to_all | solution.py:301
  109.1 8.1 %shard_map.131 = f32[560,256]{1,0:T(8,128)} custom-call(bf16[16,8192]{1,0:T(8,128)(2,1)} %maximum_maximum_fusion.parts_ref, s32[8192,1]{1,0:T(8,128)} %copy.66.lo_ref, s32[1,8192]{1,0:T(1,128)} %bitcast.181), custom_call_target="tpu_custom_call" | custom-call | tf_op jit(solution)/shard_map/pallas_call | solution.py:110
  117.1 1.3 copy.79
  119.4 8.1 %all_to_all.83 = bf16[4,8,6,256]{3,0,2,1:T(4,128)(2,1)S(1)} all-to-all(bf16[4,8,6,256]{3,0,2,1:T(4,128)(2,1)S(1)} %bitcast.188), channel_id=1, replica_groups=mesh['tm_0'=16,'tm_1'=4,'area_0'=4,'area_1'=2] {'area_0','area_1'}, dimensions={1} | all-to-all | bytes 196608 | tf_op jit(solution)/shard_map/all_to_all | solution.py:217
  128.7 1.7 scatter_fusion.3
  132.0 1.5 scatter_fusion.4
  133.6 1.4 maximum_bitcast_fusion
  135.0 9.6 %all_to_all.82 = f32[4,8,7,256]{3,0,2,1:T(4,128)S(1)} all-to-all(f32[4,8,7,256]{3,0,2,1:T(4,128)S(1)} %pad_maximum_fusion.1), channel_id=1, replica_groups=mesh['tm_0'=16,'tm_1'=4,'area_0'=4,'area_1'=2] {'area_0','area_1'}, dimensions={1} | all-to-all | bytes 458752 | tf_op jit(solution)/shard_map/all_to_all | solution.py:259
  144.6 2.4 %scatter_fusion.5 = f32[4,35,256]{2,0,1:T(4,128)S(1)} fusion(f32[4,35,256]{2,0,1:T(4,128)S(1)} %broadcast.317, s32[48]{0:T(128)S(1)} %fusion.66, f32[48,4,256]{2,1,0:T(4,128)S(1)} %bitcast.178), kind=kCustom, calls=%fused_computation.11 | custom fusion | flops 49152 | bytes 590016 | tf_op jit(solution)/shard_map/scatter-add | solution.py:266
  148.1 6.2 %shard_map.132 = f32[16,8192]{1,0:T(8,128)} custom-call(bf16[560,256]{1,0:T(8,128)(2,1)} %bitcast.173, s32[1,8192]{1,0:T(1,128)} %bitcast.184, s32[1,8192]{1,0:T(1,128)} %bitcast.182), custom_call_target="tpu_custom_call" | custom-call | tf_op jit(solution)/shard_map/pallas_call | solution.py:74
  156.7 4.6 %all-to-all-start.6 = ((f32[4,64,128]{2,0,1:T(4,128)}), f32[4,64,128]{2,0,1:T(4,128)S(1)}, u32[]{:S(2)}, u32[]{:S(2)}) async-start(f32[4,64,128]{2,0,1:T(4,128)} %fusion.17), calls=%async_computation.6 | async-start | bytes 262144 | tf_op jit(solution)/shard_map/all_to_all | solution.py:271
  161.4 17.7 %all-to-all-done.6 = f32[4,64,128]{2,0,1:T(4,128)S(1)} async-done(((f32[4,64,128]{2,0,1:T(4,128)}), f32[4,64,128]{2,0,1:T(4,128)S(1)}, u32[]{:S(2)}, u32[]{:S(2)}) %all-to-all-start.6) | async-done | bytes 131104 | tf_op jit(solution)/shard_map/all_to_all | solution.py:271
  179.1 2.2 %fusion.23 = f32[256,128]{1,0:T(8,128)S(1)} fusion(f32[256,128]{1,0:T(8,128)S(1)} %bitcast.192, s32[256]{0:T(256)S(1)} %get-tuple-element.35, pred[256]{0:T(512)(128)(4,1)S(1)} %iota_compare_fusion.4), kind=kOutput, calls=%fused_computation.65 | convolution fusion | flops 101711872 | bytes 263424 | tf_op jit(solution)/shard_map/dot_general | solution.py:272
  181.4 1.7 fusion
  183.9 4.6 %all-to-all-start.7 = ((f32[64,5,128]{2,1,0:T(8,128)}), f32[64,5,128]{2,1,0:T(8,128)S(1)}, u32[]{:S(2)}, u32[]{:S(2)}) async-start(f32[64,5,128]{2,1,0:T(8,128)} %pad_maximum_fusion), calls=%async_computation.7 | async-start | bytes 524288 | tf_op jit(solution)/shard_map/all_to_all | solution.py:295
  189.1 20.9 %all-to-all-done.7 = f32[64,5,128]{2,1,0:T(8,128)S(1)} async-done(((f32[64,5,128]{2,1,0:T(8,128)}), f32[64,5,128]{2,1,0:T(8,128)S(1)}, u32[]{:S(2)}, u32[]{:S(2)}) %all-to-all-start.7) | async-done | bytes 163872 | tf_op jit(solution)/shard_map/all_to_all | solution.py:295
  (108 shorter events, 25.8 us)
Async XLA Ops:
  0.6 19.8 %copy-start = (bf16[24,128,256]{2,1,0:T(8,128)(2,1)S(1)}, bf16[24,128,256]{2,1,0:T(8,128)(2,1)}, u32[]{:S(2)}) copy-start(bf16[24,128,256]{2,1,0:T(8,128)(2,1)} %param.23) | copy-start | bytes 4718596
  0.6 22.1 %copy-start.4 = (f32[1536]{0:T(1024)S(1)}, f32[1536]{0:T(1024)}, u32[]{:S(2)}) copy-start(f32[1536]{0:T(1024)} %param.30) | copy-start | bytes 18436
  6.3 13.5 %all-to-all-start = ((bf16[4,8,6,256]{3,0,2,1:T(4,128)(2,1)}), bf16[4,8,6,256]{3,0,2,1:T(4,128)(2,1)S(1)}, u32[]{:S(2)}, u32[]{:S(2)}) async-start(bf16[4,8,6,256]{3,0,2,1:T(4,128)(2,1)} %bitcast.10), calls=%async_computation | async-start | bytes 196608 | tf_op jit(solution)/shard_map/all_to_all | solution.py:217
  28.1 10.1 %all-to-all-start.1 = ((f32[4,8,6,256]{3,0,2,1:T(4,128)}), f32[4,8,6,256]{3,0,2,1:T(4,128)S(1)}, u32[]{:S(2)}, u32[]{:S(2)}) async-start(f32[4,8,6,256]{3,0,2,1:T(4,128)} %bitcast.16), calls=%async_computation.1 | async-start | bytes 393216 | tf_op jit(solution)/shard_map/all_to_all | solution.py:259
  40.9 8.5 %copy-start.3 = (f32[4,8192]{1,0:T(4,128)S(1)}, f32[4,8192]{1,0:T(4,128)}, u32[]{:S(2)}) copy-start(f32[4,8192]{1,0:T(4,128)} %param.22) | copy-start | bytes 393220
  47.8 16.9 %copy-start.5 = (f32[3,256]{1,0:T(4,128)S(1)}, f32[3,256]{1,0:T(4,128)}, u32[]{:S(2)}) copy-start(f32[3,256]{1,0:T(4,128)} %param.31) | copy-start | bytes 9220
  50.3 31.8 %all-to-all-start.2 = ((f32[4,64,128]{2,0,1:T(4,128)}), f32[4,64,128]{2,0,1:T(4,128)S(1)}, u32[]{:S(2)}, u32[]{:S(2)}) async-start(f32[4,64,128]{2,0,1:T(4,128)} %fusion.22), calls=%async_computation.2 | async-start | bytes 262144 | tf_op jit(solution)/shard_map/all_to_all | solution.py:271
  84.3 7.3 %copy-start.2 = (s32[8192]{0:T(1024)S(1)}, s32[8192]{0:T(1024)}, u32[]{:S(2)}) copy-start(s32[8192]{0:T(1024)} %get-tuple-element.64) | copy-start | bytes 98308
  86.7 21.4 %all-to-all-start.3 = ((f32[64,4,128]{2,1,0:T(4,128)}), f32[64,4,128]{2,1,0:T(4,128)S(1)}, u32[]{:S(2)}, u32[]{:S(2)}) async-start(f32[64,4,128]{2,1,0:T(4,128)} %bitcast.31), calls=%async_computation.3 | async-start | bytes 262144 | tf_op jit(solution)/shard_map/all_to_all | solution.py:301
  117.1 1.5 copy-start.1
  156.7 22.4 %all-to-all-start.6 = ((f32[4,64,128]{2,0,1:T(4,128)}), f32[4,64,128]{2,0,1:T(4,128)S(1)}, u32[]{:S(2)}, u32[]{:S(2)}) async-start(f32[4,64,128]{2,0,1:T(4,128)} %fusion.17), calls=%async_computation.6 | async-start | bytes 262144 | tf_op jit(solution)/shard_map/all_to_all | solution.py:271
  183.9 26.2 %all-to-all-start.7 = ((f32[64,5,128]{2,1,0:T(8,128)}), f32[64,5,128]{2,1,0:T(8,128)S(1)}, u32[]{:S(2)}, u32[]{:S(2)}) async-start(f32[64,5,128]{2,1,0:T(8,128)} %pad_maximum_fusion), calls=%async_computation.7 | async-start | bytes 524288 | tf_op jit(solution)/shard_map/all_to_all | solution.py:295

commit v4 on v3

--- a/solution.py
+++ b/solution.py
@@ -200,6 +200,11 @@
     empty_row = jnp.zeros((1, unit_width), jnp.float32)
     kernel_real = unit_spectrum[: half_steps + 1]
     kernel_imag = jnp.concatenate([empty_row, unit_spectrum[half_steps + 1 :], empty_row], axis=0)
+    row_table = (my_rows[:, None] == jnp.arange(row_blocks, dtype=jnp.int32)[None, :]).astype(jnp.float32)
+    slot_table = (
+        slot_of_tile[:, None] == jnp.arange(area_devices * capacity, dtype=jnp.int32)[None, :]
+    ).astype(jnp.float32)
+    block_table = (send_block[:, None] == jnp.arange(col_blocks, dtype=jnp.int32)[None, :]).astype(jnp.float32)
     lo_row = (unit_bus % panel_width).reshape(1, unit_area)
     hi_row = (unit_bus // panel_width).reshape(1, unit_area)
     lo_col = lo_row.reshape(unit_area, 1)
@@ -227,10 +232,9 @@
         partial_value = jnp.einsum(
             "tjb,jlb->tjl", panels, ptdf_tiles, preferred_element_type=jnp.float32
         )
-        line_flows = (
-            jnp.zeros((block_steps, row_blocks, line_block), jnp.float32)
-            .at[:, my_rows]
-            .add(partial_value)
+        line_flows = jnp.einsum(
+            "tjl,jr->trl", partial_value, row_table, precision=lax.Precision.HIGHEST,
+            preferred_element_type=jnp.float32,
         )
         line_flows = line_flows.reshape(block_steps, row_blocks * line_block)
         limits = line_limit[None, :]
@@ -242,10 +246,9 @@
         weights = (line_duals + line_flows - clipped).astype(jnp.bfloat16)
         picked = jnp.take(weights.reshape(block_steps, row_blocks, line_block), my_rows, axis=1)
         contrib = jnp.einsum("tjl,jlb->tjb", picked, ptdf_tiles, preferred_element_type=jnp.float32)
-        outbound = (
-            jnp.zeros((block_steps, area_devices * capacity, panel_width), jnp.float32)
-            .at[:, slot_of_tile]
-            .set(contrib)
+        outbound = jnp.einsum(
+            "tjb,js->tsb", contrib, slot_table, precision=lax.Precision.HIGHEST,
+            preferred_element_type=jnp.float32,
         )
         outbound = outbound.reshape(block_steps, area_devices, capacity, panel_width)
         last = repeat == ITERATIONS - 1
@@ -260,10 +263,12 @@
         if last:
             area_totals = jnp.sum(returned[0, :, capacity, :ITERATIONS], axis=0)
             returned = returned[:, :, :capacity]
-        prices = (
-            jnp.zeros((block_steps, col_blocks, panel_width), jnp.float32)
-            .at[:, send_block]
-            .add(returned.reshape(block_steps, area_devices * capacity, panel_width))
+        prices = jnp.einsum(
+            "tsb,sc->tcb",
+            returned.reshape(block_steps, area_devices * capacity, panel_width),
+            block_table,
+            precision=lax.Precision.HIGHEST,
+            preferred_element_type=jnp.float32,
         )
         prices = prices.reshape(block_steps, bus_area)
         gradient = unit_cost + rho_weight * bus_to_units(prices, lo_row, hi_row)

time: 213 us -> 201 us (0.944)
  other arithmetic: 22.4 us -> 12.5 us
  local copies, waits for them, and re-layouts: 22.3 us -> 17.3 us
    scatter-add x4 -> x0, other arithmetic: 8.17 us -> none  [the longest x2 4.71 us: per_device(): prices = jnp.zeros((block_steps, col_blocks, panel_width), jnp.float32).a...]
    scatter x2 -> x0, local copies, waits for them, and re-layouts: 5.17 us -> none  [per_device(): outbound = jnp.zeros((block_steps, area_devices * capacity, panel_width),...]
    dot_general x0 -> x6, matrix products: none -> 2.14 us  [the longest x2 0.94 us: per_device(): jnp.einsum('tjl,jr->trl', partial_value, row_table, precision=lax.Precisi...]
where the time goes in v4:
time: 201 us; the launch traced here: 199 us
  waiting for transfers between devices  73.7 us (37%)
  starting transfers between devices  42.1 us (21%)
  Pallas kernels  20.4 us (10%)
  blocking collectives  17.9 us (9%)
  local copies, waits for them, and re-layouts  17.3 us (9%)
  matrix products  14.4 us (7%)
  other arithmetic  12.5 us (6%)
    all_to_all x2, waiting for transfers between devices, per_device(): lax.all_to_all(target, TM, split_axis=1, concat_axis=0, tiled=True)  32.3 us
    all_to_all x1, waiting for transfers between devices, per_device(): lax.all_to_all(jnp.concatenate([chunks, extra], axis=1), TM, split_axis=0...  20.9 us
    all_to_all x2, starting transfers between devices, per_device(): lax.all_to_all(target, TM, split_axis=1, concat_axis=0, tiled=True)  19 us
    all_to_all x1, waiting for transfers between devices, per_device(): lax.all_to_all(power_cols, TM, split_axis=0, concat_axis=1, tiled=True)  14 us
    pallas_call x2, Pallas kernels, bus_to_units(): pl.pallas_call(gather_kernel, grid=(units // UNIT_BLOCK,), in_specs=[pl.B...  12.3 us
    all_to_all x1, blocking collectives, per_device(): lax.all_to_all(outbound, AREA, split_axis=1, concat_axis=1, tiled=True)  9.74 us
    all_to_all x1, starting transfers between devices, per_device(): lax.all_to_all(sending.reshape(block_steps, area_devices, capacity, panel...  9.15 us
    all_to_all x1, blocking collectives, per_device(): lax.all_to_all(sending.reshape(block_steps, area_devices, capacity, panel...  8.17 us
  transfers between devices with their start and end apart: 6, of which 6 were waited for; matrix products, arithmetic and copies ran while one was open for 5% of the time, Pallas kernels for 0%

profile of v4, /device:TPU:2, one launch (start us, length us, event | category | flops | bytes accessed | tf_op | source)
XLA Modules:
  0.0 199.4 jit_solution(16211277905967586662)
XLA Ops:
  1.2 1.3 reduce.11
  3.9 0.9 convert_element_type.87
  6.3 9.2 %all-to-all-start = ((bf16[4,8,6,256]{3,0,2,1:T(4,128)(2,1)}), bf16[4,8,6,256]{3,0,2,1:T(4,128)(2,1)S(1)}, u32[]{:S(2)}, u32[]{:S(2)}) async-start(bf16[4,8,6,256]{3,0,2,1:T(4,128)(2,1)} %bitcast.7), calls=%async_computation | async-start | bytes 196608 | tf_op jit(solution)/shard_map/all_to_all | solution.py:222
  18.0 1.8 all-to-all-done
  23.3 4.7 %all-to-all-start.1 = ((f32[4,8,6,256]{3,0,2,1:T(4,128)}), f32[4,8,6,256]{3,0,2,1:T(4,128)S(1)}, u32[]{:S(2)}, u32[]{:S(2)}) async-start(f32[4,8,6,256]{3,0,2,1:T(4,128)} %bitcast.17), calls=%async_computation.1 | async-start | bytes 393216 | tf_op jit(solution)/shard_map/all_to_all | solution.py:262
  28.7 4.7 %all-to-all-done.1 = f32[4,8,6,256]{3,0,2,1:T(4,128)S(1)} async-done(((f32[4,8,6,256]{3,0,2,1:T(4,128)}), f32[4,8,6,256]{3,0,2,1:T(4,128)S(1)}, u32[]{:S(2)}, u32[]{:S(2)}) %all-to-all-start.1) | async-done | bytes 196640 | tf_op jit(solution)/shard_map/all_to_all | solution.py:262
  34.5 6.2 %shard_map.130 = f32[16,8192]{1,0:T(8,128)} custom-call(bf16[560,256]{1,0:T(8,128)(2,1)} %bitcast.239, s32[1,8192]{1,0:T(1,128)} %bitcast.249, s32[1,8192]{1,0:T(1,128)} %bitcast.246), custom_call_target="tpu_custom_call" | custom-call | tf_op jit(solution)/shard_map/pallas_call | solution.py:74
  40.7 1.2 reshape.327
  42.3 0.9 fusion.24
  43.2 14.4 %all-to-all-start.2 = ((f32[4,64,128]{2,0,1:T(4,128)}), f32[4,64,128]{2,0,1:T(4,128)S(1)}, u32[]{:S(2)}, u32[]{:S(2)}) async-start(f32[4,64,128]{2,0,1:T(4,128)} %fusion.24), calls=%async_computation.2 | async-start | bytes 262144 | tf_op jit(solution)/shard_map/all_to_all | solution.py:276
  57.6 1.7 fusion.26
  60.4 14.6 %all-to-all-done.2 = f32[4,64,128]{2,0,1:T(4,128)S(1)} async-done(((f32[4,64,128]{2,0,1:T(4,128)}), f32[4,64,128]{2,0,1:T(4,128)S(1)}, u32[]{:S(2)}, u32[]{:S(2)}) %all-to-all-start.2) | async-done | bytes 131104 | tf_op jit(solution)/shard_map/all_to_all | solution.py:276
  75.0 2.2 %fusion.27 = f32[256,128]{1,0:T(8,128)S(1)} fusion(f32[256,128]{1,0:T(8,128)S(1)} %bitcast.260, s32[256]{0:T(256)S(1)} %get-tuple-element.35, pred[256]{0:T(512)(128)(4,1)S(1)} %iota_compare_fusion.7), kind=kOutput, calls=%fused_computation.71 | convolution fusion | flops 101711872 | bytes 263424 | tf_op jit(solution)/shard_map/dot_general | solution.py:277
  77.3 2.3 %fusion.1 = f32[256,128]{1,0:T(8,128)} fusion(f32[127,128]{1,0:T(8,128)S(1)} %fusion.38, f32[129,128]{1,0:T(8,128)S(1)} %get-tuple-element.56, s32[256]{0:T(256)S(1)} %get-tuple-element.35, pred[256]{0:T(512)(128)(4,1)S(1)} %iota_compare_fusion.7, f32[256]{0:T(256)S(1)} %get-tuple-element.34, f32[128]{0:T(128)S(1)} %get-tuple-element.32, ...), kind=kOutput, calls=%fused_computation.13 | convolution fusion | flops 101842944 | bytes 265472 | tf_op jit(solution)/shard_map/dot_general | solution.py:285
  79.6 4.6 %all-to-all-start.3 = ((f32[64,4,128]{2,1,0:T(4,128)}), f32[64,4,128]{2,1,0:T(4,128)S(1)}, u32[]{:S(2)}, u32[]{:S(2)}) async-start(f32[64,4,128]{2,1,0:T(4,128)} %bitcast.32), calls=%async_computation.3 | async-start | bytes 262144 | tf_op jit(solution)/shard_map/all_to_all | solution.py:306
  84.3 2.6 %copy.86.lo_ref = s32[8192,1]{1,0:T(8,128)} copy(s32[8192,1]{0,1:T(1,128)S(1)} %bitcast.251) | data formatting | bytes 65536 | tf_op jit(solution)/shard_map/reshape;reshape | solution.py:210
  87.0 14.0 %all-to-all-done.3 = f32[64,4,128]{2,1,0:T(4,128)S(1)} async-done(((f32[64,4,128]{2,1,0:T(4,128)}), f32[64,4,128]{2,1,0:T(4,128)S(1)}, u32[]{:S(2)}, u32[]{:S(2)}) %all-to-all-start.3) | async-done | bytes 131104 | tf_op jit(solution)/shard_map/all_to_all | solution.py:306
  101.1 0.9 maximum_maximum_fusion.parts_ref
  102.0 8.1 %shard_map.131 = f32[560,256]{1,0:T(8,128)} custom-call(bf16[16,8192]{1,0:T(8,128)(2,1)} %maximum_maximum_fusion.parts_ref, s32[8192,1]{1,0:T(8,128)} %copy.86.lo_ref, s32[1,8192]{1,0:T(1,128)} %bitcast.247), custom_call_target="tpu_custom_call" | custom-call | tf_op jit(solution)/shard_map/pallas_call | solution.py:110
  110.1 1.3 copy.104
  112.4 8.2 %all_to_all.82 = bf16[4,8,6,256]{3,0,2,1:T(4,128)(2,1)S(1)} all-to-all(bf16[4,8,6,256]{3,0,2,1:T(4,128)(2,1)S(1)} %bitcast.254), channel_id=1, replica_groups=mesh['tm_0'=16,'tm_1'=4,'area_0'=4,'area_1'=2] {'area_0','area_1'}, dimensions={1} | all-to-all | bytes 196608 | tf_op jit(solution)/shard_map/all_to_all | solution.py:222
  122.5 1.4 maximum_bitcast_fusion
  125.4 9.7 %all_to_all.83 = f32[4,8,7,256]{3,0,2,1:T(4,128)S(1)} all-to-all(f32[4,8,7,256]{3,0,2,1:T(4,128)S(1)} %pad_maximum_fusion.3), channel_id=1, replica_groups=mesh['tm_0'=16,'tm_1'=4,'area_0'=4,'area_1'=2] {'area_0','area_1'}, dimensions={1} | all-to-all | bytes 458752 | tf_op jit(solution)/shard_map/all_to_all | solution.py:262
  136.2 6.2 %shard_map.132 = f32[16,8192]{1,0:T(8,128)} custom-call(bf16[560,256]{1,0:T(8,128)(2,1)} %bitcast.238, s32[1,8192]{1,0:T(1,128)} %bitcast.250, s32[1,8192]{1,0:T(1,128)} %bitcast.248), custom_call_target="tpu_custom_call" | custom-call | tf_op jit(solution)/shard_map/pallas_call | solution.py:74
  142.4 1.2 reshape.339
  143.9 0.9 fusion.19
  144.9 4.6 %all-to-all-start.6 = ((f32[4,64,128]{2,0,1:T(4,128)}), f32[4,64,128]{2,0,1:T(4,128)S(1)}, u32[]{:S(2)}, u32[]{:S(2)}) async-start(f32[4,64,128]{2,0,1:T(4,128)} %fusion.19), calls=%async_computation.6 | async-start | bytes 262144 | tf_op jit(solution)/shard_map/all_to_all | solution.py:276
  149.5 17.7 %all-to-all-done.6 = f32[4,64,128]{2,0,1:T(4,128)S(1)} async-done(((f32[4,64,128]{2,0,1:T(4,128)}), f32[4,64,128]{2,0,1:T(4,128)S(1)}, u32[]{:S(2)}, u32[]{:S(2)}) %all-to-all-start.6) | async-done | bytes 131104 | tf_op jit(solution)/shard_map/all_to_all | solution.py:276
  167.2 2.2 %fusion.25 = f32[256,128]{1,0:T(8,128)S(1)} fusion(f32[256,128]{1,0:T(8,128)S(1)} %bitcast.261, s32[256]{0:T(256)S(1)} %get-tuple-element.35, pred[256]{0:T(512)(128)(4,1)S(1)} %iota_compare_fusion.7), kind=kOutput, calls=%fused_computation.69 | convolution fusion | flops 101711872 | bytes 263424 | tf_op jit(solution)/shard_map/dot_general | solution.py:277
  169.5 1.7 fusion
  172.0 4.6 %all-to-all-start.7 = ((f32[64,5,128]{2,1,0:T(8,128)}), f32[64,5,128]{2,1,0:T(8,128)S(1)}, u32[]{:S(2)}, u32[]{:S(2)}) async-start(f32[64,5,128]{2,1,0:T(8,128)} %pad_maximum_fusion), calls=%async_computation.7 | async-start | bytes 524288 | tf_op jit(solution)/shard_map/all_to_all | solution.py:300
  177.2 20.9 %all-to-all-done.7 = f32[64,5,128]{2,1,0:T(8,128)S(1)} async-done(((f32[64,5,128]{2,1,0:T(8,128)}), f32[64,5,128]{2,1,0:T(8,128)S(1)}, u32[]{:S(2)}, u32[]{:S(2)}) %all-to-all-start.7) | async-done | bytes 163872 | tf_op jit(solution)/shard_map/all_to_all | solution.py:300
  (102 shorter events, 21.2 us)
Async XLA Ops:
  0.6 19.8 %copy-start = (bf16[24,128,256]{2,1,0:T(8,128)(2,1)S(1)}, bf16[24,128,256]{2,1,0:T(8,128)(2,1)}, u32[]{:S(2)}) copy-start(bf16[24,128,256]{2,1,0:T(8,128)(2,1)} %param.23) | copy-start | bytes 4718596
  0.6 20.3 %copy-start.4 = (f32[1536]{0:T(1024)S(1)}, f32[1536]{0:T(1024)}, u32[]{:S(2)}) copy-start(f32[1536]{0:T(1024)} %param.30) | copy-start | bytes 18436
  6.3 13.5 %all-to-all-start = ((bf16[4,8,6,256]{3,0,2,1:T(4,128)(2,1)}), bf16[4,8,6,256]{3,0,2,1:T(4,128)(2,1)S(1)}, u32[]{:S(2)}, u32[]{:S(2)}) async-start(bf16[4,8,6,256]{3,0,2,1:T(4,128)(2,1)} %bitcast.7), calls=%async_computation | async-start | bytes 196608 | tf_op jit(solution)/shard_map/all_to_all | solution.py:222
  21.0 7.1 %copy-start.5 = (s32[8192]{0:T(1024)S(1)}, s32[8192]{0:T(1024)}, u32[]{:S(2)}) copy-start(s32[8192]{0:T(1024)} %param.27) | copy-start | bytes 98308
  23.3 10.1 %all-to-all-start.1 = ((f32[4,8,6,256]{3,0,2,1:T(4,128)}), f32[4,8,6,256]{3,0,2,1:T(4,128)S(1)}, u32[]{:S(2)}, u32[]{:S(2)}) async-start(f32[4,8,6,256]{3,0,2,1:T(4,128)} %bitcast.17), calls=%async_computation.1 | async-start | bytes 393216 | tf_op jit(solution)/shard_map/all_to_all | solution.py:262
  33.8 8.5 %copy-start.3 = (f32[4,8192]{1,0:T(4,128)S(1)}, f32[4,8192]{1,0:T(4,128)}, u32[]{:S(2)}) copy-start(f32[4,8192]{1,0:T(4,128)} %param.22) | copy-start | bytes 393220
  40.7 16.9 %copy-start.6 = (f32[3,256]{1,0:T(4,128)S(1)}, f32[3,256]{1,0:T(4,128)}, u32[]{:S(2)}) copy-start(f32[3,256]{1,0:T(4,128)} %param.31) | copy-start | bytes 9220
  43.2 31.8 %all-to-all-start.2 = ((f32[4,64,128]{2,0,1:T(4,128)}), f32[4,64,128]{2,0,1:T(4,128)S(1)}, u32[]{:S(2)}, u32[]{:S(2)}) async-start(f32[4,64,128]{2,0,1:T(4,128)} %fusion.24), calls=%async_computation.2 | async-start | bytes 262144 | tf_op jit(solution)/shard_map/all_to_all | solution.py:276
  77.2 7.1 %copy-start.2 = (s32[8192]{0:T(1024)S(1)}, s32[8192]{0:T(1024)}, u32[]{:S(2)}) copy-start(s32[8192]{0:T(1024)} %get-tuple-element.64) | copy-start | bytes 98308
  79.6 21.4 %all-to-all-start.3 = ((f32[64,4,128]{2,1,0:T(4,128)}), f32[64,4,128]{2,1,0:T(4,128)S(1)}, u32[]{:S(2)}, u32[]{:S(2)}) async-start(f32[64,4,128]{2,1,0:T(4,128)} %bitcast.32), calls=%async_computation.3 | async-start | bytes 262144 | tf_op jit(solution)/shard_map/all_to_all | solution.py:306
  110.1 1.5 copy-start.1
  144.9 22.4 %all-to-all-start.6 = ((f32[4,64,128]{2,0,1:T(4,128)}), f32[4,64,128]{2,0,1:T(4,128)S(1)}, u32[]{:S(2)}, u32[]{:S(2)}) async-start(f32[4,64,128]{2,0,1:T(4,128)} %fusion.19), calls=%async_computation.6 | async-start | bytes 262144 | tf_op jit(solution)/shard_map/all_to_all | solution.py:276
  172.0 26.2 %all-to-all-start.7 = ((f32[64,5,128]{2,1,0:T(8,128)}), f32[64,5,128]{2,1,0:T(8,128)S(1)}, u32[]{:S(2)}, u32[]{:S(2)}) async-start(f32[64,5,128]{2,1,0:T(8,128)} %pad_maximum_fusion), calls=%async_computation.7 | async-start | bytes 524288 | tf_op jit(solution)/shard_map/all_to_all | solution.py:300

commit v5 on v4

--- a/solution.py
+++ b/solution.py
@@ -35,7 +35,7 @@
     return laid_out(copy_for_each(array, axis), dim)
 
 
-PARTS = 3
+PARTS = 2
 ROWS = 16
 UNIT_BLOCK = 1024
 
@@ -50,6 +50,11 @@
     return pieces
 
 
+def group_targets(group):
+    half = (lax.broadcasted_iota(jnp.int32, (ROWS, 1), 0) >= ROWS // 2).astype(jnp.int32)
+    return 2 * group + half
+
+
 def gather_kernel(table_ref, lo_ref, hi_ref, out_ref):
     lanes = table_ref.shape[1]
     width = lo_ref.shape[1]
@@ -57,8 +62,9 @@
     picked = jnp.dot(table_ref[...], onehot, preferred_element_type=jnp.float32)
     hi = hi_ref[...]
     total = jnp.zeros((ROWS, width), jnp.float32)
-    for block in range(table_ref.shape[0] // ROWS):
-        total = total + jnp.where(hi == block, picked[block * ROWS : (block + 1) * ROWS], 0.0)
+    for group in range(table_ref.shape[0] // ROWS):
+        block = picked[group * ROWS : (group + 1) * ROWS]
+        total = total + jnp.where(hi == group_targets(group), block, 0.0)
     out_ref[...] = total
 
 
@@ -66,24 +72,24 @@
     steps, buses = prices.shape
     panel = 256
     blocks = buses // panel
+    groups = (blocks + 1) // 2
     units = lo_row.shape[1]
-    pieces = split_parts(prices.reshape(steps, blocks, panel))
-    stacked = jnp.stack(pieces, axis=1).reshape(steps * PARTS, blocks, panel)
-    stacked = jnp.pad(stacked, ((0, ROWS - steps * PARTS), (0, 0), (0, 0)))
-    table = jnp.transpose(stacked, (1, 0, 2)).reshape(blocks * ROWS, panel)
+    pieces = jnp.stack(split_parts(prices.reshape(steps, blocks, panel)), axis=0)
+    pieces = jnp.pad(pieces, ((0, 0), (0, 0), (0, 2 * groups - blocks), (0, 0)))
+    pieces = pieces.reshape(PARTS, steps, groups, 2, panel)
+    table = jnp.transpose(pieces, (2, 3, 0, 1, 4)).reshape(groups * ROWS, panel)
     picked = pl.pallas_call(
         gather_kernel,
         grid=(units // UNIT_BLOCK,),
         in_specs=[
-            pl.BlockSpec((blocks * ROWS, panel), lambda i: (0, 0)),
+            pl.BlockSpec((groups * ROWS, panel), lambda i: (0, 0)),
             pl.BlockSpec((1, UNIT_BLOCK), lambda i: (0, i)),
             pl.BlockSpec((1, UNIT_BLOCK), lambda i: (0, i)),
         ],
         out_specs=pl.BlockSpec((ROWS, UNIT_BLOCK), lambda i: (0, i)),
         out_shape=jax.ShapeDtypeStruct((ROWS, units), jnp.float32),
     )(table, lo_row, hi_row)
-    parts = picked[: steps * PARTS].reshape(steps, PARTS, units)
-    return parts[:, 0] + parts[:, 1] + parts[:, 2]
+    return jnp.sum(picked.reshape(ROWS // steps, steps, units), axis=0)
 
 
 def scatter_kernel(parts_ref, lo_ref, hi_ref, out_ref):
@@ -97,7 +103,10 @@
     parts = parts_ref[...]
     hi = hi_ref[...]
     masked = jnp.concatenate(
-        [jnp.where(hi == block, parts, jnp.zeros_like(parts)) for block in range(out_ref.shape[0] // ROWS)],
+        [
+            jnp.where(hi == group_targets(group), parts, jnp.zeros_like(parts))
+            for group in range(out_ref.shape[0] // ROWS)
+        ],
         axis=0,
     )
     out_ref[...] += jnp.dot(masked, onehot, preferred_element_type=jnp.float32)
@@ -105,8 +114,9 @@
 
 def units_to_bus(power, lo_col, hi_row, blocks, panel):
     steps, units = power.shape
+    groups = (blocks + 1) // 2
     pieces = split_parts(power)
-    parts = jnp.concatenate(pieces + [jnp.zeros((ROWS - steps * PARTS, units), jnp.bfloat16)], axis=0)
+    parts = jnp.concatenate(pieces + pieces, axis=0)
     summed = pl.pallas_call(
         scatter_kernel,
         grid=(units // UNIT_BLOCK,),
@@ -115,12 +125,12 @@
             pl.BlockSpec((UNIT_BLOCK, 1), lambda i: (i, 0)),
             pl.BlockSpec((1, UNIT_BLOCK), lambda i: (0, i)),
         ],
-        out_specs=pl.BlockSpec((blocks * ROWS, panel), lambda i: (0, 0)),
-        out_shape=jax.ShapeDtypeStruct((blocks * ROWS, panel), jnp.float32),
+        out_specs=pl.BlockSpec((groups * ROWS, panel), lambda i: (0, 0)),
+        out_shape=jax.ShapeDtypeStruct((groups * ROWS, panel), jnp.float32),
     )(parts, lo_col, hi_row)
-    summed = summed.reshape(blocks, ROWS, panel)[:, : steps * PARTS].reshape(blocks, PARTS, steps, panel)
-    summed = summed[:, 0] + summed[:, 1] + summed[:, 2]
-    return jnp.transpose(summed, (1, 0, 2)).reshape(steps, blocks * panel)
+    summed = jnp.sum(summed.reshape(groups, 2, PARTS, steps, panel), axis=2)
+    summed = jnp.transpose(summed, (2, 0, 1, 3)).reshape(steps, 2 * groups * panel)
+    return summed[:, : blocks * panel]
 
 
 def one_axis_at_a_time(array, axes):

time: 201 us -> 197 us (0.980)
    reshape x2 -> x5, local copies, waits for them, and re-layouts: 2.45 us -> 4.84 us  [the longest x2 2.38 us: bus_to_units(): return jnp.sum(picked.reshape(ROWS // steps, steps, units), axis=0)]
where the time goes in v5:
time: 197 us; the launch traced here: 196 us
  waiting for transfers between devices  73.8 us (37%)
  starting transfers between devices  42.2 us (21%)
  Pallas kernels  18.4 us (9%)
  blocking collectives  17.7 us (9%)
  local copies, waits for them, and re-layouts  16.2 us (8%)
  matrix products  14.4 us (7%)
  other arithmetic  12.2 us (6%)
    all_to_all x2, waiting for transfers between devices, per_device(): lax.all_to_all(target, TM, split_axis=1, concat_axis=0, tiled=True)  32.3 us
    all_to_all x1, waiting for transfers between devices, per_device(): lax.all_to_all(jnp.concatenate([chunks, extra], axis=1), TM, split_axis=0...  20.9 us
    all_to_all x2, starting transfers between devices, per_device(): lax.all_to_all(target, TM, split_axis=1, concat_axis=0, tiled=True)  19 us
    all_to_all x1, waiting for transfers between devices, per_device(): lax.all_to_all(power_cols, TM, split_axis=0, concat_axis=1, tiled=True)  14.2 us
    pallas_call x2, Pallas kernels, bus_to_units(): pl.pallas_call(gather_kernel, grid=(units // UNIT_BLOCK,), in_specs=[pl.B...  11.1 us
    all_to_all x1, blocking collectives, per_device(): lax.all_to_all(outbound, AREA, split_axis=1, concat_axis=1, tiled=True)  9.56 us
    all_to_all x1, starting transfers between devices, per_device(): lax.all_to_all(sending.reshape(block_steps, area_devices, capacity, panel...  9.15 us
    all_to_all x1, blocking collectives, per_device(): lax.all_to_all(sending.reshape(block_steps, area_devices, capacity, panel...  8.17 us
  transfers between devices with their start and end apart: 6, of which 6 were waited for; matrix products, arithmetic and copies ran while one was open for 5% of the time, Pallas kernels for 0%

profile of v5, /device:TPU:2, one launch (start us, length us, event | category | flops | bytes accessed | tf_op | source)
XLA Modules:
  0.0 196.0 jit_solution(4135518403571325336)
XLA Ops:
  1.2 1.3 reduce.11
  3.9 0.9 convert_element_type.69
  6.3 9.1 %all-to-all-start = ((bf16[4,8,6,256]{3,0,2,1:T(4,128)(2,1)}), bf16[4,8,6,256]{3,0,2,1:T(4,128)(2,1)S(1)}, u32[]{:S(2)}, u32[]{:S(2)}) async-start(bf16[4,8,6,256]{3,0,2,1:T(4,128)(2,1)} %bitcast.7), calls=%async_computation | async-start | bytes 196608 | tf_op jit(solution)/shard_map/all_to_all | solution.py:232
  18.0 1.8 all-to-all-done
  22.5 0.8 copy.60
  23.3 4.7 %all-to-all-start.1 = ((f32[4,8,6,256]{3,0,2,1:T(4,128)}), f32[4,8,6,256]{3,0,2,1:T(4,128)S(1)}, u32[]{:S(2)}, u32[]{:S(2)}) async-start(f32[4,8,6,256]{3,0,2,1:T(4,128)} %bitcast.17), calls=%async_computation.1 | async-start | bytes 393216 | tf_op jit(solution)/shard_map/all_to_all | solution.py:272
  28.7 4.7 %all-to-all-done.1 = f32[4,8,6,256]{3,0,2,1:T(4,128)S(1)} async-done(((f32[4,8,6,256]{3,0,2,1:T(4,128)}), f32[4,8,6,256]{3,0,2,1:T(4,128)S(1)}, u32[]{:S(2)}, u32[]{:S(2)}) %all-to-all-start.1) | async-done | bytes 196640 | tf_op jit(solution)/shard_map/all_to_all | solution.py:272
  34.6 5.6 %shard_map.130 = f32[16,8192]{1,0:T(8,128)} custom-call(bf16[288,256]{1,0:T(8,128)(2,1)} %reshape.315.table_ref, s32[1,8192]{1,0:T(1,128)} %bitcast.204, s32[1,8192]{1,0:T(1,128)} %bitcast.201), custom_call_target="tpu_custom_call" | custom-call | tf_op jit(solution)/shard_map/pallas_call | solution.py:81
  40.1 1.2 reshape.318
  42.1 14.4 %all-to-all-start.2 = ((f32[4,64,128]{2,0,1:T(4,128)}), f32[4,64,128]{2,0,1:T(4,128)S(1)}, u32[]{:S(2)}, u32[]{:S(2)}) async-start(f32[4,64,128]{2,0,1:T(4,128)} %subtract_bitcast_fusion), calls=%async_computation.2 | async-start | bytes 262144 | tf_op jit(solution)/shard_map/all_to_all | solution.py:286
  56.6 1.6 fusion.18
  59.3 14.6 %all-to-all-done.2 = f32[4,64,128]{2,0,1:T(4,128)S(1)} async-done(((f32[4,64,128]{2,0,1:T(4,128)}), f32[4,64,128]{2,0,1:T(4,128)S(1)}, u32[]{:S(2)}, u32[]{:S(2)}) %all-to-all-start.2) | async-done | bytes 131104 | tf_op jit(solution)/shard_map/all_to_all | solution.py:286
  73.9 2.2 %fusion.19 = f32[256,128]{1,0:T(8,128)S(1)} fusion(f32[256,128]{1,0:T(8,128)S(1)} %bitcast.215, s32[256]{0:T(256)S(1)} %get-tuple-element.37, pred[256]{0:T(512)(128)(4,1)S(1)} %iota_compare_fusion.7), kind=kOutput, calls=%fused_computation.54 | convolution fusion | flops 101711872 | bytes 263424 | tf_op jit(solution)/shard_map/dot_general | solution.py:287
  76.2 2.3 %fusion.1 = f32[256,128]{1,0:T(8,128)} fusion(f32[127,128]{1,0:T(8,128)S(1)} %fusion.25, f32[129,128]{1,0:T(8,128)S(1)} %get-tuple-element.48, s32[256]{0:T(256)S(1)} %get-tuple-element.37, pred[256]{0:T(512)(128)(4,1)S(1)} %iota_compare_fusion.7, f32[256]{0:T(256)S(1)} %get-tuple-element.36, f32[128]{0:T(128)S(1)} %get-tuple-element.34, ...), kind=kOutput, calls=%fused_computation.13 | convolution fusion | flops 101842944 | bytes 265472 | tf_op jit(solution)/shard_map/dot_general | solution.py:295
  78.6 4.6 %all-to-all-start.3 = ((f32[64,4,128]{2,1,0:T(4,128)}), f32[64,4,128]{2,1,0:T(4,128)S(1)}, u32[]{:S(2)}, u32[]{:S(2)}) async-start(f32[64,4,128]{2,1,0:T(4,128)} %bitcast.30), calls=%async_computation.3 | async-start | bytes 262144 | tf_op jit(solution)/shard_map/all_to_all | solution.py:316
  83.2 2.6 %copy.65.lo_ref = s32[8192,1]{1,0:T(8,128)} copy(s32[8192,1]{0,1:T(1,128)S(1)} %bitcast.206) | data formatting | bytes 65536 | tf_op jit(solution)/shard_map/reshape;reshape | solution.py:220
  85.8 14.2 %all-to-all-done.3 = f32[64,4,128]{2,1,0:T(4,128)S(1)} async-done(((f32[64,4,128]{2,1,0:T(4,128)}), f32[64,4,128]{2,1,0:T(4,128)S(1)}, u32[]{:S(2)}, u32[]{:S(2)}) %all-to-all-start.3) | async-done | bytes 131104 | tf_op jit(solution)/shard_map/all_to_all | solution.py:316
  100.0 0.8 pad_maximum_fusion.parts_ref
  100.9 7.3 %shard_map.131 = f32[288,256]{1,0:T(8,128)} custom-call(bf16[16,8192]{1,0:T(8,128)(2,1)} %pad_maximum_fusion.parts_ref, s32[8192,1]{1,0:T(8,128)} %copy.65.lo_ref, s32[1,8192]{1,0:T(1,128)} %bitcast.202), custom_call_target="tpu_custom_call" | custom-call | tf_op jit(solution)/shard_map/pallas_call | solution.py:120
  108.1 1.0 reshape.319
  110.1 8.2 %all_to_all.82 = bf16[4,8,6,256]{3,0,2,1:T(4,128)(2,1)S(1)} all-to-all(bf16[4,8,6,256]{3,0,2,1:T(4,128)(2,1)S(1)} %bitcast.209), channel_id=1, replica_groups=mesh['tm_0'=16,'tm_1'=4,'area_0'=4,'area_1'=2] {'area_0','area_1'}, dimensions={1} | all-to-all | bytes 196608 | tf_op jit(solution)/shard_map/all_to_all | solution.py:232
  119.4 0.8 fusion.45
  120.2 1.4 maximum_bitcast_fusion
  123.1 9.6 %all_to_all.83 = f32[4,8,7,256]{3,0,2,1:T(4,128)S(1)} all-to-all(f32[4,8,7,256]{3,0,2,1:T(4,128)S(1)} %pad_maximum_fusion.2), channel_id=1, replica_groups=mesh['tm_0'=16,'tm_1'=4,'area_0'=4,'area_1'=2] {'area_0','area_1'}, dimensions={1} | all-to-all | bytes 458752 | tf_op jit(solution)/shard_map/all_to_all | solution.py:272
  133.8 5.5 %shard_map.132 = f32[16,8192]{1,0:T(8,128)} custom-call(bf16[288,256]{1,0:T(8,128)(2,1)} %reshape.328.table_ref, s32[1,8192]{1,0:T(1,128)} %bitcast.205, s32[1,8192]{1,0:T(1,128)} %bitcast.203), custom_call_target="tpu_custom_call" | custom-call | tf_op jit(solution)/shard_map/pallas_call | solution.py:81
  139.4 1.2 reshape.329
  141.4 4.6 %all-to-all-start.6 = ((f32[4,64,128]{2,0,1:T(4,128)}), f32[4,64,128]{2,0,1:T(4,128)S(1)}, u32[]{:S(2)}, u32[]{:S(2)}) async-start(f32[4,64,128]{2,0,1:T(4,128)} %fusion.16), calls=%async_computation.6 | async-start | bytes 262144 | tf_op jit(solution)/shard_map/all_to_all | solution.py:286
  146.1 17.7 %all-to-all-done.6 = f32[4,64,128]{2,0,1:T(4,128)S(1)} async-done(((f32[4,64,128]{2,0,1:T(4,128)}), f32[4,64,128]{2,0,1:T(4,128)S(1)}, u32[]{:S(2)}, u32[]{:S(2)}) %all-to-all-start.6) | async-done | bytes 131104 | tf_op jit(solution)/shard_map/all_to_all | solution.py:286
  163.8 2.2 %fusion.17 = f32[256,128]{1,0:T(8,128)S(1)} fusion(f32[256,128]{1,0:T(8,128)S(1)} %bitcast.216, s32[256]{0:T(256)S(1)} %get-tuple-element.37, pred[256]{0:T(512)(128)(4,1)S(1)} %iota_compare_fusion.7), kind=kOutput, calls=%fused_computation.52 | convolution fusion | flops 101711872 | bytes 263424 | tf_op jit(solution)/shard_map/dot_general | solution.py:287
  166.1 1.7 fusion
  168.5 4.6 %all-to-all-start.7 = ((f32[64,5,128]{2,1,0:T(8,128)}), f32[64,5,128]{2,1,0:T(8,128)S(1)}, u32[]{:S(2)}, u32[]{:S(2)}) async-start(f32[64,5,128]{2,1,0:T(8,128)} %pad_maximum_fusion.1), calls=%async_computation.7 | async-start | bytes 524288 | tf_op jit(solution)/shard_map/all_to_all | solution.py:310
  173.8 20.9 %all-to-all-done.7 = f32[64,5,128]{2,1,0:T(8,128)S(1)} async-done(((f32[64,5,128]{2,1,0:T(8,128)}), f32[64,5,128]{2,1,0:T(8,128)S(1)}, u32[]{:S(2)}, u32[]{:S(2)}) %all-to-all-start.7) | async-done | bytes 163872 | tf_op jit(solution)/shard_map/all_to_all | solution.py:310
  (98 shorter events, 20.6 us)
Async XLA Ops:
  0.6 19.8 %copy-start = (bf16[24,128,256]{2,1,0:T(8,128)(2,1)S(1)}, bf16[24,128,256]{2,1,0:T(8,128)(2,1)}, u32[]{:S(2)}) copy-start(bf16[24,128,256]{2,1,0:T(8,128)(2,1)} %param.23) | copy-start | bytes 4718596
  0.6 20.3 %copy-start.4 = (f32[1536]{0:T(1024)S(1)}, f32[1536]{0:T(1024)}, u32[]{:S(2)}) copy-start(f32[1536]{0:T(1024)} %param.30) | copy-start | bytes 18436
  6.3 13.5 %all-to-all-start = ((bf16[4,8,6,256]{3,0,2,1:T(4,128)(2,1)}), bf16[4,8,6,256]{3,0,2,1:T(4,128)(2,1)S(1)}, u32[]{:S(2)}, u32[]{:S(2)}) async-start(bf16[4,8,6,256]{3,0,2,1:T(4,128)(2,1)} %bitcast.7), calls=%async_computation | async-start | bytes 196608 | tf_op jit(solution)/shard_map/all_to_all | solution.py:232
  21.0 7.1 %copy-start.5 = (s32[8192]{0:T(1024)S(1)}, s32[8192]{0:T(1024)}, u32[]{:S(2)}) copy-start(s32[8192]{0:T(1024)} %param.27) | copy-start | bytes 98308
  23.3 10.1 %all-to-all-start.1 = ((f32[4,8,6,256]{3,0,2,1:T(4,128)}), f32[4,8,6,256]{3,0,2,1:T(4,128)S(1)}, u32[]{:S(2)}, u32[]{:S(2)}) async-start(f32[4,8,6,256]{3,0,2,1:T(4,128)} %bitcast.17), calls=%async_computation.1 | async-start | bytes 393216 | tf_op jit(solution)/shard_map/all_to_all | solution.py:272
  33.8 7.7 %copy-start.3 = (f32[4,8192]{1,0:T(4,128)S(1)}, f32[4,8192]{1,0:T(4,128)}, u32[]{:S(2)}) copy-start(f32[4,8192]{1,0:T(4,128)} %param.22) | copy-start | bytes 393220
  34.5 22.0 %copy-start.6 = (f32[3,256]{1,0:T(4,128)S(1)}, f32[3,256]{1,0:T(4,128)}, u32[]{:S(2)}) copy-start(f32[3,256]{1,0:T(4,128)} %param.31) | copy-start | bytes 9220
  42.1 31.8 %all-to-all-start.2 = ((f32[4,64,128]{2,0,1:T(4,128)}), f32[4,64,128]{2,0,1:T(4,128)S(1)}, u32[]{:S(2)}, u32[]{:S(2)}) async-start(f32[4,64,128]{2,0,1:T(4,128)} %subtract_bitcast_fusion), calls=%async_computation.2 | async-start | bytes 262144 | tf_op jit(solution)/shard_map/all_to_all | solution.py:286
  76.1 7.1 %copy-start.2 = (s32[8192]{0:T(1024)S(1)}, s32[8192]{0:T(1024)}, u32[]{:S(2)}) copy-start(s32[8192]{0:T(1024)} %get-tuple-element.56) | copy-start | bytes 98308
  78.6 21.4 %all-to-all-start.3 = ((f32[64,4,128]{2,1,0:T(4,128)}), f32[64,4,128]{2,1,0:T(4,128)S(1)}, u32[]{:S(2)}, u32[]{:S(2)}) async-start(f32[64,4,128]{2,1,0:T(4,128)} %bitcast.30), calls=%async_computation.3 | async-start | bytes 262144 | tf_op jit(solution)/shard_map/all_to_all | solution.py:316
  100.9 8.4 %copy-start.1 = (f32[4,8960]{1,0:T(4,128)S(1)}, f32[4,8960]{1,0:T(4,128)}, u32[]{:S(2)}) copy-start(f32[4,8960]{1,0:T(4,128)} %param.21) | copy-start | bytes 430084
  141.4 22.4 %all-to-all-start.6 = ((f32[4,64,128]{2,0,1:T(4,128)}), f32[4,64,128]{2,0,1:T(4,128)S(1)}, u32[]{:S(2)}, u32[]{:S(2)}) async-start(f32[4,64,128]{2,0,1:T(4,128)} %fusion.16), calls=%async_computation.6 | async-start | bytes 262144 | tf_op jit(solution)/shard_map/all_to_all | solution.py:286
  168.5 26.2 %all-to-all-start.7 = ((f32[64,5,128]{2,1,0:T(8,128)}), f32[64,5,128]{2,1,0:T(8,128)S(1)}, u32[]{:S(2)}, u32[]{:S(2)}) async-start(f32[64,5,128]{2,1,0:T(8,128)} %pad_maximum_fusion.1), calls=%async_computation.7 | async-start | bytes 524288 | tf_op jit(solution)/shard_map/all_to_all | solution.py:310

commit v6 on v5

--- a/solution.py
+++ b/solution.py
@@ -37,7 +37,7 @@
 
 PARTS = 2
 ROWS = 16
-UNIT_BLOCK = 1024
+UNIT_BLOCK = 2048
 
 
 def split_parts(values):

time: 197 us -> 192 us (0.975)
  Pallas kernels: 18.4 us -> 13.1 us
    pallas_call x2, Pallas kernels: 11.1 us -> 8.05 us  [bus_to_units(): pl.pallas_call(gather_kernel, grid=(units // UNIT_BLOCK,), in_specs=[pl.B...]
    pallas_call x1, Pallas kernels: 7.27 us -> 5.09 us  [units_to_bus(): pl.pallas_call(scatter_kernel, grid=(units // UNIT_BLOCK,), in_specs=[pl....]
where the time goes in v6:
time: 192 us; the launch traced here: 191 us
  waiting for transfers between devices  73.8 us (38%)
  starting transfers between devices  42.1 us (22%)
  blocking collectives  17.7 us (9%)
  local copies, waits for them, and re-layouts  16.2 us (8%)
  matrix products  14.4 us (8%)
  Pallas kernels  13.1 us (7%)
  other arithmetic  12.2 us (6%)
    all_to_all x2, waiting for transfers between devices, per_device(): lax.all_to_all(target, TM, split_axis=1, concat_axis=0, tiled=True)  32.3 us
    all_to_all x1, waiting for transfers between devices, per_device(): lax.all_to_all(jnp.concatenate([chunks, extra], axis=1), TM, split_axis=0...  20.9 us
    all_to_all x2, starting transfers between devices, per_device(): lax.all_to_all(target, TM, split_axis=1, concat_axis=0, tiled=True)  19 us
    all_to_all x1, waiting for transfers between devices, per_device(): lax.all_to_all(power_cols, TM, split_axis=0, concat_axis=1, tiled=True)  14.2 us
    all_to_all x1, blocking collectives, per_device(): lax.all_to_all(outbound, AREA, split_axis=1, concat_axis=1, tiled=True)  9.56 us
    all_to_all x1, starting transfers between devices, per_device(): lax.all_to_all(sending.reshape(block_steps, area_devices, capacity, panel...  9.15 us
    all_to_all x1, blocking collectives, per_device(): lax.all_to_all(sending.reshape(block_steps, area_devices, capacity, panel...  8.17 us
    pallas_call x2, Pallas kernels, bus_to_units(): pl.pallas_call(gather_kernel, grid=(units // UNIT_BLOCK,), in_specs=[pl.B...  8.05 us
  transfers between devices with their start and end apart: 6, of which 6 were waited for; matrix products, arithmetic and copies ran while one was open for 5% of the time, Pallas kernels for 0%

profile of v6, /device:TPU:2, one launch (start us, length us, event | category | flops | bytes accessed | tf_op | source)
XLA Modules:
  0.0 190.7 jit_solution(15825271118832858137)
XLA Ops:
  1.2 1.3 reduce.11
  3.9 0.9 convert_element_type.69
  6.3 9.2 %all-to-all-start = ((bf16[4,8,6,256]{3,0,2,1:T(4,128)(2,1)}), bf16[4,8,6,256]{3,0,2,1:T(4,128)(2,1)S(1)}, u32[]{:S(2)}, u32[]{:S(2)}) async-start(bf16[4,8,6,256]{3,0,2,1:T(4,128)(2,1)} %bitcast.7), calls=%async_computation | async-start | bytes 196608 | tf_op jit(solution)/shard_map/all_to_all | solution.py:232
  18.0 1.8 all-to-all-done
  22.5 0.8 copy.60
  23.3 4.7 %all-to-all-start.1 = ((f32[4,8,6,256]{3,0,2,1:T(4,128)}), f32[4,8,6,256]{3,0,2,1:T(4,128)S(1)}, u32[]{:S(2)}, u32[]{:S(2)}) async-start(f32[4,8,6,256]{3,0,2,1:T(4,128)} %bitcast.17), calls=%async_computation.1 | async-start | bytes 393216 | tf_op jit(solution)/shard_map/all_to_all | solution.py:272
  28.7 4.7 %all-to-all-done.1 = f32[4,8,6,256]{3,0,2,1:T(4,128)S(1)} async-done(((f32[4,8,6,256]{3,0,2,1:T(4,128)}), f32[4,8,6,256]{3,0,2,1:T(4,128)S(1)}, u32[]{:S(2)}, u32[]{:S(2)}) %all-to-all-start.1) | async-done | bytes 196640 | tf_op jit(solution)/shard_map/all_to_all | solution.py:272
  34.6 4.0 %shard_map.130 = f32[16,8192]{1,0:T(8,128)} custom-call(bf16[288,256]{1,0:T(8,128)(2,1)} %reshape.315.table_ref, s32[1,8192]{1,0:T(1,128)} %bitcast.204, s32[1,8192]{1,0:T(1,128)} %bitcast.201), custom_call_target="tpu_custom_call" | custom-call | tf_op jit(solution)/shard_map/pallas_call | solution.py:81
  38.6 1.2 reshape.318
  40.6 14.4 %all-to-all-start.2 = ((f32[4,64,128]{2,0,1:T(4,128)}), f32[4,64,128]{2,0,1:T(4,128)S(1)}, u32[]{:S(2)}, u32[]{:S(2)}) async-start(f32[4,64,128]{2,0,1:T(4,128)} %subtract_bitcast_fusion), calls=%async_computation.2 | async-start | bytes 262144 | tf_op jit(solution)/shard_map/all_to_all | solution.py:286
  55.0 1.6 fusion.18
  57.8 14.6 %all-to-all-done.2 = f32[4,64,128]{2,0,1:T(4,128)S(1)} async-done(((f32[4,64,128]{2,0,1:T(4,128)}), f32[4,64,128]{2,0,1:T(4,128)S(1)}, u32[]{:S(2)}, u32[]{:S(2)}) %all-to-all-start.2) | async-done | bytes 131104 | tf_op jit(solution)/shard_map/all_to_all | solution.py:286
  72.4 2.2 %fusion.19 = f32[256,128]{1,0:T(8,128)S(1)} fusion(f32[256,128]{1,0:T(8,128)S(1)} %bitcast.215, s32[256]{0:T(256)S(1)} %get-tuple-element.37, pred[256]{0:T(512)(128)(4,1)S(1)} %iota_compare_fusion.7), kind=kOutput, calls=%fused_computation.54 | convolution fusion | flops 101711872 | bytes 263424 | tf_op jit(solution)/shard_map/dot_general | solution.py:287
  74.7 2.3 %fusion.1 = f32[256,128]{1,0:T(8,128)} fusion(f32[127,128]{1,0:T(8,128)S(1)} %fusion.25, f32[129,128]{1,0:T(8,128)S(1)} %get-tuple-element.48, s32[256]{0:T(256)S(1)} %get-tuple-element.37, pred[256]{0:T(512)(128)(4,1)S(1)} %iota_compare_fusion.7, f32[256]{0:T(256)S(1)} %get-tuple-element.36, f32[128]{0:T(128)S(1)} %get-tuple-element.34, ...), kind=kOutput, calls=%fused_computation.13 | convolution fusion | flops 101842944 | bytes 265472 | tf_op jit(solution)/shard_map/dot_general | solution.py:295
  77.1 4.6 %all-to-all-start.3 = ((f32[64,4,128]{2,1,0:T(4,128)}), f32[64,4,128]{2,1,0:T(4,128)S(1)}, u32[]{:S(2)}, u32[]{:S(2)}) async-start(f32[64,4,128]{2,1,0:T(4,128)} %bitcast.30), calls=%async_computation.3 | async-start | bytes 262144 | tf_op jit(solution)/shard_map/all_to_all | solution.py:316
  81.7 2.6 %copy.65.lo_ref = s32[8192,1]{1,0:T(8,128)} copy(s32[8192,1]{0,1:T(1,128)S(1)} %bitcast.206) | data formatting | bytes 65536 | tf_op jit(solution)/shard_map/reshape;reshape | solution.py:220
  84.3 14.2 %all-to-all-done.3 = f32[64,4,128]{2,1,0:T(4,128)S(1)} async-done(((f32[64,4,128]{2,1,0:T(4,128)}), f32[64,4,128]{2,1,0:T(4,128)S(1)}, u32[]{:S(2)}, u32[]{:S(2)}) %all-to-all-start.3) | async-done | bytes 131104 | tf_op jit(solution)/shard_map/all_to_all | solution.py:316
  98.5 0.8 pad_maximum_fusion.parts_ref
  99.4 5.1 %shard_map.131 = f32[288,256]{1,0:T(8,128)} custom-call(bf16[16,8192]{1,0:T(8,128)(2,1)} %pad_maximum_fusion.parts_ref, s32[8192,1]{1,0:T(8,128)} %copy.65.lo_ref, s32[1,8192]{1,0:T(1,128)} %bitcast.202), custom_call_target="tpu_custom_call" | custom-call | tf_op jit(solution)/shard_map/pallas_call | solution.py:120
  104.4 1.0 reshape.319
  106.4 8.2 %all_to_all.82 = bf16[4,8,6,256]{3,0,2,1:T(4,128)(2,1)S(1)} all-to-all(bf16[4,8,6,256]{3,0,2,1:T(4,128)(2,1)S(1)} %bitcast.209), channel_id=1, replica_groups=mesh['tm_0'=16,'tm_1'=4,'area_0'=4,'area_1'=2] {'area_0','area_1'}, dimensions={1} | all-to-all | bytes 196608 | tf_op jit(solution)/shard_map/all_to_all | solution.py:232
  115.7 0.8 fusion.45
  116.5 1.4 maximum_bitcast_fusion
  119.4 9.6 %all_to_all.83 = f32[4,8,7,256]{3,0,2,1:T(4,128)S(1)} all-to-all(f32[4,8,7,256]{3,0,2,1:T(4,128)S(1)} %pad_maximum_fusion.2), channel_id=1, replica_groups=mesh['tm_0'=16,'tm_1'=4,'area_0'=4,'area_1'=2] {'area_0','area_1'}, dimensions={1} | all-to-all | bytes 458752 | tf_op jit(solution)/shard_map/all_to_all | solution.py:272
  130.1 4.0 %shard_map.132 = f32[16,8192]{1,0:T(8,128)} custom-call(bf16[288,256]{1,0:T(8,128)(2,1)} %reshape.328.table_ref, s32[1,8192]{1,0:T(1,128)} %bitcast.205, s32[1,8192]{1,0:T(1,128)} %bitcast.203), custom_call_target="tpu_custom_call" | custom-call | tf_op jit(solution)/shard_map/pallas_call | solution.py:81
  134.1 1.2 reshape.329
  136.2 4.6 %all-to-all-start.6 = ((f32[4,64,128]{2,0,1:T(4,128)}), f32[4,64,128]{2,0,1:T(4,128)S(1)}, u32[]{:S(2)}, u32[]{:S(2)}) async-start(f32[4,64,128]{2,0,1:T(4,128)} %fusion.16), calls=%async_computation.6 | async-start | bytes 262144 | tf_op jit(solution)/shard_map/all_to_all | solution.py:286
  140.8 17.7 %all-to-all-done.6 = f32[4,64,128]{2,0,1:T(4,128)S(1)} async-done(((f32[4,64,128]{2,0,1:T(4,128)}), f32[4,64,128]{2,0,1:T(4,128)S(1)}, u32[]{:S(2)}, u32[]{:S(2)}) %all-to-all-start.6) | async-done | bytes 131104 | tf_op jit(solution)/shard_map/all_to_all | solution.py:286
  158.5 2.2 %fusion.17 = f32[256,128]{1,0:T(8,128)S(1)} fusion(f32[256,128]{1,0:T(8,128)S(1)} %bitcast.216, s32[256]{0:T(256)S(1)} %get-tuple-element.37, pred[256]{0:T(512)(128)(4,1)S(1)} %iota_compare_fusion.7), kind=kOutput, calls=%fused_computation.52 | convolution fusion | flops 101711872 | bytes 263424 | tf_op jit(solution)/shard_map/dot_general | solution.py:287
  160.8 1.7 fusion
  163.3 4.6 %all-to-all-start.7 = ((f32[64,5,128]{2,1,0:T(8,128)}), f32[64,5,128]{2,1,0:T(8,128)S(1)}, u32[]{:S(2)}, u32[]{:S(2)}) async-start(f32[64,5,128]{2,1,0:T(8,128)} %pad_maximum_fusion.1), calls=%async_computation.7 | async-start | bytes 524288 | tf_op jit(solution)/shard_map/all_to_all | solution.py:310
  168.6 20.9 %all-to-all-done.7 = f32[64,5,128]{2,1,0:T(8,128)S(1)} async-done(((f32[64,5,128]{2,1,0:T(8,128)}), f32[64,5,128]{2,1,0:T(8,128)S(1)}, u32[]{:S(2)}, u32[]{:S(2)}) %all-to-all-start.7) | async-done | bytes 163872 | tf_op jit(solution)/shard_map/all_to_all | solution.py:310
  (98 shorter events, 20.6 us)
Async XLA Ops:
  0.6 19.8 %copy-start = (bf16[24,128,256]{2,1,0:T(8,128)(2,1)S(1)}, bf16[24,128,256]{2,1,0:T(8,128)(2,1)}, u32[]{:S(2)}) copy-start(bf16[24,128,256]{2,1,0:T(8,128)(2,1)} %param.23) | copy-start | bytes 4718596
  0.6 20.3 %copy-start.4 = (f32[1536]{0:T(1024)S(1)}, f32[1536]{0:T(1024)}, u32[]{:S(2)}) copy-start(f32[1536]{0:T(1024)} %param.30) | copy-start | bytes 18436
  6.3 13.5 %all-to-all-start = ((bf16[4,8,6,256]{3,0,2,1:T(4,128)(2,1)}), bf16[4,8,6,256]{3,0,2,1:T(4,128)(2,1)S(1)}, u32[]{:S(2)}, u32[]{:S(2)}) async-start(bf16[4,8,6,256]{3,0,2,1:T(4,128)(2,1)} %bitcast.7), calls=%async_computation | async-start | bytes 196608 | tf_op jit(solution)/shard_map/all_to_all | solution.py:232
  21.0 7.1 %copy-start.5 = (s32[8192]{0:T(1024)S(1)}, s32[8192]{0:T(1024)}, u32[]{:S(2)}) copy-start(s32[8192]{0:T(1024)} %param.27) | copy-start | bytes 98308
  23.3 10.1 %all-to-all-start.1 = ((f32[4,8,6,256]{3,0,2,1:T(4,128)}), f32[4,8,6,256]{3,0,2,1:T(4,128)S(1)}, u32[]{:S(2)}, u32[]{:S(2)}) async-start(f32[4,8,6,256]{3,0,2,1:T(4,128)} %bitcast.17), calls=%async_computation.1 | async-start | bytes 393216 | tf_op jit(solution)/shard_map/all_to_all | solution.py:272
  33.8 6.1 %copy-start.3 = (f32[4,8192]{1,0:T(4,128)S(1)}, f32[4,8192]{1,0:T(4,128)}, u32[]{:S(2)}) copy-start(f32[4,8192]{1,0:T(4,128)} %param.22) | copy-start | bytes 393220
  34.5 20.5 %copy-start.6 = (f32[3,256]{1,0:T(4,128)S(1)}, f32[3,256]{1,0:T(4,128)}, u32[]{:S(2)}) copy-start(f32[3,256]{1,0:T(4,128)} %param.31) | copy-start | bytes 9220
  40.6 31.8 %all-to-all-start.2 = ((f32[4,64,128]{2,0,1:T(4,128)}), f32[4,64,128]{2,0,1:T(4,128)S(1)}, u32[]{:S(2)}, u32[]{:S(2)}) async-start(f32[4,64,128]{2,0,1:T(4,128)} %subtract_bitcast_fusion), calls=%async_computation.2 | async-start | bytes 262144 | tf_op jit(solution)/shard_map/all_to_all | solution.py:286
  74.6 7.1 %copy-start.2 = (s32[8192]{0:T(1024)S(1)}, s32[8192]{0:T(1024)}, u32[]{:S(2)}) copy-start(s32[8192]{0:T(1024)} %get-tuple-element.56) | copy-start | bytes 98308
  77.1 21.4 %all-to-all-start.3 = ((f32[64,4,128]{2,1,0:T(4,128)}), f32[64,4,128]{2,1,0:T(4,128)S(1)}, u32[]{:S(2)}, u32[]{:S(2)}) async-start(f32[64,4,128]{2,1,0:T(4,128)} %bitcast.30), calls=%async_computation.3 | async-start | bytes 262144 | tf_op jit(solution)/shard_map/all_to_all | solution.py:316
  99.4 6.2 %copy-start.1 = (f32[4,8960]{1,0:T(4,128)S(1)}, f32[4,8960]{1,0:T(4,128)}, u32[]{:S(2)}) copy-start(f32[4,8960]{1,0:T(4,128)} %param.21) | copy-start | bytes 430084
  136.2 22.4 %all-to-all-start.6 = ((f32[4,64,128]{2,0,1:T(4,128)}), f32[4,64,128]{2,0,1:T(4,128)S(1)}, u32[]{:S(2)}, u32[]{:S(2)}) async-start(f32[4,64,128]{2,0,1:T(4,128)} %fusion.16), calls=%async_computation.6 | async-start | bytes 262144 | tf_op jit(solution)/shard_map/all_to_all | solution.py:286
  163.3 26.2 %all-to-all-start.7 = ((f32[64,5,128]{2,1,0:T(8,128)}), f32[64,5,128]{2,1,0:T(8,128)S(1)}, u32[]{:S(2)}, u32[]{:S(2)}) async-start(f32[64,5,128]{2,1,0:T(8,128)} %pad_maximum_fusion.1), calls=%async_computation.7 | async-start | bytes 524288 | tf_op jit(solution)/shard_map/all_to_all | solution.py:310

commit v7 on v6

--- a/solution.py
+++ b/solution.py
@@ -37,7 +37,7 @@
 
 PARTS = 2
 ROWS = 16
-UNIT_BLOCK = 2048
+UNIT_BLOCK = 4096
 
 
 def split_parts(values):

time: 192 us -> 191 us (level)
  no operation moved by 1% of the time
where the time goes in v7:
time: 191 us; the launch traced here: 190 us
  waiting for transfers between devices  73.8 us (39%)
  starting transfers between devices  42.2 us (22%)
  blocking collectives  17.7 us (9%)
  local copies, waits for them, and re-layouts  16.2 us (8%)
  matrix products  14.4 us (8%)
  other arithmetic  12.2 us (6%)
  Pallas kernels  12.2 us (6%)
    all_to_all x2, waiting for transfers between devices, per_device(): lax.all_to_all(target, TM, split_axis=1, concat_axis=0, tiled=True)  32.3 us
    all_to_all x1, waiting for transfers between devices, per_device(): lax.all_to_all(jnp.concatenate([chunks, extra], axis=1), TM, split_axis=0...  20.9 us
    all_to_all x2, starting transfers between devices, per_device(): lax.all_to_all(target, TM, split_axis=1, concat_axis=0, tiled=True)  19 us
    all_to_all x1, waiting for transfers between devices, per_device(): lax.all_to_all(power_cols, TM, split_axis=0, concat_axis=1, tiled=True)  14.2 us
    all_to_all x1, blocking collectives, per_device(): lax.all_to_all(outbound, AREA, split_axis=1, concat_axis=1, tiled=True)  9.56 us
    all_to_all x1, starting transfers between devices, per_device(): lax.all_to_all(sending.reshape(block_steps, area_devices, capacity, panel...  9.15 us
    all_to_all x1, blocking collectives, per_device(): lax.all_to_all(sending.reshape(block_steps, area_devices, capacity, panel...  8.17 us
    pallas_call x2, Pallas kernels, bus_to_units(): pl.pallas_call(gather_kernel, grid=(units // UNIT_BLOCK,), in_specs=[pl.B...  7.71 us
  transfers between devices with their start and end apart: 6, of which 6 were waited for; matrix products, arithmetic and copies ran while one was open for 5% of the time, Pallas kernels for 0%

profile of v7, /device:TPU:2, one launch (start us, length us, event | category | flops | bytes accessed | tf_op | source)
XLA Modules:
  0.0 189.8 jit_solution(9966064776809652325)
XLA Ops:
  1.2 1.3 reduce.11
  3.9 0.9 convert_element_type.69
  6.3 9.2 %all-to-all-start = ((bf16[4,8,6,256]{3,0,2,1:T(4,128)(2,1)}), bf16[4,8,6,256]{3,0,2,1:T(4,128)(2,1)S(1)}, u32[]{:S(2)}, u32[]{:S(2)}) async-start(bf16[4,8,6,256]{3,0,2,1:T(4,128)(2,1)} %bitcast.7), calls=%async_computation | async-start | bytes 196608 | tf_op jit(solution)/shard_map/all_to_all | solution.py:232
  18.0 1.8 all-to-all-done
  22.5 0.8 copy.60
  23.3 4.7 %all-to-all-start.1 = ((f32[4,8,6,256]{3,0,2,1:T(4,128)}), f32[4,8,6,256]{3,0,2,1:T(4,128)S(1)}, u32[]{:S(2)}, u32[]{:S(2)}) async-start(f32[4,8,6,256]{3,0,2,1:T(4,128)} %bitcast.17), calls=%async_computation.1 | async-start | bytes 393216 | tf_op jit(solution)/shard_map/all_to_all | solution.py:272
  28.7 4.7 %all-to-all-done.1 = f32[4,8,6,256]{3,0,2,1:T(4,128)S(1)} async-done(((f32[4,8,6,256]{3,0,2,1:T(4,128)}), f32[4,8,6,256]{3,0,2,1:T(4,128)S(1)}, u32[]{:S(2)}, u32[]{:S(2)}) %all-to-all-start.1) | async-done | bytes 196640 | tf_op jit(solution)/shard_map/all_to_all | solution.py:272
  34.6 3.9 %shard_map.130 = f32[16,8192]{1,0:T(8,128)} custom-call(bf16[288,256]{1,0:T(8,128)(2,1)} %reshape.315.table_ref, s32[1,8192]{1,0:T(1,128)} %bitcast.204, s32[1,8192]{1,0:T(1,128)} %bitcast.201), custom_call_target="tpu_custom_call" | custom-call | tf_op jit(solution)/shard_map/pallas_call | solution.py:81
  38.4 1.2 reshape.318
  40.4 14.4 %all-to-all-start.2 = ((f32[4,64,128]{2,0,1:T(4,128)}), f32[4,64,128]{2,0,1:T(4,128)S(1)}, u32[]{:S(2)}, u32[]{:S(2)}) async-start(f32[4,64,128]{2,0,1:T(4,128)} %subtract_bitcast_fusion), calls=%async_computation.2 | async-start | bytes 262144 | tf_op jit(solution)/shard_map/all_to_all | solution.py:286
  54.9 1.6 fusion.18
  57.6 14.6 %all-to-all-done.2 = f32[4,64,128]{2,0,1:T(4,128)S(1)} async-done(((f32[4,64,128]{2,0,1:T(4,128)}), f32[4,64,128]{2,0,1:T(4,128)S(1)}, u32[]{:S(2)}, u32[]{:S(2)}) %all-to-all-start.2) | async-done | bytes 131104 | tf_op jit(solution)/shard_map/all_to_all | solution.py:286
  72.2 2.2 %fusion.19 = f32[256,128]{1,0:T(8,128)S(1)} fusion(f32[256,128]{1,0:T(8,128)S(1)} %bitcast.215, s32[256]{0:T(256)S(1)} %get-tuple-element.37, pred[256]{0:T(512)(128)(4,1)S(1)} %iota_compare_fusion.7), kind=kOutput, calls=%fused_computation.54 | convolution fusion | flops 101711872 | bytes 263424 | tf_op jit(solution)/shard_map/dot_general | solution.py:287
  74.5 2.3 %fusion.1 = f32[256,128]{1,0:T(8,128)} fusion(f32[127,128]{1,0:T(8,128)S(1)} %fusion.25, f32[129,128]{1,0:T(8,128)S(1)} %get-tuple-element.48, s32[256]{0:T(256)S(1)} %get-tuple-element.37, pred[256]{0:T(512)(128)(4,1)S(1)} %iota_compare_fusion.7, f32[256]{0:T(256)S(1)} %get-tuple-element.36, f32[128]{0:T(128)S(1)} %get-tuple-element.34, ...), kind=kOutput, calls=%fused_computation.13 | convolution fusion | flops 101842944 | bytes 265472 | tf_op jit(solution)/shard_map/dot_general | solution.py:295
  76.9 4.6 %all-to-all-start.3 = ((f32[64,4,128]{2,1,0:T(4,128)}), f32[64,4,128]{2,1,0:T(4,128)S(1)}, u32[]{:S(2)}, u32[]{:S(2)}) async-start(f32[64,4,128]{2,1,0:T(4,128)} %bitcast.30), calls=%async_computation.3 | async-start | bytes 262144 | tf_op jit(solution)/shard_map/all_to_all | solution.py:316
  81.5 2.6 %copy.65.lo_ref = s32[8192,1]{1,0:T(8,128)} copy(s32[8192,1]{0,1:T(1,128)S(1)} %bitcast.206) | data formatting | bytes 65536 | tf_op jit(solution)/shard_map/reshape;reshape | solution.py:220
  84.1 14.2 %all-to-all-done.3 = f32[64,4,128]{2,1,0:T(4,128)S(1)} async-done(((f32[64,4,128]{2,1,0:T(4,128)}), f32[64,4,128]{2,1,0:T(4,128)S(1)}, u32[]{:S(2)}, u32[]{:S(2)}) %all-to-all-start.3) | async-done | bytes 131104 | tf_op jit(solution)/shard_map/all_to_all | solution.py:316
  98.3 0.8 pad_maximum_fusion.parts_ref
  99.2 4.5 %shard_map.131 = f32[288,256]{1,0:T(8,128)} custom-call(bf16[16,8192]{1,0:T(8,128)(2,1)} %pad_maximum_fusion.parts_ref, s32[8192,1]{1,0:T(8,128)} %copy.65.lo_ref, s32[1,8192]{1,0:T(1,128)} %bitcast.202), custom_call_target="tpu_custom_call" | custom-call | tf_op jit(solution)/shard_map/pallas_call | solution.py:120
  103.7 1.0 reshape.319
  105.7 8.2 %all_to_all.82 = bf16[4,8,6,256]{3,0,2,1:T(4,128)(2,1)S(1)} all-to-all(bf16[4,8,6,256]{3,0,2,1:T(4,128)(2,1)S(1)} %bitcast.209), channel_id=1, replica_groups=mesh['tm_0'=16,'tm_1'=4,'area_0'=4,'area_1'=2] {'area_0','area_1'}, dimensions={1} | all-to-all | bytes 196608 | tf_op jit(solution)/shard_map/all_to_all | solution.py:232
  115.0 0.8 fusion.45
  115.8 1.4 maximum_bitcast_fusion
  118.7 9.6 %all_to_all.83 = f32[4,8,7,256]{3,0,2,1:T(4,128)S(1)} all-to-all(f32[4,8,7,256]{3,0,2,1:T(4,128)S(1)} %pad_maximum_fusion.2), channel_id=1, replica_groups=mesh['tm_0'=16,'tm_1'=4,'area_0'=4,'area_1'=2] {'area_0','area_1'}, dimensions={1} | all-to-all | bytes 458752 | tf_op jit(solution)/shard_map/all_to_all | solution.py:272
  129.4 3.9 %shard_map.132 = f32[16,8192]{1,0:T(8,128)} custom-call(bf16[288,256]{1,0:T(8,128)(2,1)} %reshape.328.table_ref, s32[1,8192]{1,0:T(1,128)} %bitcast.205, s32[1,8192]{1,0:T(1,128)} %bitcast.203), custom_call_target="tpu_custom_call" | custom-call | tf_op jit(solution)/shard_map/pallas_call | solution.py:81
  133.2 1.2 reshape.329
  135.2 4.6 %all-to-all-start.6 = ((f32[4,64,128]{2,0,1:T(4,128)}), f32[4,64,128]{2,0,1:T(4,128)S(1)}, u32[]{:S(2)}, u32[]{:S(2)}) async-start(f32[4,64,128]{2,0,1:T(4,128)} %fusion.16), calls=%async_computation.6 | async-start | bytes 262144 | tf_op jit(solution)/shard_map/all_to_all | solution.py:286
  139.9 17.7 %all-to-all-done.6 = f32[4,64,128]{2,0,1:T(4,128)S(1)} async-done(((f32[4,64,128]{2,0,1:T(4,128)}), f32[4,64,128]{2,0,1:T(4,128)S(1)}, u32[]{:S(2)}, u32[]{:S(2)}) %all-to-all-start.6) | async-done | bytes 131104 | tf_op jit(solution)/shard_map/all_to_all | solution.py:286
  157.6 2.2 %fusion.17 = f32[256,128]{1,0:T(8,128)S(1)} fusion(f32[256,128]{1,0:T(8,128)S(1)} %bitcast.216, s32[256]{0:T(256)S(1)} %get-tuple-element.37, pred[256]{0:T(512)(128)(4,1)S(1)} %iota_compare_fusion.7), kind=kOutput, calls=%fused_computation.52 | convolution fusion | flops 101711872 | bytes 263424 | tf_op jit(solution)/shard_map/dot_general | solution.py:287
  159.9 1.7 fusion
  162.4 4.6 %all-to-all-start.7 = ((f32[64,5,128]{2,1,0:T(8,128)}), f32[64,5,128]{2,1,0:T(8,128)S(1)}, u32[]{:S(2)}, u32[]{:S(2)}) async-start(f32[64,5,128]{2,1,0:T(8,128)} %pad_maximum_fusion.1), calls=%async_computation.7 | async-start | bytes 524288 | tf_op jit(solution)/shard_map/all_to_all | solution.py:310
  167.6 20.9 %all-to-all-done.7 = f32[64,5,128]{2,1,0:T(8,128)S(1)} async-done(((f32[64,5,128]{2,1,0:T(8,128)}), f32[64,5,128]{2,1,0:T(8,128)S(1)}, u32[]{:S(2)}, u32[]{:S(2)}) %all-to-all-start.7) | async-done | bytes 163872 | tf_op jit(solution)/shard_map/all_to_all | solution.py:310
  (98 shorter events, 20.6 us)
Async XLA Ops:
  0.6 19.8 %copy-start = (bf16[24,128,256]{2,1,0:T(8,128)(2,1)S(1)}, bf16[24,128,256]{2,1,0:T(8,128)(2,1)}, u32[]{:S(2)}) copy-start(bf16[24,128,256]{2,1,0:T(8,128)(2,1)} %param.23) | copy-start | bytes 4718596
  0.6 20.3 %copy-start.4 = (f32[1536]{0:T(1024)S(1)}, f32[1536]{0:T(1024)}, u32[]{:S(2)}) copy-start(f32[1536]{0:T(1024)} %param.30) | copy-start | bytes 18436
  6.3 13.5 %all-to-all-start = ((bf16[4,8,6,256]{3,0,2,1:T(4,128)(2,1)}), bf16[4,8,6,256]{3,0,2,1:T(4,128)(2,1)S(1)}, u32[]{:S(2)}, u32[]{:S(2)}) async-start(bf16[4,8,6,256]{3,0,2,1:T(4,128)(2,1)} %bitcast.7), calls=%async_computation | async-start | bytes 196608 | tf_op jit(solution)/shard_map/all_to_all | solution.py:232
  21.0 7.1 %copy-start.5 = (s32[8192]{0:T(1024)S(1)}, s32[8192]{0:T(1024)}, u32[]{:S(2)}) copy-start(s32[8192]{0:T(1024)} %param.27) | copy-start | bytes 98308
  23.3 10.1 %all-to-all-start.1 = ((f32[4,8,6,256]{3,0,2,1:T(4,128)}), f32[4,8,6,256]{3,0,2,1:T(4,128)S(1)}, u32[]{:S(2)}, u32[]{:S(2)}) async-start(f32[4,8,6,256]{3,0,2,1:T(4,128)} %bitcast.17), calls=%async_computation.1 | async-start | bytes 393216 | tf_op jit(solution)/shard_map/all_to_all | solution.py:272
  33.8 6.0 %copy-start.3 = (f32[4,8192]{1,0:T(4,128)S(1)}, f32[4,8192]{1,0:T(4,128)}, u32[]{:S(2)}) copy-start(f32[4,8192]{1,0:T(4,128)} %param.22) | copy-start | bytes 393220
  34.5 20.3 %copy-start.6 = (f32[3,256]{1,0:T(4,128)S(1)}, f32[3,256]{1,0:T(4,128)}, u32[]{:S(2)}) copy-start(f32[3,256]{1,0:T(4,128)} %param.31) | copy-start | bytes 9220
  40.4 31.8 %all-to-all-start.2 = ((f32[4,64,128]{2,0,1:T(4,128)}), f32[4,64,128]{2,0,1:T(4,128)S(1)}, u32[]{:S(2)}, u32[]{:S(2)}) async-start(f32[4,64,128]{2,0,1:T(4,128)} %subtract_bitcast_fusion), calls=%async_computation.2 | async-start | bytes 262144 | tf_op jit(solution)/shard_map/all_to_all | solution.py:286
  74.4 7.1 %copy-start.2 = (s32[8192]{0:T(1024)S(1)}, s32[8192]{0:T(1024)}, u32[]{:S(2)}) copy-start(s32[8192]{0:T(1024)} %get-tuple-element.56) | copy-start | bytes 98308
  76.9 21.4 %all-to-all-start.3 = ((f32[64,4,128]{2,1,0:T(4,128)}), f32[64,4,128]{2,1,0:T(4,128)S(1)}, u32[]{:S(2)}, u32[]{:S(2)}) async-start(f32[64,4,128]{2,1,0:T(4,128)} %bitcast.30), calls=%async_computation.3 | async-start | bytes 262144 | tf_op jit(solution)/shard_map/all_to_all | solution.py:316
  99.2 5.6 %copy-start.1 = (f32[4,8960]{1,0:T(4,128)S(1)}, f32[4,8960]{1,0:T(4,128)}, u32[]{:S(2)}) copy-start(f32[4,8960]{1,0:T(4,128)} %param.21) | copy-start | bytes 430084
  135.2 22.4 %all-to-all-start.6 = ((f32[4,64,128]{2,0,1:T(4,128)}), f32[4,64,128]{2,0,1:T(4,128)S(1)}, u32[]{:S(2)}, u32[]{:S(2)}) async-start(f32[4,64,128]{2,0,1:T(4,128)} %fusion.16), calls=%async_computation.6 | async-start | bytes 262144 | tf_op jit(solution)/shard_map/all_to_all | solution.py:286
  162.4 26.2 %all-to-all-start.7 = ((f32[64,5,128]{2,1,0:T(8,128)}), f32[64,5,128]{2,1,0:T(8,128)S(1)}, u32[]{:S(2)}, u32[]{:S(2)}) async-start(f32[64,5,128]{2,1,0:T(8,128)} %pad_maximum_fusion.1), calls=%async_computation.7 | async-start | bytes 524288 | tf_op jit(solution)/shard_map/all_to_all | solution.py:310

commit v8 on v7

--- a/solution.py
+++ b/solution.py
@@ -37,7 +37,7 @@
 
 PARTS = 2
 ROWS = 16
-UNIT_BLOCK = 4096
+UNIT_BLOCK = 8192
 
 
 def split_parts(values):

time: 191 us -> 192 us (level)
  no operation moved by 1% of the time
where the time goes in v8:
time: 192 us; the launch traced here: 191 us
  waiting for transfers between devices  73.7 us (38%)
  starting transfers between devices  42.3 us (22%)
  blocking collectives  17.7 us (9%)
  local copies, waits for them, and re-layouts  16.2 us (8%)
  matrix products  14.4 us (8%)
  Pallas kernels  12.9 us (7%)
  other arithmetic  12.2 us (6%)
    all_to_all x2, waiting for transfers between devices, per_device(): lax.all_to_all(target, TM, split_axis=1, concat_axis=0, tiled=True)  32.3 us
    all_to_all x1, waiting for transfers between devices, per_device(): lax.all_to_all(jnp.concatenate([chunks, extra], axis=1), TM, split_axis=0...  20.9 us
    all_to_all x2, starting transfers between devices, per_device(): lax.all_to_all(target, TM, split_axis=1, concat_axis=0, tiled=True)  19 us
    all_to_all x1, waiting for transfers between devices, per_device(): lax.all_to_all(power_cols, TM, split_axis=0, concat_axis=1, tiled=True)  14 us
    all_to_all x1, blocking collectives, per_device(): lax.all_to_all(outbound, AREA, split_axis=1, concat_axis=1, tiled=True)  9.56 us
    all_to_all x1, starting transfers between devices, per_device(): lax.all_to_all(sending.reshape(block_steps, area_devices, capacity, panel...  9.15 us
    all_to_all x1, blocking collectives, per_device(): lax.all_to_all(sending.reshape(block_steps, area_devices, capacity, panel...  8.18 us
    pallas_call x2, Pallas kernels, bus_to_units(): pl.pallas_call(gather_kernel, grid=(units // UNIT_BLOCK,), in_specs=[pl.B...  7.93 us
  transfers between devices with their start and end apart: 6, of which 6 were waited for; matrix products, arithmetic and copies ran while one was open for 5% of the time, Pallas kernels for 0%

profile of v8, /device:TPU:2, one launch (start us, length us, event | category | flops | bytes accessed | tf_op | source)
XLA Modules:
  0.0 190.5 jit_solution(17693790754869265075)
XLA Ops:
  1.2 1.3 reduce.11
  3.9 0.9 convert_element_type.69
  6.3 9.2 %all-to-all-start = ((bf16[4,8,6,256]{3,0,2,1:T(4,128)(2,1)}), bf16[4,8,6,256]{3,0,2,1:T(4,128)(2,1)S(1)}, u32[]{:S(2)}, u32[]{:S(2)}) async-start(bf16[4,8,6,256]{3,0,2,1:T(4,128)(2,1)} %bitcast.7), calls=%async_computation | async-start | bytes 196608 | tf_op jit(solution)/shard_map/all_to_all | solution.py:232
  18.0 1.8 all-to-all-done
  22.5 0.8 copy.60
  23.3 4.7 %all-to-all-start.1 = ((f32[4,8,6,256]{3,0,2,1:T(4,128)}), f32[4,8,6,256]{3,0,2,1:T(4,128)S(1)}, u32[]{:S(2)}, u32[]{:S(2)}) async-start(f32[4,8,6,256]{3,0,2,1:T(4,128)} %bitcast.17), calls=%async_computation.1 | async-start | bytes 393216 | tf_op jit(solution)/shard_map/all_to_all | solution.py:272
  28.7 4.7 %all-to-all-done.1 = f32[4,8,6,256]{3,0,2,1:T(4,128)S(1)} async-done(((f32[4,8,6,256]{3,0,2,1:T(4,128)}), f32[4,8,6,256]{3,0,2,1:T(4,128)S(1)}, u32[]{:S(2)}, u32[]{:S(2)}) %all-to-all-start.1) | async-done | bytes 196640 | tf_op jit(solution)/shard_map/all_to_all | solution.py:272
  34.6 4.0 %shard_map.130 = f32[16,8192]{1,0:T(8,128)} custom-call(bf16[288,256]{1,0:T(8,128)(2,1)} %reshape.315.table_ref, s32[1,8192]{1,0:T(1,128)} %bitcast.204, s32[1,8192]{1,0:T(1,128)} %bitcast.201), custom_call_target="tpu_custom_call" | custom-call | tf_op jit(solution)/shard_map/pallas_call | solution.py:81
  38.5 1.2 reshape.318
  40.6 14.4 %all-to-all-start.2 = ((f32[4,64,128]{2,0,1:T(4,128)}), f32[4,64,128]{2,0,1:T(4,128)S(1)}, u32[]{:S(2)}, u32[]{:S(2)}) async-start(f32[4,64,128]{2,0,1:T(4,128)} %subtract_bitcast_fusion), calls=%async_computation.2 | async-start | bytes 262144 | tf_op jit(solution)/shard_map/all_to_all | solution.py:286
  55.0 1.6 fusion.18
  57.8 14.6 %all-to-all-done.2 = f32[4,64,128]{2,0,1:T(4,128)S(1)} async-done(((f32[4,64,128]{2,0,1:T(4,128)}), f32[4,64,128]{2,0,1:T(4,128)S(1)}, u32[]{:S(2)}, u32[]{:S(2)}) %all-to-all-start.2) | async-done | bytes 131104 | tf_op jit(solution)/shard_map/all_to_all | solution.py:286
  72.3 2.2 %fusion.19 = f32[256,128]{1,0:T(8,128)S(1)} fusion(f32[256,128]{1,0:T(8,128)S(1)} %bitcast.215, s32[256]{0:T(256)S(1)} %get-tuple-element.37, pred[256]{0:T(512)(128)(4,1)S(1)} %iota_compare_fusion.7), kind=kOutput, calls=%fused_computation.54 | convolution fusion | flops 101711872 | bytes 263424 | tf_op jit(solution)/shard_map/dot_general | solution.py:287
  74.7 2.3 %fusion.1 = f32[256,128]{1,0:T(8,128)} fusion(f32[127,128]{1,0:T(8,128)S(1)} %fusion.25, f32[129,128]{1,0:T(8,128)S(1)} %get-tuple-element.48, s32[256]{0:T(256)S(1)} %get-tuple-element.37, pred[256]{0:T(512)(128)(4,1)S(1)} %iota_compare_fusion.7, f32[256]{0:T(256)S(1)} %get-tuple-element.36, f32[128]{0:T(128)S(1)} %get-tuple-element.34, ...), kind=kOutput, calls=%fused_computation.13 | convolution fusion | flops 101842944 | bytes 265472 | tf_op jit(solution)/shard_map/dot_general | solution.py:295
  77.0 4.8 %all-to-all-start.3 = ((f32[64,4,128]{2,1,0:T(4,128)}), f32[64,4,128]{2,1,0:T(4,128)S(1)}, u32[]{:S(2)}, u32[]{:S(2)}) async-start(f32[64,4,128]{2,1,0:T(4,128)} %bitcast.30), calls=%async_computation.3 | async-start | bytes 262144 | tf_op jit(solution)/shard_map/all_to_all | solution.py:316
  81.8 2.6 %copy.65.lo_ref = s32[8192,1]{1,0:T(8,128)} copy(s32[8192,1]{0,1:T(1,128)S(1)} %bitcast.206) | data formatting | bytes 65536 | tf_op jit(solution)/shard_map/reshape;reshape | solution.py:220
  84.4 14.0 %all-to-all-done.3 = f32[64,4,128]{2,1,0:T(4,128)S(1)} async-done(((f32[64,4,128]{2,1,0:T(4,128)}), f32[64,4,128]{2,1,0:T(4,128)S(1)}, u32[]{:S(2)}, u32[]{:S(2)}) %all-to-all-start.3) | async-done | bytes 131104 | tf_op jit(solution)/shard_map/all_to_all | solution.py:316
  98.4 0.8 pad_maximum_fusion.parts_ref
  99.3 5.0 %shard_map.131 = f32[288,256]{1,0:T(8,128)} custom-call(bf16[16,8192]{1,0:T(8,128)(2,1)} %pad_maximum_fusion.parts_ref, s32[8192,1]{1,0:T(8,128)} %copy.65.lo_ref, s32[1,8192]{1,0:T(1,128)} %bitcast.202), custom_call_target="tpu_custom_call" | custom-call | tf_op jit(solution)/shard_map/pallas_call | solution.py:120
  104.3 1.0 reshape.319
  106.3 8.2 %all_to_all.82 = bf16[4,8,6,256]{3,0,2,1:T(4,128)(2,1)S(1)} all-to-all(bf16[4,8,6,256]{3,0,2,1:T(4,128)(2,1)S(1)} %bitcast.209), channel_id=1, replica_groups=mesh['tm_0'=16,'tm_1'=4,'area_0'=4,'area_1'=2] {'area_0','area_1'}, dimensions={1} | all-to-all | bytes 196608 | tf_op jit(solution)/shard_map/all_to_all | solution.py:232
  115.6 0.8 fusion.45
  116.4 1.4 maximum_bitcast_fusion
  119.3 9.6 %all_to_all.83 = f32[4,8,7,256]{3,0,2,1:T(4,128)S(1)} all-to-all(f32[4,8,7,256]{3,0,2,1:T(4,128)S(1)} %pad_maximum_fusion.2), channel_id=1, replica_groups=mesh['tm_0'=16,'tm_1'=4,'area_0'=4,'area_1'=2] {'area_0','area_1'}, dimensions={1} | all-to-all | bytes 458752 | tf_op jit(solution)/shard_map/all_to_all | solution.py:272
  130.0 4.0 %shard_map.132 = f32[16,8192]{1,0:T(8,128)} custom-call(bf16[288,256]{1,0:T(8,128)(2,1)} %reshape.328.table_ref, s32[1,8192]{1,0:T(1,128)} %bitcast.205, s32[1,8192]{1,0:T(1,128)} %bitcast.203), custom_call_target="tpu_custom_call" | custom-call | tf_op jit(solution)/shard_map/pallas_call | solution.py:81
  133.9 1.2 reshape.329
  136.0 4.6 %all-to-all-start.6 = ((f32[4,64,128]{2,0,1:T(4,128)}), f32[4,64,128]{2,0,1:T(4,128)S(1)}, u32[]{:S(2)}, u32[]{:S(2)}) async-start(f32[4,64,128]{2,0,1:T(4,128)} %fusion.16), calls=%async_computation.6 | async-start | bytes 262144 | tf_op jit(solution)/shard_map/all_to_all | solution.py:286
  140.6 17.7 %all-to-all-done.6 = f32[4,64,128]{2,0,1:T(4,128)S(1)} async-done(((f32[4,64,128]{2,0,1:T(4,128)}), f32[4,64,128]{2,0,1:T(4,128)S(1)}, u32[]{:S(2)}, u32[]{:S(2)}) %all-to-all-start.6) | async-done | bytes 131104 | tf_op jit(solution)/shard_map/all_to_all | solution.py:286
  158.3 2.2 %fusion.17 = f32[256,128]{1,0:T(8,128)S(1)} fusion(f32[256,128]{1,0:T(8,128)S(1)} %bitcast.216, s32[256]{0:T(256)S(1)} %get-tuple-element.37, pred[256]{0:T(512)(128)(4,1)S(1)} %iota_compare_fusion.7), kind=kOutput, calls=%fused_computation.52 | convolution fusion | flops 101711872 | bytes 263424 | tf_op jit(solution)/shard_map/dot_general | solution.py:287
  160.6 1.7 fusion
  163.1 4.6 %all-to-all-start.7 = ((f32[64,5,128]{2,1,0:T(8,128)}), f32[64,5,128]{2,1,0:T(8,128)S(1)}, u32[]{:S(2)}, u32[]{:S(2)}) async-start(f32[64,5,128]{2,1,0:T(8,128)} %pad_maximum_fusion.1), calls=%async_computation.7 | async-start | bytes 524288 | tf_op jit(solution)/shard_map/all_to_all | solution.py:310
  168.4 20.9 %all-to-all-done.7 = f32[64,5,128]{2,1,0:T(8,128)S(1)} async-done(((f32[64,5,128]{2,1,0:T(8,128)}), f32[64,5,128]{2,1,0:T(8,128)S(1)}, u32[]{:S(2)}, u32[]{:S(2)}) %all-to-all-start.7) | async-done | bytes 163872 | tf_op jit(solution)/shard_map/all_to_all | solution.py:310
  (98 shorter events, 20.6 us)
Async XLA Ops:
  0.6 19.8 %copy-start = (bf16[24,128,256]{2,1,0:T(8,128)(2,1)S(1)}, bf16[24,128,256]{2,1,0:T(8,128)(2,1)}, u32[]{:S(2)}) copy-start(bf16[24,128,256]{2,1,0:T(8,128)(2,1)} %param.23) | copy-start | bytes 4718596
  0.6 20.3 %copy-start.4 = (f32[1536]{0:T(1024)S(1)}, f32[1536]{0:T(1024)}, u32[]{:S(2)}) copy-start(f32[1536]{0:T(1024)} %param.30) | copy-start | bytes 18436
  6.3 13.5 %all-to-all-start = ((bf16[4,8,6,256]{3,0,2,1:T(4,128)(2,1)}), bf16[4,8,6,256]{3,0,2,1:T(4,128)(2,1)S(1)}, u32[]{:S(2)}, u32[]{:S(2)}) async-start(bf16[4,8,6,256]{3,0,2,1:T(4,128)(2,1)} %bitcast.7), calls=%async_computation | async-start | bytes 196608 | tf_op jit(solution)/shard_map/all_to_all | solution.py:232
  21.0 7.1 %copy-start.5 = (s32[8192]{0:T(1024)S(1)}, s32[8192]{0:T(1024)}, u32[]{:S(2)}) copy-start(s32[8192]{0:T(1024)} %param.27) | copy-start | bytes 98308
  23.3 10.1 %all-to-all-start.1 = ((f32[4,8,6,256]{3,0,2,1:T(4,128)}), f32[4,8,6,256]{3,0,2,1:T(4,128)S(1)}, u32[]{:S(2)}, u32[]{:S(2)}) async-start(f32[4,8,6,256]{3,0,2,1:T(4,128)} %bitcast.17), calls=%async_computation.1 | async-start | bytes 393216 | tf_op jit(solution)/shard_map/all_to_all | solution.py:272
  33.8 6.1 %copy-start.3 = (f32[4,8192]{1,0:T(4,128)S(1)}, f32[4,8192]{1,0:T(4,128)}, u32[]{:S(2)}) copy-start(f32[4,8192]{1,0:T(4,128)} %param.22) | copy-start | bytes 393220
  34.6 20.4 %copy-start.6 = (f32[3,256]{1,0:T(4,128)S(1)}, f32[3,256]{1,0:T(4,128)}, u32[]{:S(2)}) copy-start(f32[3,256]{1,0:T(4,128)} %param.31) | copy-start | bytes 9220
  40.6 31.8 %all-to-all-start.2 = ((f32[4,64,128]{2,0,1:T(4,128)}), f32[4,64,128]{2,0,1:T(4,128)S(1)}, u32[]{:S(2)}, u32[]{:S(2)}) async-start(f32[4,64,128]{2,0,1:T(4,128)} %subtract_bitcast_fusion), calls=%async_computation.2 | async-start | bytes 262144 | tf_op jit(solution)/shard_map/all_to_all | solution.py:286
  74.5 7.3 %copy-start.2 = (s32[8192]{0:T(1024)S(1)}, s32[8192]{0:T(1024)}, u32[]{:S(2)}) copy-start(s32[8192]{0:T(1024)} %get-tuple-element.56) | copy-start | bytes 98308
  77.0 21.4 %all-to-all-start.3 = ((f32[64,4,128]{2,1,0:T(4,128)}), f32[64,4,128]{2,1,0:T(4,128)S(1)}, u32[]{:S(2)}, u32[]{:S(2)}) async-start(f32[64,4,128]{2,1,0:T(4,128)} %bitcast.30), calls=%async_computation.3 | async-start | bytes 262144 | tf_op jit(solution)/shard_map/all_to_all | solution.py:316
  99.3 6.1 %copy-start.1 = (f32[4,8960]{1,0:T(4,128)S(1)}, f32[4,8960]{1,0:T(4,128)}, u32[]{:S(2)}) copy-start(f32[4,8960]{1,0:T(4,128)} %param.21) | copy-start | bytes 430084
  136.0 22.4 %all-to-all-start.6 = ((f32[4,64,128]{2,0,1:T(4,128)}), f32[4,64,128]{2,0,1:T(4,128)S(1)}, u32[]{:S(2)}, u32[]{:S(2)}) async-start(f32[4,64,128]{2,0,1:T(4,128)} %fusion.16), calls=%async_computation.6 | async-start | bytes 262144 | tf_op jit(solution)/shard_map/all_to_all | solution.py:286
  163.1 26.2 %all-to-all-start.7 = ((f32[64,5,128]{2,1,0:T(8,128)}), f32[64,5,128]{2,1,0:T(8,128)S(1)}, u32[]{:S(2)}, u32[]{:S(2)}) async-start(f32[64,5,128]{2,1,0:T(8,128)} %pad_maximum_fusion.1), calls=%async_computation.7 | async-start | bytes 524288 | tf_op jit(solution)/shard_map/all_to_all | solution.py:310

commit v9 on v7

--- a/solution.py
+++ b/solution.py
@@ -55,7 +55,7 @@
     return 2 * group + half
 
 
-def gather_kernel(table_ref, lo_ref, hi_ref, out_ref):
+def gather_kernel(table_ref, lo_ref, hi_ref, power_ref, cost_ref, out_ref):
     lanes = table_ref.shape[1]
     width = lo_ref.shape[1]
     onehot = (lax.broadcasted_iota(jnp.int32, (lanes, width), 0) == lo_ref[...]).astype(jnp.bfloat16)
@@ -65,10 +65,12 @@
     for group in range(table_ref.shape[0] // ROWS):
         block = picked[group * ROWS : (group + 1) * ROWS]
         total = total + jnp.where(hi == group_targets(group), block, 0.0)
-    out_ref[...] = total
-
-
-def bus_to_units(prices, lo_row, hi_row):
+    quarter = ROWS // 4
+    price = total[0:quarter] + total[quarter : 2 * quarter] + total[2 * quarter : 3 * quarter] + total[3 * quarter :]
+    out_ref[...] = power_ref[...] - step_size * (cost_ref[...] + rho_weight * price)
+
+
+def bus_to_units(prices, lo_row, hi_row, power, cost):
     steps, buses = prices.shape
     panel = 256
     blocks = buses // panel
@@ -85,11 +87,13 @@
             pl.BlockSpec((groups * ROWS, panel), lambda i: (0, 0)),
             pl.BlockSpec((1, UNIT_BLOCK), lambda i: (0, i)),
             pl.BlockSpec((1, UNIT_BLOCK), lambda i: (0, i)),
+            pl.BlockSpec((steps, UNIT_BLOCK), lambda i: (0, i)),
+            pl.BlockSpec((steps, UNIT_BLOCK), lambda i: (0, i)),
         ],
-        out_specs=pl.BlockSpec((ROWS, UNIT_BLOCK), lambda i: (0, i)),
-        out_shape=jax.ShapeDtypeStruct((ROWS, units), jnp.float32),
-    )(table, lo_row, hi_row)
-    return jnp.sum(picked.reshape(ROWS // steps, steps, units), axis=0)
+        out_specs=pl.BlockSpec((steps, UNIT_BLOCK), lambda i: (0, i)),
+        out_shape=jax.ShapeDtypeStruct((steps, units), jnp.float32),
+    )(table, lo_row, hi_row, power, cost)
+    return picked
 
 
 def scatter_kernel(parts_ref, lo_ref, hi_ref, out_ref):
@@ -281,8 +285,7 @@
             preferred_element_type=jnp.float32,
         )
         prices = prices.reshape(block_steps, bus_area)
-        gradient = unit_cost + rho_weight * bus_to_units(prices, lo_row, hi_row)
-        target = power_time - step_size * gradient
+        target = bus_to_units(prices, lo_row, hi_row, power_time, unit_cost)
         columns = lax.all_to_all(target, TM, split_axis=1, concat_axis=0, tiled=True)
         spectrum = jnp.dot(
             forward, columns, precision=lax.Precision.HIGHEST, preferred_element_type=jnp.float32

time: 191 us -> 188 us (0.984)
    reshape x2 -> x0, local copies, waits for them, and re-layouts: 2.38 us -> none  [bus_to_units(): return jnp.sum(picked.reshape(ROWS // steps, steps, units), axis=0)]
where the time goes in v9:
time: 188 us; the launch traced here: 187 us
  waiting for transfers between devices  73.8 us (39%)
  starting transfers between devices  42.2 us (22%)
  blocking collectives  17.7 us (9%)
  local copies, waits for them, and re-layouts  14.5 us (8%)
  matrix products  14.4 us (8%)
  Pallas kernels  12.4 us (7%)
  other arithmetic  10.6 us (6%)
    all_to_all x2, waiting for transfers between devices, per_device(): lax.all_to_all(target, TM, split_axis=1, concat_axis=0, tiled=True)  32.3 us
    all_to_all x1, waiting for transfers between devices, per_device(): lax.all_to_all(jnp.concatenate([chunks, extra], axis=1), TM, split_axis=0...  20.9 us
    all_to_all x2, starting transfers between devices, per_device(): lax.all_to_all(target, TM, split_axis=1, concat_axis=0, tiled=True)  19 us
    all_to_all x1, waiting for transfers between devices, per_device(): lax.all_to_all(power_cols, TM, split_axis=0, concat_axis=1, tiled=True)  14.1 us
    all_to_all x1, blocking collectives, per_device(): lax.all_to_all(outbound, AREA, split_axis=1, concat_axis=1, tiled=True)  9.56 us
    all_to_all x1, starting transfers between devices, per_device(): lax.all_to_all(sending.reshape(block_steps, area_devices, capacity, panel...  9.15 us
    all_to_all x1, blocking collectives, per_device(): lax.all_to_all(sending.reshape(block_steps, area_devices, capacity, panel...  8.17 us
    pallas_call x2, Pallas kernels, bus_to_units(): pl.pallas_call(gather_kernel, grid=(units // UNIT_BLOCK,), in_specs=[pl.B...  7.95 us
  transfers between devices with their start and end apart: 6, of which 6 were waited for; matrix products, arithmetic and copies ran while one was open for 5% of the time, Pallas kernels for 0%

profile of v9, /device:TPU:2, one launch (start us, length us, event | category | flops | bytes accessed | tf_op | source)
XLA Modules:
  0.0 186.8 jit_solution(7695452892069934712)
XLA Ops:
  1.2 1.3 reduce.11
  3.9 0.9 convert_element_type.69
  5.5 0.8 broadcast_select_fusion.1
  6.3 9.1 %all-to-all-start = ((bf16[4,8,6,256]{3,0,2,1:T(4,128)(2,1)}), bf16[4,8,6,256]{3,0,2,1:T(4,128)(2,1)S(1)}, u32[]{:S(2)}, u32[]{:S(2)}) async-start(bf16[4,8,6,256]{3,0,2,1:T(4,128)(2,1)} %bitcast.7), calls=%async_computation | async-start | bytes 196608 | tf_op jit(solution)/shard_map/all_to_all | solution.py:236
  18.0 1.8 all-to-all-done
  22.5 0.8 copy.60
  23.3 4.9 %all-to-all-start.1 = ((f32[4,8,6,256]{3,0,2,1:T(4,128)}), f32[4,8,6,256]{3,0,2,1:T(4,128)S(1)}, u32[]{:S(2)}, u32[]{:S(2)}) async-start(f32[4,8,6,256]{3,0,2,1:T(4,128)} %bitcast.17), calls=%async_computation.1 | async-start | bytes 393216 | tf_op jit(solution)/shard_map/all_to_all | solution.py:276
  28.8 4.7 %all-to-all-done.1 = f32[4,8,6,256]{3,0,2,1:T(4,128)S(1)} async-done(((f32[4,8,6,256]{3,0,2,1:T(4,128)}), f32[4,8,6,256]{3,0,2,1:T(4,128)S(1)}, u32[]{:S(2)}, u32[]{:S(2)}) %all-to-all-start.1) | async-done | bytes 196640 | tf_op jit(solution)/shard_map/all_to_all | solution.py:276
  35.3 4.0 %shard_map.130 = f32[4,8192]{1,0:T(4,128)} custom-call(bf16[288,256]{1,0:T(8,128)(2,1)} %reshape.309.table_ref, s32[1,8192]{1,0:T(1,128)} %bitcast.199, s32[1,8192]{1,0:T(1,128)} %bitcast.196, f32[4,8192]{1,0:T(4,128)} %broadcast_in_dim.45.power_ref, f32[4,8192]{1,0:T(4,128)} %cost_ref.3), custom_call_target="tpu_custom_call" | custom-call | tf_op jit(solution)/shard_map/pallas_call | solution.py:83
  39.3 14.4 %all-to-all-start.2 = ((f32[4,64,128]{2,0,1:T(4,128)}), f32[4,64,128]{2,0,1:T(4,128)S(1)}, u32[]{:S(2)}, u32[]{:S(2)}) async-start(f32[4,64,128]{2,0,1:T(4,128)} %bitcast.202), calls=%async_computation.2 | async-start | bytes 262144 | tf_op jit(solution)/shard_map/all_to_all | solution.py:289
  53.7 1.6 fusion.16
  55.7 0.8 fusion.103
  56.5 14.6 %all-to-all-done.2 = f32[4,64,128]{2,0,1:T(4,128)S(1)} async-done(((f32[4,64,128]{2,0,1:T(4,128)}), f32[4,64,128]{2,0,1:T(4,128)S(1)}, u32[]{:S(2)}, u32[]{:S(2)}) %all-to-all-start.2) | async-done | bytes 131104 | tf_op jit(solution)/shard_map/all_to_all | solution.py:289
  71.1 2.2 %fusion.17 = f32[256,128]{1,0:T(8,128)S(1)} fusion(f32[256,128]{1,0:T(8,128)S(1)} %bitcast.212, s32[256]{0:T(256)S(1)} %get-tuple-element.35, pred[256]{0:T(512)(128)(4,1)S(1)} %iota_compare_fusion.7), kind=kOutput, calls=%fused_computation.49 | convolution fusion | flops 101711872 | bytes 263424 | tf_op jit(solution)/shard_map/dot_general | solution.py:290
  73.4 2.3 %fusion.1 = f32[256,128]{1,0:T(8,128)} fusion(f32[127,128]{1,0:T(8,128)S(1)} %fusion.23, f32[129,128]{1,0:T(8,128)S(1)} %get-tuple-element.46, s32[256]{0:T(256)S(1)} %get-tuple-element.35, pred[256]{0:T(512)(128)(4,1)S(1)} %iota_compare_fusion.7, f32[256]{0:T(256)S(1)} %get-tuple-element.34, f32[128]{0:T(128)S(1)} %get-tuple-element.32, ...), kind=kOutput, calls=%fused_computation.13 | convolution fusion | flops 101842944 | bytes 265472 | tf_op jit(solution)/shard_map/dot_general | solution.py:298
  75.7 4.6 %all-to-all-start.3 = ((f32[64,4,128]{2,1,0:T(4,128)}), f32[64,4,128]{2,1,0:T(4,128)S(1)}, u32[]{:S(2)}, u32[]{:S(2)}) async-start(f32[64,4,128]{2,1,0:T(4,128)} %bitcast.30), calls=%async_computation.3 | async-start | bytes 262144 | tf_op jit(solution)/shard_map/all_to_all | solution.py:319
  80.4 2.6 %copy.65.lo_ref = s32[8192,1]{1,0:T(8,128)} copy(s32[8192,1]{0,1:T(1,128)S(1)} %bitcast.201) | data formatting | bytes 65536 | tf_op jit(solution)/shard_map/reshape;reshape | solution.py:224
  83.0 14.1 %all-to-all-done.3 = f32[64,4,128]{2,1,0:T(4,128)S(1)} async-done(((f32[64,4,128]{2,1,0:T(4,128)}), f32[64,4,128]{2,1,0:T(4,128)S(1)}, u32[]{:S(2)}, u32[]{:S(2)}) %all-to-all-start.3) | async-done | bytes 131104 | tf_op jit(solution)/shard_map/all_to_all | solution.py:319
  97.2 0.9 pad_maximum_fusion.parts_ref
  98.1 4.5 %shard_map.131 = f32[288,256]{1,0:T(8,128)} custom-call(bf16[16,8192]{1,0:T(8,128)(2,1)} %pad_maximum_fusion.parts_ref, s32[8192,1]{1,0:T(8,128)} %copy.65.lo_ref, s32[1,8192]{1,0:T(1,128)} %bitcast.197), custom_call_target="tpu_custom_call" | custom-call | tf_op jit(solution)/shard_map/pallas_call | solution.py:124
  102.6 1.0 reshape.312
  104.6 8.2 %all_to_all.82 = bf16[4,8,6,256]{3,0,2,1:T(4,128)(2,1)S(1)} all-to-all(bf16[4,8,6,256]{3,0,2,1:T(4,128)(2,1)S(1)} %bitcast.206), channel_id=1, replica_groups=mesh['tm_0'=16,'tm_1'=4,'area_0'=4,'area_1'=2] {'area_0','area_1'}, dimensions={1} | all-to-all | bytes 196608 | tf_op jit(solution)/shard_map/all_to_all | solution.py:236
  113.9 0.8 fusion.43
  114.7 1.4 maximum_bitcast_fusion
  117.6 9.6 %all_to_all.83 = f32[4,8,7,256]{3,0,2,1:T(4,128)S(1)} all-to-all(f32[4,8,7,256]{3,0,2,1:T(4,128)S(1)} %pad_maximum_fusion.2), channel_id=1, replica_groups=mesh['tm_0'=16,'tm_1'=4,'area_0'=4,'area_1'=2] {'area_0','area_1'}, dimensions={1} | all-to-all | bytes 458752 | tf_op jit(solution)/shard_map/all_to_all | solution.py:276
  128.2 4.0 %shard_map.132 = f32[4,8192]{1,0:T(4,128)} custom-call(bf16[288,256]{1,0:T(8,128)(2,1)} %reshape.321.table_ref, s32[1,8192]{1,0:T(1,128)} %bitcast.200, s32[1,8192]{1,0:T(1,128)} %bitcast.198, f32[4,8192]{1,0:T(4,128)} %bitcast.189, f32[4,8192]{1,0:T(4,128)} %cost_ref.3), custom_call_target="tpu_custom_call" | custom-call | tf_op jit(solution)/shard_map/pallas_call | solution.py:83
  132.2 4.6 %all-to-all-start.6 = ((f32[4,64,128]{2,0,1:T(4,128)}), f32[4,64,128]{2,0,1:T(4,128)S(1)}, u32[]{:S(2)}, u32[]{:S(2)}) async-start(f32[4,64,128]{2,0,1:T(4,128)} %bitcast.203), calls=%async_computation.6 | async-start | bytes 262144 | tf_op jit(solution)/shard_map/all_to_all | solution.py:289
  136.9 17.7 %all-to-all-done.6 = f32[4,64,128]{2,0,1:T(4,128)S(1)} async-done(((f32[4,64,128]{2,0,1:T(4,128)}), f32[4,64,128]{2,0,1:T(4,128)S(1)}, u32[]{:S(2)}, u32[]{:S(2)}) %all-to-all-start.6) | async-done | bytes 131104 | tf_op jit(solution)/shard_map/all_to_all | solution.py:289
  154.6 2.2 %fusion.15 = f32[256,128]{1,0:T(8,128)S(1)} fusion(f32[256,128]{1,0:T(8,128)S(1)} %bitcast.213, s32[256]{0:T(256)S(1)} %get-tuple-element.35, pred[256]{0:T(512)(128)(4,1)S(1)} %iota_compare_fusion.7), kind=kOutput, calls=%fused_computation.47 | convolution fusion | flops 101711872 | bytes 263424 | tf_op jit(solution)/shard_map/dot_general | solution.py:290
  156.9 1.7 fusion
  159.3 4.6 %all-to-all-start.7 = ((f32[64,5,128]{2,1,0:T(8,128)}), f32[64,5,128]{2,1,0:T(8,128)S(1)}, u32[]{:S(2)}, u32[]{:S(2)}) async-start(f32[64,5,128]{2,1,0:T(8,128)} %pad_maximum_fusion.1), calls=%async_computation.7 | async-start | bytes 524288 | tf_op jit(solution)/shard_map/all_to_all | solution.py:313
  164.6 20.9 %all-to-all-done.7 = f32[64,5,128]{2,1,0:T(8,128)S(1)} async-done(((f32[64,5,128]{2,1,0:T(8,128)}), f32[64,5,128]{2,1,0:T(8,128)S(1)}, u32[]{:S(2)}, u32[]{:S(2)}) %all-to-all-start.7) | async-done | bytes 163872 | tf_op jit(solution)/shard_map/all_to_all | solution.py:313
  (94 shorter events, 18.1 us)
Async XLA Ops:
  0.6 19.8 %copy-start = (bf16[24,128,256]{2,1,0:T(8,128)(2,1)S(1)}, bf16[24,128,256]{2,1,0:T(8,128)(2,1)}, u32[]{:S(2)}) copy-start(bf16[24,128,256]{2,1,0:T(8,128)(2,1)} %param.23) | copy-start | bytes 4718596
  0.6 20.3 %copy-start.4 = (f32[1536]{0:T(1024)S(1)}, f32[1536]{0:T(1024)}, u32[]{:S(2)}) copy-start(f32[1536]{0:T(1024)} %param.30) | copy-start | bytes 18436
  6.3 13.5 %all-to-all-start = ((bf16[4,8,6,256]{3,0,2,1:T(4,128)(2,1)}), bf16[4,8,6,256]{3,0,2,1:T(4,128)(2,1)S(1)}, u32[]{:S(2)}, u32[]{:S(2)}) async-start(bf16[4,8,6,256]{3,0,2,1:T(4,128)(2,1)} %bitcast.7), calls=%async_computation | async-start | bytes 196608 | tf_op jit(solution)/shard_map/all_to_all | solution.py:236
  21.0 7.2 %copy-start.5 = (s32[8192]{0:T(1024)S(1)}, s32[8192]{0:T(1024)}, u32[]{:S(2)}) copy-start(s32[8192]{0:T(1024)} %param.27) | copy-start | bytes 98308
  23.3 30.4 %copy-start.6 = (f32[3,256]{1,0:T(4,128)S(1)}, f32[3,256]{1,0:T(4,128)}, u32[]{:S(2)}) copy-start(f32[3,256]{1,0:T(4,128)} %param.31) | copy-start | bytes 9220
  23.3 10.3 %all-to-all-start.1 = ((f32[4,8,6,256]{3,0,2,1:T(4,128)}), f32[4,8,6,256]{3,0,2,1:T(4,128)S(1)}, u32[]{:S(2)}, u32[]{:S(2)}) async-start(f32[4,8,6,256]{3,0,2,1:T(4,128)} %bitcast.17), calls=%async_computation.1 | async-start | bytes 393216 | tf_op jit(solution)/shard_map/all_to_all | solution.py:276
  39.3 31.8 %all-to-all-start.2 = ((f32[4,64,128]{2,0,1:T(4,128)}), f32[4,64,128]{2,0,1:T(4,128)S(1)}, u32[]{:S(2)}, u32[]{:S(2)}) async-start(f32[4,64,128]{2,0,1:T(4,128)} %bitcast.202), calls=%async_computation.2 | async-start | bytes 262144 | tf_op jit(solution)/shard_map/all_to_all | solution.py:289
  73.3 7.1 %copy-start.3 = (s32[8192]{0:T(1024)S(1)}, s32[8192]{0:T(1024)}, u32[]{:S(2)}) copy-start(s32[8192]{0:T(1024)} %get-tuple-element.54) | copy-start | bytes 98308
  75.7 21.4 %all-to-all-start.3 = ((f32[64,4,128]{2,1,0:T(4,128)}), f32[64,4,128]{2,1,0:T(4,128)S(1)}, u32[]{:S(2)}, u32[]{:S(2)}) async-start(f32[64,4,128]{2,1,0:T(4,128)} %bitcast.30), calls=%async_computation.3 | async-start | bytes 262144 | tf_op jit(solution)/shard_map/all_to_all | solution.py:319
  97.2 5.4 %copy-start.1 = (f32[64,4,128]{2,1,0:T(4,128)}, f32[64,4,128]{2,1,0:T(4,128)S(1)}, u32[]{:S(2)}) copy-start(f32[64,4,128]{2,1,0:T(4,128)S(1)} %all-to-all-done.3) | copy-start | bytes 393220
  98.1 5.6 %copy-start.2 = (f32[4,8960]{1,0:T(4,128)S(1)}, f32[4,8960]{1,0:T(4,128)}, u32[]{:S(2)}) copy-start(f32[4,8960]{1,0:T(4,128)} %param.21) | copy-start | bytes 430084
  132.2 22.3 %all-to-all-start.6 = ((f32[4,64,128]{2,0,1:T(4,128)}), f32[4,64,128]{2,0,1:T(4,128)S(1)}, u32[]{:S(2)}, u32[]{:S(2)}) async-start(f32[4,64,128]{2,0,1:T(4,128)} %bitcast.203), calls=%async_computation.6 | async-start | bytes 262144 | tf_op jit(solution)/shard_map/all_to_all | solution.py:289
  159.3 26.2 %all-to-all-start.7 = ((f32[64,5,128]{2,1,0:T(8,128)}), f32[64,5,128]{2,1,0:T(8,128)S(1)}, u32[]{:S(2)}, u32[]{:S(2)}) async-start(f32[64,5,128]{2,1,0:T(8,128)} %pad_maximum_fusion.1), calls=%async_computation.7 | async-start | bytes 524288 | tf_op jit(solution)/shard_map/all_to_all | solution.py:313
